TPU v7x, 32 devices: a whole 2x2x4 slice. The times are simulated.
32 devices in a mesh: grp: 2 (over x), gx: 16 (over z, y, core).
Axes of the slice: x: 2, y: 2, z: 4, core: 2. Of those that a mesh axis runs over, the one named last changes fastest.
Arguments:
- e_forward: float32 [3, 256, 32, 256], P(None, ('grp', 'gx')), parts along dimension 1, may hold values from -6 to 6
- h_forward: float32 [3, 256, 32, 256], P(None, ('grp', 'gx')), parts along dimension 1, may hold values from -6 to 6
- p_forward: float32 [3, 256, 32, 256], P(None, ('grp', 'gx')), parts along dimension 1, may hold values from -6 to 6
- j_forward: float32 [3, 256, 32, 256], P(None, ('grp', 'gx')), parts along dimension 1, may hold values from -6 to 6
- e_adjoint: float32 [3, 256, 32, 256], P(None, ('grp', 'gx')), parts along dimension 1, may hold values from -6 to 6
- h_adjoint: float32 [3, 256, 32, 256], P(None, ('grp', 'gx')), parts along dimension 1, may hold values from -6 to 6
- p_adjoint: float32 [3, 256, 32, 256], P(None, ('grp', 'gx')), parts along dimension 1, may hold values from -6 to 6
- j_adjoint: float32 [3, 256, 32, 256], P(None, ('grp', 'gx')), parts along dimension 1, may hold values from -6 to 6
- design: float32 [32, 32, 256], P(('grp', 'gx')), parts along dimension 0, may hold values from 0 to 1
- source_amp: float32 [32, 3], P('grp'), parts along dimension 0, may hold values from -6 to 6
- source_cell: int32 [32], P('grp'), parts along dimension 0, may hold values from 0 to 1048575
- monitor_cell: int32 [32], P('grp'), parts along dimension 0, may hold values from 0 to 1048575
- slab_start: int32 [2], P('grp'), parts along dimension 0, may hold values from 8 to 15
- radius: int32 [2], P('grp'), parts along dimension 0, may hold values from 1 to 4
Outputs:
- e_forward_next: float32 [3, 256, 32, 256], P(None, ('grp', 'gx')), parts along dimension 1
- h_forward_next: float32 [3, 256, 32, 256], P(None, ('grp', 'gx')), parts along dimension 1
- e_adjoint_next: float32 [3, 256, 32, 256], P(None, ('grp', 'gx')), parts along dimension 1
- h_adjoint_next: float32 [3, 256, 32, 256], P(None, ('grp', 'gx')), parts along dimension 1
- design_grad: float32 [32, 32, 256], P(('grp', 'gx')), parts along dimension 0
There are 2 independent parts, one for each index of `grp`. A program takes and returns all parts, laid end to end along the dimension named above; each array names one. Nothing has to cross between parts.
Inputs may be any that keep to these rules, and one draw needn't show every extreme that they name: `slab_start`: the slab begins within planes 8 to 15 of the grid.
All inputs are finite; a program needn't handle non-finite values.
Results may differ from a plain program's by a relative error of at most 0.0003.
Values sent between devices are 32-bit elements; how exact they have to be, the bound alone decides.
No kernel may reach another device: no remote copies, remote signals or barrier semaphores. Data moves between devices by JAX's collectives and lax.ppermute only.
A program may use at most 128 MiB of HBM per device.

v0:
```python
import jax
import jax.numpy as jnp
from jax import lax
from jax.sharding import PartitionSpec as P

DT = 0.5
EPS_RANGE = 10.0
STRENGTH_BASE = 0.5
STRENGTH_RANGE = 3.0
DAMPING = 0.2
GAIN_FIELD = 0.25
HIGH = lax.Precision.HIGHEST


def passed_along(block, axis, distance):
    devices = range(lax.axis_size(axis))
    route = [(i - distance, i) for i in devices if i - distance in devices]
    return lax.ppermute(block, axis, route)


def band_matrix(count, radius):
    rows = jnp.arange(count, dtype=jnp.int32)
    dist = jnp.abs(rows[:, None] - rows[None, :])
    weights = jnp.maximum(radius + 1 - dist, 0).astype(jnp.float32)
    return weights / jnp.sum(weights, axis=1, keepdims=True)


def ahead(field, axis):
    count = field.shape[axis]
    rest = lax.slice_in_dim(field, 1, count, axis=axis)
    return jnp.concatenate([rest, jnp.zeros_like(lax.slice_in_dim(field, 0, 1, axis=axis))], axis)


def behind(field, axis):
    count = field.shape[axis]
    rest = lax.slice_in_dim(field, 0, count - 1, axis=axis)
    return jnp.concatenate([jnp.zeros_like(lax.slice_in_dim(field, 0, 1, axis=axis)), rest], axis)


def update_h(efield, hfield, upper):
    ex, ey, ez = (efield[0], efield[1], efield[2])
    ex_next = jnp.concatenate([ex[1:], upper[0][None]], 0)
    ey_next = jnp.concatenate([ey[1:], upper[1][None]], 0)
    curl_x = ahead(ez, 2) - ez - (ey_next - ey)
    curl_y = ex_next - ex - (ahead(ez, 1) - ez)
    curl_z = ahead(ey, 1) - ey - (ahead(ex, 2) - ex)
    return hfield - DT * jnp.stack([curl_x, curl_y, curl_z])


def update_e(efield, hnext, lower, jnext, permittivity, drive):
    hx, hy, hz = (hnext[0], hnext[1], hnext[2])
    hx_prev = jnp.concatenate([lower[0][None], hx[:-1]], 0)
    hy_prev = jnp.concatenate([lower[1][None], hy[:-1]], 0)
    curl_x = hz - behind(hz, 2) - (hy - hy_prev)
    curl_y = hx - hx_prev - (hz - behind(hz, 1))
    curl_z = hy - behind(hy, 1) - (hx - behind(hx, 2))
    curl = jnp.stack([curl_x, curl_y, curl_z])
    return efield + (DT / permittivity)[None] * (curl - jnext + drive)


def update_j(jfield, pfield, efield, strength):
    return ((1.0 - DAMPING * DT / 2.0) * jfield + DT * (strength[None] * efield - pfield)) / (
        1.0 + DAMPING * DT / 2.0
    )


def smooth(wx, wy, planes):
    inner = jnp.einsum("ax,zxy->zay", wx, planes, precision=HIGH)
    return jnp.einsum("zay,by->zab", inner, wy, precision=HIGH)


def smooth_adjoint(wx, wy, planes):
    inner = jnp.einsum("ax,zab->zxb", wx, planes, precision=HIGH)
    return jnp.einsum("zxb,by->zxy", inner, wy, precision=HIGH)


def locate(cells, first, depth, width_x, width_y):
    zz = cells // (width_x * width_y)
    rest = cells % (width_x * width_y)
    local = zz - first
    inside = ((local >= 0) & (local < depth)).astype(jnp.float32)
    return (jnp.clip(local, 0, depth - 1), rest // width_y, rest % width_y, inside)


def body(
    e_forward,
    h_forward,
    p_forward,
    j_forward,
    e_adjoint,
    h_adjoint,
    p_adjoint,
    j_adjoint,
    design,
    source_amp,
    source_cell,
    monitor_cell,
    slab_start,
    radius,
):
    count = lax.axis_size("gx")
    index = lax.axis_index("gx")
    depth, width_x, width_y = (e_forward.shape[1], e_forward.shape[2], e_forward.shape[3])
    start = slab_start[0]
    wx = band_matrix(width_x, radius[0])
    wy = band_matrix(width_y, radius[0])
    planes = index * depth + jnp.arange(depth, dtype=jnp.int32) - start
    select = (planes[:, None] == jnp.arange(count, dtype=jnp.int32)[None, :]).astype(jnp.float32)
    upper = passed_along(
        jnp.stack([e_forward[0, 0], e_forward[1, 0], e_adjoint[0, 0], e_adjoint[1, 0]]), "gx", -1
    )
    hf = update_h(e_forward, h_forward, upper[0:2])
    ha = update_h(e_adjoint, h_adjoint, upper[2:4])
    owned = smooth(wx, wy, design)
    holder = (start + index) // depth
    target = (jnp.arange(count, dtype=jnp.int32) == holder).astype(jnp.float32)
    slots = target[:, None, None] * owned
    arrived = lax.all_to_all(slots, "gx", split_axis=0, concat_axis=0, tiled=True)
    density = jnp.einsum("lo,oxy->lxy", select, arrived, precision=HIGH)
    permittivity = 1.0 + EPS_RANGE * density
    strength = STRENGTH_BASE + STRENGTH_RANGE * density
    lower = passed_along(jnp.stack([hf[0, -1], hf[1, -1], ha[0, -1], ha[1, -1]]), "gx", 1)
    zs, xs, ys, inside_s = locate(source_cell, index * depth, depth, width_x, width_y)
    drive = (
        jnp.zeros((3, depth, width_x, width_y), jnp.float32)
        .at[:, zs, xs, ys]
        .add(source_amp.T * inside_s[None, :])
    )
    zm, xm, ym, inside_m = locate(monitor_cell, index * depth, depth, width_x, width_y)
    probe = e_forward[:, zm, xm, ym] * inside_m[None, :]
    drive_adj = jnp.zeros((3, depth, width_x, width_y), jnp.float32).at[:, zm, xm, ym].add(probe)
    jf = update_j(j_forward, p_forward, e_forward, strength)
    ja = update_j(j_adjoint, p_adjoint, e_adjoint, strength)
    ef = update_e(e_forward, hf, lower[0:2], jf, permittivity, drive)
    ea = update_e(e_adjoint, ha, lower[2:4], ja, permittivity, drive_adj)
    intersection = jnp.sum(ea * (ef - e_forward + GAIN_FIELD * ef), axis=0)
    returned = jnp.einsum("lo,lxy->oxy", select, intersection, precision=HIGH)
    arrived_back = lax.all_to_all(returned, "gx", split_axis=0, concat_axis=0, tiled=True)
    own_intersection = jnp.sum(arrived_back, axis=0, keepdims=True)
    design_grad = smooth_adjoint(wx, wy, own_intersection)
    return (ef, hf, ea, ha, design_grad)


def solution(mesh):
    return jax.shard_map(
        body,
        mesh=mesh,
        in_specs=(
            P(None, ("grp", "gx"), None, None),
            P(None, ("grp", "gx"), None, None),
            P(None, ("grp", "gx"), None, None),
            P(None, ("grp", "gx"), None, None),
            P(None, ("grp", "gx"), None, None),
            P(None, ("grp", "gx"), None, None),
            P(None, ("grp", "gx"), None, None),
            P(None, ("grp", "gx"), None, None),
            P(("grp", "gx"), None, None),
            P("grp", None),
            P("grp"),
            P("grp"),
            P("grp"),
            P("grp"),
        ),
        out_specs=(
            P(None, ("grp", "gx"), None, None),
            P(None, ("grp", "gx"), None, None),
            P(None, ("grp", "gx"), None, None),
            P(None, ("grp", "gx"), None, None),
            P(("grp", "gx"), None, None),
        ),
        check_vma=False,
    )
```

profile of v0, /device:TPU:0, one launch (start us, length us, event | category | flops | bytes accessed | tf_op | source)
XLA Modules:
  0.0 170.6 jit_solution(10110285703534453992)
XLA Ops:
  2.3 1.3 collective-permute-start
  6.8 8.8 %all-to-all-start = ((f32[16,32,256]{2,1,0:T(8,128)}), f32[16,32,256]{2,1,0:T(8,128)}, u32[]{:S(2)}, u32[]{:S(2)}) async-start(f32[16,32,256]{2,1,0:T(8,128)} %broadcast_multiply_fusion), calls=%async_computation | async-start | bytes 1048576 | tf_op jit(solution)/shard_map/all_to_all | solution.py:118
  15.6 1.9 %slice_bitcast_fusion.17 = (f32[7,32,256]{2,1,0:T(8,128)}, f32[7,32,256]{2,1,0:T(8,128)}) fusion(f32[3,8,32,256]{3,2,1,0:T(8,128)} %param.18), kind=kLoop, calls=%fused_computation.69 | loop fusion | bytes 917504 | tf_op jit(solution)/shard_map/slice | solution.py:43
  17.5 1.9 %slice_bitcast_fusion.19 = (f32[7,32,256]{2,1,0:T(8,128)}, f32[7,32,256]{2,1,0:T(8,128)}) fusion(f32[3,8,32,256]{3,2,1,0:T(8,128)} %param.14), kind=kLoop, calls=%fused_computation.71 | loop fusion | bytes 917504 | tf_op jit(solution)/shard_map/slice | solution.py:43
  19.3 2.0 %slice_bitcast_fusion.8 = (f32[8,32,256]{2,1,0:T(8,128)S(1)}, f32[8,32,256]{2,1,0:T(8,128)}, f32[8,32,256]{2,1,0:T(8,128)}) fusion(f32[3,8,32,256]{3,2,1,0:T(8,128)} %param.18), kind=kLoop, calls=%fused_computation.54 | loop fusion | bytes 1572864 | tf_op jit(solution)/shard_map/squeeze | solution.py:41
  21.3 1.9 %slice_bitcast_fusion.11 = (f32[8,32,256]{2,1,0:T(8,128)S(1)}, f32[8,32,256]{2,1,0:T(8,128)}, f32[8,32,256]{2,1,0:T(8,128)S(1)}) fusion(f32[3,8,32,256]{3,2,1,0:T(8,128)} %param.14), kind=kLoop, calls=%fused_computation.58 | loop fusion | bytes 1572864 | tf_op jit(solution)/shard_map/squeeze | solution.py:41
  23.2 17.6 %copy.649 = f32[3,8,32,256]{0,3,2,1:T(8,128)} copy(f32[3,8,32,256]{3,2,1,0:T(8,128)} %param.14) | data formatting | bytes 1572864 | tf_op args[0]
  40.8 1.3 gather_fusion
  46.7 1.3 fusion.9
  47.9 1.2 fusion.1
  49.3 1.4 fusion.5
  50.7 1.2 fusion
  52.1 2.3 %collective-permute-start.1 = (f32[4,32,256]{2,1,0:T(8,128)S(1)}, f32[4,32,256]{2,1,0:T(8,128)S(1)}, u32[]{:S(2)}, u32[]{:S(2)}) collective-permute-start(f32[4,32,256]{2,1,0:T(8,128)S(1)} %pad_maximum_fusion.1), channel_id=1, source_target_pairs={{0,1},{1,2},{2,3},{3,4},{4,5},{5,6},{6,7},{7,8},{8,9},{9,10},{10,1... | collective-permute-start | bytes 393224 | tf_op jit(solution)/shard_map/ppermute | solution.py:18
  56.3 1.1 fusion.13
  57.5 1.7 add_divide_fusion
  60.0 4.2 %maximum_subtract_fusion = (f32[3,8,32,256]{3,2,1,0:T(8,128)}, f32[3,8,32,256]{3,2,1,0:T(8,128)}) fusion(f32[1,8,32,256]{3,2,1,0:T(8,128)} %get-tuple-element.109, f32[1,8,32,256]{3,2,1,0:T(8,128)} %get-tuple-element.110, f32[1,8,32,256]{3,2,1,0:T(8,128)} %get-tuple-element.108, f32[3,8,32,256]{3,2,1,0:T(8,128)} %param.16, ...), kind=kLoop, calls=%fused_computation.9 | loop fusion | flops 3538944 | bytes 8126464 | tf_op jit(solution)/shard_map/sub | solution.py:58
  64.2 17.6 %copy.646 = f32[3,8,32,256]{0,3,2,1:T(8,128)} copy(f32[3,8,32,256]{3,2,1,0:T(8,128)} %get-tuple-element.148) | data formatting | bytes 1572864 | tf_op jit(solution)/shard_map/sub | solution.py:58
  81.8 2.2 %scatter_fusion = f32[3,8,32,256]{0,3,2,1:T(8,128)} fusion(f32[3,8,32,256]{0,3,2,1:T(8,128)} %copy.646, s32[16]{0:T(128)S(1)} %fusion.52, f32[16,3]{1,0:T(8,128)S(1)} %copy.647), kind=kCustom, calls=%fused_computation.1 | custom fusion | flops 48 | bytes 768 | tf_op jit(solution)/shard_map/scatter-add | solution.py:127
  84.0 20.2 %copy.648 = f32[3,8,32,256]{3,2,1,0:T(8,128)} copy(f32[3,8,32,256]{0,3,2,1:T(8,128)} %scatter_fusion) | data formatting | bytes 1572864 | tf_op jit(solution)/shard_map/scatter-add | solution.py:127
  104.2 17.7 %copy.650 = f32[3,8,32,256]{0,3,2,1:T(8,128)} copy(f32[3,8,32,256]{3,2,1,0:T(8,128)} %get-tuple-element.149) | data formatting | bytes 1572864 | tf_op jit(solution)/shard_map/sub | solution.py:58
  121.9 2.2 %scatter_fusion.1 = f32[3,8,32,256]{0,3,2,1:T(8,128)} fusion(f32[3,8,32,256]{0,3,2,1:T(8,128)} %copy.650, s32[16]{0:T(128)S(1)} %get-tuple-element.161, f32[16,3]{1,0:T(8,128)S(1)} %broadcast_multiply_fusion.1), kind=kCustom, calls=%fused_computation.2 | custom fusion | flops 48 | bytes 768 | tf_op jit(solution)/shard_map/scatter-add | solution.py:131
  124.1 19.5 %copy.651 = f32[3,8,32,256]{3,2,1,0:T(8,128)S(1)} copy(f32[3,8,32,256]{0,3,2,1:T(8,128)} %scatter_fusion.1) | data formatting | bytes 1572864 | tf_op jit(solution)/shard_map/scatter-add | solution.py:131
  143.5 1.6 multiply_reduce_fusion
  146.0 23.4 %all_to_all.10 = f32[16,32,256]{2,1,0:T(8,128)S(1)} all-to-all(f32[16,32,256]{2,1,0:T(8,128)S(1)} %copy.654), channel_id=1, replica_groups=mesh['grp'=2,'gx'=16] {'gx'}, dimensions={0} | all-to-all | bytes 1048576 | tf_op jit(solution)/shard_map/all_to_all | solution.py:138
  (65 shorter events, 13.1 us)
Async XLA Ops:
  0.6 4.6 %copy-start = (f32[1,32,256]{2,1,0:T(8,128)S(1)}, f32[1,32,256]{2,1,0:T(8,128)}, u32[]{:S(2)}) copy-start(f32[1,32,256]{2,1,0:T(8,128)} %param.22) | copy-start | bytes 98308
  0.6 48.7 %copy-start.2 = (f32[3,8,32,256]{3,2,1,0:T(8,128)S(1)}, f32[3,8,32,256]{3,2,1,0:T(8,128)}, u32[]{:S(2)}) copy-start(f32[3,8,32,256]{3,2,1,0:T(8,128)} %param.14) | copy-start | bytes 2359300
  0.7 46.0 %copy-start.3 = (f32[3,8,32,256]{3,2,1,0:T(8,128)S(1)}, f32[3,8,32,256]{3,2,1,0:T(8,128)}, u32[]{:S(2)}) copy-start(f32[3,8,32,256]{3,2,1,0:T(8,128)} %param.18) | copy-start | bytes 2359300
  0.7 40.1 %copy-start.10 = (s32[16]{0:T(128)S(1)}, s32[16]{0:T(128)}, u32[]{:S(2)}) copy-start(s32[16]{0:T(128)} %param.24) | copy-start | bytes 196
  0.7 40.1 %copy-start.9 = (s32[16]{0:T(128)S(1)}, s32[16]{0:T(128)}, u32[]{:S(2)}) copy-start(s32[16]{0:T(128)} %param.25) | copy-start | bytes 196
  0.7 40.1 %copy-start.8 = (f32[16,3]{0,1:T(4,128)S(1)}, f32[16,3]{0,1:T(4,128)}, u32[]{:S(2)}) copy-start(f32[16,3]{0,1:T(4,128)} %param.23) | copy-start | bytes 580
  2.3 43.6 %collective-permute-start = (f32[4,32,256]{2,1,0:T(8,128)}, f32[4,32,256]{2,1,0:T(8,128)}, u32[]{:S(2)}, u32[]{:S(2)}) collective-permute-start(f32[4,32,256]{2,1,0:T(8,128)} %pad_maximum_fusion), channel_id=1, source_target_pairs={{1,0},{2,1},{3,2},{4,3},{5,4},{6,5},{7,6},{8,7},{9,8},{10,9},{11,1... | collective-permute-start | bytes 393224 | tf_op jit(solution)/shard_map/ppermute | solution.py:18
  6.8 50.7 %all-to-all-start = ((f32[16,32,256]{2,1,0:T(8,128)}), f32[16,32,256]{2,1,0:T(8,128)}, u32[]{:S(2)}, u32[]{:S(2)}) async-start(f32[16,32,256]{2,1,0:T(8,128)} %broadcast_multiply_fusion), calls=%async_computation | async-start | bytes 1048576 | tf_op jit(solution)/shard_map/all_to_all | solution.py:118
  49.2 55.0 %copy-start.4 = (f32[3,8,32,256]{3,2,1,0:T(8,128)}, f32[3,8,32,256]{3,2,1,0:T(8,128)S(1)}, u32[]{:S(2)}) copy-start(f32[3,8,32,256]{3,2,1,0:T(8,128)S(1)} %fusion.1) | copy-start | bytes 2359300
  52.0 52.2 %copy-start.5 = (f32[3,8,32,256]{3,2,1,0:T(8,128)}, f32[3,8,32,256]{3,2,1,0:T(8,128)S(1)}, u32[]{:S(2)}) copy-start(f32[3,8,32,256]{3,2,1,0:T(8,128)S(1)} %fusion) | copy-start | bytes 2359300
  52.1 3.2 %collective-permute-start.1 = (f32[4,32,256]{2,1,0:T(8,128)S(1)}, f32[4,32,256]{2,1,0:T(8,128)S(1)}, u32[]{:S(2)}, u32[]{:S(2)}) collective-permute-start(f32[4,32,256]{2,1,0:T(8,128)S(1)} %pad_maximum_fusion.1), channel_id=1, source_target_pairs={{0,1},{1,2},{2,3},{3,4},{4,5},{5,6},{6,7},{7,8},{8,9},{9,10},{10,1... | collective-permute-start | bytes 393224 | tf_op jit(solution)/shard_map/ppermute | solution.py:18
  104.2 66.4 %copy-start.1 = (f32[1,32,256]{2,1,0:T(8,128)S(1)}, f32[1,32,256]{2,1,0:T(8,128)}, u32[]{:S(2)}) copy-start(f32[1,32,256]{2,1,0:T(8,128)} %param.22) | copy-start | bytes 98308
  104.2 39.3 %copy-start.6 = (f32[3,8,32,256]{3,2,1,0:T(8,128)S(1)}, f32[3,8,32,256]{3,2,1,0:T(8,128)}, u32[]{:S(2)}) copy-start(f32[3,8,32,256]{3,2,1,0:T(8,128)} %copy.648) | copy-start | bytes 2359300
  104.2 39.3 %copy-start.7 = (f32[8,32,256]{2,1,0:T(8,128)S(1)}, f32[8,32,256]{2,1,0:T(8,128)}, u32[]{:S(2)}) copy-start(f32[8,32,256]{2,1,0:T(8,128)} %copy.644) | copy-start | bytes 786436
where the time goes:
time: 174 us; the launch traced here: 171 us
  local copies, waits for them, and re-layouts  108 us (62%)
  blocking collectives  23.4 us (13%)
  other arithmetic  19.4 us (11%)
  starting transfers between devices  12.4 us (7%)
  matrix products  4.06 us (2%)
  between operations  2.36 us (1%)
    sub x2, local copies, waits for them, and re-layouts, update_e(): return efield + (DT / permittivity)[None] * (curl - jnext + drive)  35.2 us
    all_to_all x1, blocking collectives, body(): lax.all_to_all(returned, 'gx', split_axis=0, concat_axis=0, tiled=True)  23.4 us
    scatter-add x1, local copies, waits for them, and re-layouts, body(): drive = jnp.zeros((3, depth, width_x, width_y), jnp.float32).at[:, zs, xs...  20.2 us
    scatter-add x1, local copies, waits for them, and re-layouts, body(): jnp.zeros((3, depth, width_x, width_y), jnp.float32).at[:, zm, xm, ym]  19.5 us
    unnamed x23, local copies, waits for them, and re-layouts  17.6 us
    all_to_all x1, starting transfers between devices, body(): lax.all_to_all(slots, 'gx', split_axis=0, concat_axis=0, tiled=True)  8.81 us
    slice x3, local copies, waits for them, and re-layouts, update_h(): ey_next = jnp.concatenate([ey[1:], upper[1][None]], 0)  4.59 us
    sub x1, other arithmetic, update_e(): return efield + (DT / permittivity)[None] * (curl - jnext + drive)  4.2 us
  transfers between devices with their start and end apart: 3, of which 1 were waited for; matrix products, arithmetic and copies ran while one was open for 24% of the time, Pallas kernels for 0%

commit v1 on v0

--- a/solution.py
+++ b/solution.py
@@ -98,45 +98,45 @@
     slab_start,
     radius,
 ):
-    count = lax.axis_size("gx")
     index = lax.axis_index("gx")
     depth, width_x, width_y = (e_forward.shape[1], e_forward.shape[2], e_forward.shape[3])
     start = slab_start[0]
     wx = band_matrix(width_x, radius[0])
     wy = band_matrix(width_y, radius[0])
-    planes = index * depth + jnp.arange(depth, dtype=jnp.int32) - start
-    select = (planes[:, None] == jnp.arange(count, dtype=jnp.int32)[None, :]).astype(jnp.float32)
     upper = passed_along(
         jnp.stack([e_forward[0, 0], e_forward[1, 0], e_adjoint[0, 0], e_adjoint[1, 0]]), "gx", -1
     )
     hf = update_h(e_forward, h_forward, upper[0:2])
     ha = update_h(e_adjoint, h_adjoint, upper[2:4])
-    owned = smooth(wx, wy, design)
-    holder = (start + index) // depth
-    target = (jnp.arange(count, dtype=jnp.int32) == holder).astype(jnp.float32)
-    slots = target[:, None, None] * owned
-    arrived = lax.all_to_all(slots, "gx", split_axis=0, concat_axis=0, tiled=True)
-    density = jnp.einsum("lo,oxy->lxy", select, arrived, precision=HIGH)
+    gathered = lax.all_gather(design, "gx", axis=0, tiled=True)
+    slab = gathered.shape[0]
+    planes = index * depth + jnp.arange(depth, dtype=jnp.int32) - start
+    valid = ((planes >= 0) & (planes < slab)).astype(jnp.float32)
+    picked = jnp.take(gathered, jnp.clip(planes, 0, slab - 1), axis=0) * valid[:, None, None]
+    density = smooth(wx, wy, picked)
     permittivity = 1.0 + EPS_RANGE * density
     strength = STRENGTH_BASE + STRENGTH_RANGE * density
     lower = passed_along(jnp.stack([hf[0, -1], hf[1, -1], ha[0, -1], ha[1, -1]]), "gx", 1)
     zs, xs, ys, inside_s = locate(source_cell, index * depth, depth, width_x, width_y)
+    nsrc = zs.shape[0]
+    comp = jnp.repeat(jnp.arange(3, dtype=jnp.int32), nsrc)
     drive = (
         jnp.zeros((3, depth, width_x, width_y), jnp.float32)
-        .at[:, zs, xs, ys]
-        .add(source_amp.T * inside_s[None, :])
+        .at[comp, jnp.tile(zs, 3), jnp.tile(xs, 3), jnp.tile(ys, 3)]
+        .add((source_amp.T * inside_s[None, :]).reshape(-1))
     )
     zm, xm, ym, inside_m = locate(monitor_cell, index * depth, depth, width_x, width_y)
-    probe = e_forward[:, zm, xm, ym] * inside_m[None, :]
-    drive_adj = jnp.zeros((3, depth, width_x, width_y), jnp.float32).at[:, zm, xm, ym].add(probe)
+    count = jnp.zeros((depth, width_x, width_y), jnp.float32).at[zm, xm, ym].add(inside_m)
+    drive_adj = count[None] * e_forward
     jf = update_j(j_forward, p_forward, e_forward, strength)
     ja = update_j(j_adjoint, p_adjoint, e_adjoint, strength)
     ef = update_e(e_forward, hf, lower[0:2], jf, permittivity, drive)
     ea = update_e(e_adjoint, ha, lower[2:4], ja, permittivity, drive_adj)
     intersection = jnp.sum(ea * (ef - e_forward + GAIN_FIELD * ef), axis=0)
+    slots = jnp.arange(slab, dtype=jnp.int32)
+    select = (planes[:, None] == slots[None, :]).astype(jnp.float32)
     returned = jnp.einsum("lo,lxy->oxy", select, intersection, precision=HIGH)
-    arrived_back = lax.all_to_all(returned, "gx", split_axis=0, concat_axis=0, tiled=True)
-    own_intersection = jnp.sum(arrived_back, axis=0, keepdims=True)
+    own_intersection = lax.psum_scatter(returned, "gx", scatter_dimension=0, tiled=True)
     design_grad = smooth_adjoint(wx, wy, own_intersection)
     return (ef, hf, ea, ha, design_grad)
 

time: 174 us -> 143 us (0.82); the launches traced: 171 us -> 142 us
  local copies, waits for them, and re-layouts: 108 us -> 22.6 us
  waiting for transfers between devices: 0.93 us -> 56.8 us
  between operations: 2.36 us -> 15.9 us
  starting transfers between devices: 12.4 us -> 3.57 us
  other arithmetic: 19.4 us -> 13.9 us
  blocking collectives: 23.4 us -> 25.4 us
    reduce_scatter x0 -> x1, waiting for transfers between devices: none -> 55.9 us  [body(): lax.psum_scatter(returned, 'gx', scatter_dimension=0, tiled=True)]
    scatter-add x2 -> x0, local copies, waits for them, and re-layouts: 39.7 us -> none  [the longest x1 20.2 us: body(): drive = jnp.zeros((3, depth, width_x, width_y), jnp.float32).at[:, zs, xs...]
    sub x2 -> x0, local copies, waits for them, and re-layouts: 35.2 us -> none  [update_e(): return efield + (DT / permittivity)[None] * (curl - jnext + drive)]
    all_gather x0 -> x1, blocking collectives: none -> 25.4 us  [body(): gathered = lax.all_gather(design, 'gx', axis=0, tiled=True)]
    all_to_all x1 -> x0, blocking collectives: 23.4 us -> none  [body(): lax.all_to_all(returned, 'gx', split_axis=0, concat_axis=0, tiled=True)]
    unnamed x23 -> x76, local copies, waits for them, and re-layouts: 17.6 us -> 7.77 us
    all_to_all x1 -> x0, starting transfers between devices: 8.81 us -> none  [body(): lax.all_to_all(slots, 'gx', split_axis=0, concat_axis=0, tiled=True)]
    sub x1, other arithmetic: 4.2 us -> 0.35 us  [update_e(): return efield + (DT / permittivity)[None] * (curl - jnext + drive)]
  transfers between devices with their start and end apart: 3 -> 3, of which waited for: 1 -> 2; matrix products, arithmetic and copies ran while one was open for 24% -> 12% of each run, Pallas kernels for 0% -> 0%
where the time goes in v1:
time: 143 us; the launch traced here: 142 us
  waiting for transfers between devices  56.8 us (40%)
  blocking collectives  25.4 us (18%)
  local copies, waits for them, and re-layouts  22.6 us (16%)
  between operations  15.9 us (11%)
  other arithmetic  13.9 us (10%)
  matrix products  4.26 us (3%)
  starting transfers between devices  3.57 us (2%)
    reduce_scatter x1, waiting for transfers between devices, body(): lax.psum_scatter(returned, 'gx', scatter_dimension=0, tiled=True)  55.9 us
    all_gather x1, blocking collectives, body(): gathered = lax.all_gather(design, 'gx', axis=0, tiled=True)  25.4 us
    unnamed x76, local copies, waits for them, and re-layouts  7.77 us
    scatter-add x1, other arithmetic, body(): drive = jnp.zeros((3, depth, width_x, width_y), jnp.float32).at[comp, jnp...  4.23 us
    slice x8, local copies, waits for them, and re-layouts, ahead(): rest = lax.slice_in_dim(field, 1, count, axis=axis)  4.17 us
    ppermute x2, starting transfers between devices, passed_along(): return lax.ppermute(block, axis, route)  3.54 us
  transfers between devices with their start and end apart: 3, of which 2 were waited for; matrix products, arithmetic and copies ran while one was open for 12% of the time, Pallas kernels for 0%

profile of v1, /device:TPU:0, one launch (start us, length us, event | category | flops | bytes accessed | tf_op | source)
XLA Modules:
  0.0 142.4 jit_solution(9310592674110908171)
XLA Ops:
  7.2 0.9 slice_bitcast_fusion.25
  8.8 1.3 collective-permute-start
  12.1 1.9 %slice_bitcast_fusion.17 = (f32[7,32,256]{2,1,0:T(8,128)}, f32[7,32,256]{2,1,0:T(8,128)}) fusion(f32[3,8,32,256]{3,2,1,0:T(8,128)} %param.18), kind=kLoop, calls=%fused_computation.73 | loop fusion | bytes 917504 | tf_op jit(solution)/shard_map/slice | solution.py:43
  14.0 0.8 slice_bitcast_fusion.19
  16.6 0.8 slice.269
  22.5 25.4 %all_gather.3 = f32[16,32,256]{2,1,0:T(8,128)S(1)} all-gather(f32[1,32,256]{2,1,0:T(8,128)} %param.22), channel_id=1, replica_groups=mesh['grp'=2,'gx'=16] {'gx'}, dimensions={0}, use_global_device_ids=true | all-gather | bytes 557056 | tf_op jit(solution)/shard_map/all_gather | solution.py:111
  48.7 0.8 copy-done.11
  49.6 0.8 slice.274
  53.1 1.3 add_divide_fusion
  54.5 1.6 %scatter_fusion.1 = f32[8,32,256]{2,1,0:T(8,128)S(1)} fusion(f32[8,32,256]{2,1,0:T(8,128)S(1)} %broadcast_in_dim.23, s32[16]{0:T(128)S(1)} %fusion.56, f32[16]{0:T(128)S(1)} %get-tuple-element.8), kind=kCustom, calls=%fused_computation.2 | custom fusion | flops 16 | bytes 384 | tf_op jit(solution)/shard_map/scatter-add | solution.py:129
  56.1 0.9 copy-done.10
  57.2 0.9 copy-done.20
  58.3 0.9 slice_bitcast_fusion.13
  59.2 0.9 slice_bitcast_fusion.2
  61.0 0.9 copy-done.21
  62.2 2.3 %collective-permute-start.1 = (f32[4,32,256]{2,1,0:T(8,128)S(1)}, f32[4,32,256]{2,1,0:T(8,128)S(1)}, u32[]{:S(2)}, u32[]{:S(2)}) collective-permute-start(f32[4,32,256]{2,1,0:T(8,128)S(1)} %pad_maximum_fusion.1), channel_id=1, source_target_pairs={{0,1},{1,2},{2,3},{3,4},{4,5},{5,6},{6,7},{7,8},{8,9},{9,10},{10,1... | collective-permute-start | bytes 393224 | tf_op jit(solution)/shard_map/ppermute | solution.py:18
  64.5 0.9 collective-permute-done.1
  67.3 4.2 %scatter_fusion = f32[3,8,32,256]{3,2,1,0:T(8,128)S(1)} fusion(f32[3,8,32,256]{3,2,1,0:T(8,128)S(1)} %maximum_subtract_fusion, s32[48]{0:T(128)S(1)} %fusion.59, f32[48]{0:T(128)S(1)} %reshape.207), kind=kCustom, calls=%fused_computation.1 | custom fusion | flops 48 | bytes 1344 | tf_op jit(solution)/shard_map/scatter-add | solution.py:126
  71.6 1.7 %fusion.18 = (f32[1,8,32,256]{3,2,1,0:T(8,128)S(1)}, f32[1,8,32,256]{3,2,1,0:T(8,128)S(1)}, f32[1,8,32,256]{3,2,1,0:T(8,128)S(1)}) fusion(f32[7,32,256]{2,1,0:T(8,128)} %get-tuple-element.28, f32[1,32,256]{2,1,0:T(8,128)S(1)} %get-tuple-element.61, f32[8,32,255]{2,1,0:T(8,128)} %bitcast.192, f32[3,8,32,256]{3,2,1,0:T(8,128)S(1)} %fusion.1, ...), kind=kLoop, calls=%fused_computation.43 | loop fusion | flops 720896 | bytes 3127296 | tf_op jit(solution)/shard_map/stack | solution.py:57
  73.5 1.8 %multiply_reduce_fusion = (f32[8,32,256]{2,1,0:T(8,128)S(1)}, f32[3,8,32,256]{3,2,1,0:T(8,128)}, f32[3,8,32,256]{3,2,1,0:T(8,128)}) fusion(f32[3,8,32,256]{3,2,1,0:T(8,128)S(1)} %copy-done, f32[3,8,32,256]{3,2,1,0:T(8,128)S(1)} %copy-done.1, f32[8,32,256]{2,1,0:T(8,128)S(1)} %scatter_fusion.1, f32[3,8,32,256]{3,2,1,0:T(8,128)S(1)} %copy-done.18, ...), kind=kLoop, calls=%fused_computation.15 | loop fusion | flops 3866624 | bytes 7340032 | tf_op jit(solution)/shard_map/reduce_sum | solution.py:135
  76.5 1.1 copy.22
  77.7 55.9 %reduce-scatter.2.cloned.1.call-done = f32[1,32,256]{2,1,0:T(8,128)} async-done(((f32[16,32,256]{2,1,0:T(8,128)}), f32[1,32,256]{2,1,0:T(8,128)}) %reduce-scatter.2.cloned.1.call-update) | async-done | bytes 32784 | tf_op jit(solution)/shard_map/reduce_scatter | solution.py:139
  133.6 1.0 convolution_bitcast_fusion.2
  134.6 0.9 convolution_bitcast_fusion.1
  (123 shorter events, 16.4 us)
Async XLA Ops:
  7.2 6.9 %copy-start = (f32[3,8,32,256]{3,2,1,0:T(8,128)S(1)}, f32[3,8,32,256]{3,2,1,0:T(8,128)}, u32[]{:S(2)}) copy-start(f32[3,8,32,256]{3,2,1,0:T(8,128)} %param.14) | copy-start | bytes 2359300
  7.2 126.4 %reduce-scatter.2.cloned.1.call-start = ((), (), s32[]{:S(2)}) async-start(), calls=%async_computation.1 | async-start | bytes 557056 | tf_op jit(solution)/shard_map/reduce_scatter | solution.py:139
  8.8 47.3 %collective-permute-start = (f32[4,32,256]{2,1,0:T(8,128)}, f32[4,32,256]{2,1,0:T(8,128)S(1)}, u32[]{:S(2)}, u32[]{:S(2)}) collective-permute-start(f32[4,32,256]{2,1,0:T(8,128)} %pad_maximum_fusion), channel_id=1, source_target_pairs={{1,0},{2,1},{3,2},{4,3},{5,4},{6,5},{7,6},{8,7},{9,8},{10,9},{11,1... | collective-permute-start | bytes 393224 | tf_op jit(solution)/shard_map/ppermute | solution.py:18
  12.1 2.7 %copy-start.1 = (f32[3,8,32,256]{3,2,1,0:T(8,128)S(1)}, f32[3,8,32,256]{3,2,1,0:T(8,128)}, u32[]{:S(2)}) copy-start(f32[3,8,32,256]{3,2,1,0:T(8,128)} %param.18) | copy-start | bytes 2359300
  54.4 1.6 %copy-start.23 = (s32[48,1]{0,1:T(1,128)S(1)}, s32[48,1]{0,1:T(1,128)}, u32[]{:S(2)}) copy-start(s32[48,1]{0,1:T(1,128)} %reshape.193) | copy-start | bytes 580
  54.4 1.6 %copy-start.24 = (s32[48,1]{0,1:T(1,128)S(1)}, s32[48,1]{0,1:T(1,128)}, u32[]{:S(2)}) copy-start(s32[48,1]{0,1:T(1,128)} %tile.32) | copy-start | bytes 580
  54.4 1.6 %copy-start.25 = (s32[48,1]{0,1:T(1,128)S(1)}, s32[48,1]{0,1:T(1,128)}, u32[]{:S(2)}) copy-start(s32[48,1]{0,1:T(1,128)} %tile.30) | copy-start | bytes 580
  54.4 1.6 %copy-start.26 = (s32[48,1]{0,1:T(1,128)S(1)}, s32[48,1]{0,1:T(1,128)}, u32[]{:S(2)}) copy-start(s32[48,1]{0,1:T(1,128)} %tile.13) | copy-start | bytes 580
  54.4 1.7 %copy-start.14 = (f32[7,32,256]{2,1,0:T(8,128)S(1)}, f32[7,32,256]{2,1,0:T(8,128)}, u32[]{:S(2)}) copy-start(f32[7,32,256]{2,1,0:T(8,128)} %get-tuple-element.48) | copy-start | bytes 688132
  54.4 1.7 %copy-start.15 = (f32[7,32,256]{2,1,0:T(8,128)S(1)}, f32[7,32,256]{2,1,0:T(8,128)}, u32[]{:S(2)}) copy-start(f32[7,32,256]{2,1,0:T(8,128)} %get-tuple-element.49) | copy-start | bytes 688132
  58.3 13.2 %copy-start.2 = (f32[3,8,32,256]{3,2,1,0:T(8,128)}, f32[3,8,32,256]{3,2,1,0:T(8,128)S(1)}, u32[]{:S(2)}) copy-start(f32[3,8,32,256]{3,2,1,0:T(8,128)S(1)} %fusion.1) | copy-start | bytes 2359300
  59.2 1.4 copy-start.8
  59.2 1.5 %copy-start.9 = (f32[8,31,256]{2,1,0:T(8,128)S(1)}, f32[8,31,256]{2,1,0:T(8,128)}, u32[]{:S(2)}) copy-start(f32[8,31,256]{2,1,0:T(8,128)} %slice.273) | copy-start | bytes 761860
  59.2 1.5 %copy-start.12 = (f32[7,32,256]{2,1,0:T(8,128)S(1)}, f32[7,32,256]{2,1,0:T(8,128)}, u32[]{:S(2)}) copy-start(f32[7,32,256]{2,1,0:T(8,128)} %get-tuple-element.38) | copy-start | bytes 688132
  59.2 1.6 %copy-start.13 = (f32[7,32,256]{2,1,0:T(8,128)S(1)}, f32[7,32,256]{2,1,0:T(8,128)}, u32[]{:S(2)}) copy-start(f32[7,32,256]{2,1,0:T(8,128)} %get-tuple-element.39) | copy-start | bytes 688132
  62.1 3.4 %copy-start.3 = (f32[3,8,32,256]{3,2,1,0:T(8,128)}, f32[3,8,32,256]{3,2,1,0:T(8,128)S(1)}, u32[]{:S(2)}) copy-start(f32[3,8,32,256]{3,2,1,0:T(8,128)S(1)} %fusion) | copy-start | bytes 2359300
  62.2 3.2 %collective-permute-start.1 = (f32[4,32,256]{2,1,0:T(8,128)S(1)}, f32[4,32,256]{2,1,0:T(8,128)S(1)}, u32[]{:S(2)}, u32[]{:S(2)}) collective-permute-start(f32[4,32,256]{2,1,0:T(8,128)S(1)} %pad_maximum_fusion.1), channel_id=1, source_target_pairs={{0,1},{1,2},{2,3},{3,4},{4,5},{5,6},{6,7},{7,8},{8,9},{9,10},{10,1... | collective-permute-start | bytes 393224 | tf_op jit(solution)/shard_map/ppermute | solution.py:18
  65.5 1.4 %copy-start.17 = (f32[3,8,32,256]{3,2,1,0:T(8,128)S(1)}, f32[3,8,32,256]{3,2,1,0:T(8,128)}, u32[]{:S(2)}) copy-start(f32[3,8,32,256]{3,2,1,0:T(8,128)} %param.17) | copy-start | bytes 2359300
  71.5 1.8 %copy-start.5 = (f32[8,32,256]{2,1,0:T(8,128)S(1)}, f32[8,32,256]{2,1,0:T(8,128)}, u32[]{:S(2)}) copy-start(f32[8,32,256]{2,1,0:T(8,128)} %get-tuple-element.58) | copy-start | bytes 786436
  71.5 1.8 %copy-start.18 = (f32[3,8,32,256]{3,2,1,0:T(8,128)S(1)}, f32[3,8,32,256]{3,2,1,0:T(8,128)}, u32[]{:S(2)}) copy-start(f32[3,8,32,256]{3,2,1,0:T(8,128)} %param.20) | copy-start | bytes 2359300
  71.5 1.9 %copy-start.19 = (f32[3,8,32,256]{3,2,1,0:T(8,128)S(1)}, f32[3,8,32,256]{3,2,1,0:T(8,128)}, u32[]{:S(2)}) copy-start(f32[3,8,32,256]{3,2,1,0:T(8,128)} %param.21) | copy-start | bytes 2359300
  71.5 2.0 %copy-start.22 = (f32[8,32,256]{2,1,0:T(8,128)S(1)}, f32[8,32,256]{2,1,0:T(8,128)}, u32[]{:S(2)}) copy-start(f32[8,32,256]{2,1,0:T(8,128)} %get-tuple-element.57) | copy-start | bytes 786436
  77.6 55.9 %copy-start.34 = (f32[32]{0:T(128)S(1)}, f32[32]{0:T(128)}, u32[]{:S(2)}) copy-start(f32[32]{0:T(128)} %convert_reduce_fusion.1) | copy-start | bytes 388
  77.7 57.0 %copy-start.37 = (f32[256]{0:T(256)S(1)}, f32[256]{0:T(256)}, u32[]{:S(2)}) copy-start(f32[256]{0:T(256)} %convert_reduce_fusion) | copy-start | bytes 3076
  (17 other events, 14.4 us)
Sparse Core Ops, SparseCore 0:
  77.8 55.7 reduce-scatter.1

commit v2 on v0

v2 whole, which is shorter than its diff:
```python
import functools

import jax
import jax.numpy as jnp
from jax import lax
from jax.experimental import pallas as pl
from jax.experimental.pallas import tpu as pltpu
from jax.sharding import PartitionSpec as P

DT = 0.5
EPS_RANGE = 10.0
STRENGTH_BASE = 0.5
STRENGTH_RANGE = 3.0
DAMPING = 0.2
GAIN_FIELD = 0.25
HIGH = lax.Precision.HIGHEST
KEEP = 1.0 - DAMPING * DT / 2.0
LOSS = 1.0 + DAMPING * DT / 2.0


def passed_along(block, axis, distance):
    devices = range(lax.axis_size(axis))
    route = [(i - distance, i) for i in devices if i - distance in devices]
    return lax.ppermute(block, axis, route)


def band_matrix(count, radius):
    rows = jnp.arange(count, dtype=jnp.int32)
    dist = jnp.abs(rows[:, None] - rows[None, :])
    weights = jnp.maximum(radius + 1 - dist, 0).astype(jnp.float32)
    return weights / jnp.sum(weights, axis=1, keepdims=True)


def smooth(wx, wy, planes):
    inner = jnp.einsum("ax,zxy->zay", wx, planes, precision=HIGH)
    return jnp.einsum("zay,by->zab", inner, wy, precision=HIGH)


def smooth_adjoint(wx, wy, planes):
    inner = jnp.einsum("ax,zab->zxb", wx, planes, precision=HIGH)
    return jnp.einsum("zxb,by->zxy", inner, wy, precision=HIGH)


def field_kernel(
    ef, hf, pf, jf, ea, ha, pa, ja, rho, upper, below, src, mon, amp,
    ef_o, hf_o, ea_o, ha_o, inter_o,
):
    depth, width_x, width_y = rho.shape
    index = lax.axis_index("gx")
    row = lax.broadcasted_iota(jnp.int32, (width_x, width_y), 0)
    lane = lax.broadcasted_iota(jnp.int32, (width_x, width_y), 1)

    def ahead_y(f):
        return jnp.where(lane == width_y - 1, 0.0, pltpu.roll(f, width_y - 1, 1))

    def ahead_x(f):
        return jnp.where(row == width_x - 1, 0.0, pltpu.roll(f, width_x - 1, 0))

    def behind_y(f):
        return jnp.where(lane == 0, 0.0, pltpu.roll(f, 1, 1))

    def behind_x(f):
        return jnp.where(row == 0, 0.0, pltpu.roll(f, 1, 0))

    def new_h(e, h, z, ex_up, ey_up):
        ex, ey, ez = e[0, z], e[1, z], e[2, z]
        curl_x = ahead_y(ez) - ez - (ey_up - ey)
        curl_y = ex_up - ex - (ahead_x(ez) - ez)
        curl_z = ahead_x(ey) - ey - (ahead_y(ex) - ex)
        return (h[0, z] - DT * curl_x, h[1, z] - DT * curl_y, h[2, z] - DT * curl_z)

    def lower_h(e, base):
        hx, hy, ex, ey, ez = (below[base + i] for i in range(5))
        curl_x = ahead_y(ez) - ez - (e[1, 0] - ey)
        curl_y = e[0, 0] - ex - (ahead_x(ez) - ez)
        keep = index > 0
        return (
            jnp.where(keep, hx - DT * curl_x, 0.0),
            jnp.where(keep, hy - DT * curl_y, 0.0),
        )

    def new_e(e, p, j, out, z, hn, hn_dn, step, strength):
        hx, hy, hz = hn
        hx_dn, hy_dn = hn_dn
        curl = (
            hz - behind_y(hz) - (hy - hy_dn),
            hx - hx_dn - (hz - behind_x(hz)),
            hy - behind_x(hy) - (hx - behind_y(hx)),
        )
        for c in range(3):
            j_next = (KEEP * j[c, z] + DT * (strength * e[c, z] - p[c, z])) / LOSS
            out[c, z] = e[c, z] + step * (curl[c] - j_next)

    runs = ((ef, hf, pf, jf, hf_o, ef_o, 0), (ea, ha, pa, ja, ha_o, ea_o, 2))
    prev = [lower_h(ef, 0), lower_h(ea, 5)]
    for z in range(depth):
        density = rho[z]
        step = DT / (1.0 + EPS_RANGE * density)
        strength = STRENGTH_BASE + STRENGTH_RANGE * density
        for r, (e, h, p, j, h_out, e_out, up) in enumerate(runs):
            if z + 1 < depth:
                ex_up, ey_up = e[0, z + 1], e[1, z + 1]
            else:
                ex_up, ey_up = upper[up], upper[up + 1]
            hn = new_h(e, h, z, ex_up, ey_up)
            for c in range(3):
                h_out[c, z] = hn[c]
            new_e(e, p, j, e_out, z, hn, prev[r], step, strength)
            prev[r] = (hn[0], hn[1])

    plane = width_x * width_y
    tile_row = lax.broadcasted_iota(jnp.int32, (8, width_y), 0)
    tile_lane = lax.broadcasted_iota(jnp.int32, (8, width_y), 1)

    def add_at(cell, out, value_of):
        zz = cell // plane
        local = zz - index * depth
        rest = cell - zz * plane
        x = rest // width_y
        y = rest - x * width_y
        x0 = pl.multiple_of((x // 8) * 8, 8)

        @pl.when((local >= 0) & (local < depth))
        def _():
            rows = pl.ds(x0, 8)
            hit = (tile_row == x - x0) & (tile_lane == y)
            step = DT / (1.0 + EPS_RANGE * rho[local, rows, :])
            for c in range(3):
                held = out[c, local, rows, :]
                out[c, local, rows, :] = held + jnp.where(hit, step * value_of(c, local, rows), 0.0)

    for s in range(src.shape[0]):
        add_at(src[s], ef_o, lambda c, local, rows, s=s: amp[s, c])
    for m in range(mon.shape[0]):
        add_at(mon[m], ea_o, lambda c, local, rows: ef[c, local, rows, :])

    for z in range(depth):
        total = None
        for c in range(3):
            fwd = ef_o[c, z]
            term = ea_o[c, z] * (fwd - ef[c, z] + GAIN_FIELD * fwd)
            total = term if total is None else total + term
        inter_o[z] = total


def fields(e_forward, h_forward, p_forward, j_forward, e_adjoint, h_adjoint, p_adjoint, j_adjoint,
           density, upper, below, source_cell, monitor_cell, source_amp):
    shape = e_forward.shape
    depth = shape[1]
    field = jax.ShapeDtypeStruct(shape, jnp.float32)
    vmem = pl.BlockSpec(memory_space=pltpu.VMEM)
    smem = pl.BlockSpec(memory_space=pltpu.SMEM)
    cells = shape[1] * shape[2] * shape[3]
    return pl.pallas_call(
        field_kernel,
        out_shape=(field, field, field, field, jax.ShapeDtypeStruct(shape[1:], jnp.float32)),
        in_specs=[vmem] * 11 + [smem] * 3,
        out_specs=(vmem,) * 5,
        compiler_params=pltpu.CompilerParams(vmem_limit_bytes=48 * 1024 * 1024),
        cost_estimate=pl.CostEstimate(
            flops=200 * cells, bytes_accessed=4 * cells * 40, transcendentals=0
        ),
    )(e_forward, h_forward, p_forward, j_forward, e_adjoint, h_adjoint, p_adjoint, j_adjoint,
      density, upper, below, source_cell, monitor_cell, source_amp)


def body(
    e_forward,
    h_forward,
    p_forward,
    j_forward,
    e_adjoint,
    h_adjoint,
    p_adjoint,
    j_adjoint,
    design,
    source_amp,
    source_cell,
    monitor_cell,
    slab_start,
    radius,
):
    count = lax.axis_size("gx")
    index = lax.axis_index("gx")
    depth, width_x, width_y = (e_forward.shape[1], e_forward.shape[2], e_forward.shape[3])
    start = slab_start[0]
    wx = band_matrix(width_x, radius[0])
    wy = band_matrix(width_y, radius[0])
    planes = index * depth + jnp.arange(depth, dtype=jnp.int32) - start
    select = (planes[:, None] == jnp.arange(count, dtype=jnp.int32)[None, :]).astype(jnp.float32)
    upper = passed_along(
        jnp.stack([e_forward[0, 0], e_forward[1, 0], e_adjoint[0, 0], e_adjoint[1, 0]]), "gx", -1
    )
    below = passed_along(
        jnp.stack(
            [h_forward[0, -1], h_forward[1, -1], e_forward[0, -1], e_forward[1, -1], e_forward[2, -1],
             h_adjoint[0, -1], h_adjoint[1, -1], e_adjoint[0, -1], e_adjoint[1, -1], e_adjoint[2, -1]]
        ),
        "gx",
        1,
    )
    owned = smooth(wx, wy, design)
    holder = (start + index) // depth
    target = (jnp.arange(count, dtype=jnp.int32) == holder).astype(jnp.float32)
    slots = target[:, None, None] * owned
    arrived = lax.all_to_all(slots, "gx", split_axis=0, concat_axis=0, tiled=True)
    density = jnp.einsum("lo,oxy->lxy", select, arrived, precision=HIGH)
    ef, hf, ea, ha, intersection = fields(
        e_forward, h_forward, p_forward, j_forward, e_adjoint, h_adjoint, p_adjoint, j_adjoint,
        density, upper, below, source_cell, monitor_cell, source_amp,
    )
    returned = jnp.einsum("lo,lxy->oxy", select, intersection, precision=HIGH)
    arrived_back = lax.all_to_all(returned, "gx", split_axis=0, concat_axis=0, tiled=True)
    own_intersection = jnp.sum(arrived_back, axis=0, keepdims=True)
    design_grad = smooth_adjoint(wx, wy, own_intersection)
    return (ef, hf, ea, ha, design_grad)


def solution(mesh):
    return jax.shard_map(
        body,
        mesh=mesh,
        in_specs=(
            P(None, ("grp", "gx"), None, None),
            P(None, ("grp", "gx"), None, None),
            P(None, ("grp", "gx"), None, None),
            P(None, ("grp", "gx"), None, None),
            P(None, ("grp", "gx"), None, None),
            P(None, ("grp", "gx"), None, None),
            P(None, ("grp", "gx"), None, None),
            P(None, ("grp", "gx"), None, None),
            P(("grp", "gx"), None, None),
            P("grp", None),
            P("grp"),
            P("grp"),
            P("grp"),
            P("grp"),
        ),
        out_specs=(
            P(None, ("grp", "gx"), None, None),
            P(None, ("grp", "gx"), None, None),
            P(None, ("grp", "gx"), None, None),
            P(None, ("grp", "gx"), None, None),
            P(("grp", "gx"), None, None),
        ),
        check_vma=False,
    )
```

time: 174 us -> 61.7 us (0.35); the launches traced: 171 us -> 61.2 us
  local copies, waits for them, and re-layouts: 108 us -> 9.92 us
  other arithmetic: 19.4 us -> 1.87 us
  Pallas kernels: 0 us -> 5.56 us
  waiting for transfers between devices: 0.93 us -> 5.96 us
  blocking collectives: 23.4 us -> 19.1 us
    scatter-add x2 -> x0, local copies, waits for them, and re-layouts: 39.7 us -> none  [the longest x1 20.2 us: body(): drive = jnp.zeros((3, depth, width_x, width_y), jnp.float32).at[:, zs, xs...]
    sub x2 -> x0, local copies, waits for them, and re-layouts: 35.2 us -> none  [update_e(): return efield + (DT / permittivity)[None] * (curl - jnext + drive)]
    unnamed x23 -> x30, local copies, waits for them, and re-layouts: 17.6 us -> 7.34 us
    slice x14 -> x0, local copies, waits for them, and re-layouts: 8.12 us -> none  [the longest x3 4.59 us: update_h(): ey_next = jnp.concatenate([ey[1:], upper[1][None]], 0)]
    sub x3 -> x0, other arithmetic: 6.69 us -> none  [the longest x1 4.2 us: update_e(): return efield + (DT / permittivity)[None] * (curl - jnext + drive)]
    all_to_all x1, waiting for transfers between devices: 0.01 us -> 5.95 us  [body(): lax.all_to_all(slots, 'gx', split_axis=0, concat_axis=0, tiled=True)]
    pallas_call x0 -> x1, Pallas kernels: none -> 5.56 us  [fields(): pl.pallas_call(field_kernel, out_shape=(field, field, field, field, jax.S...]
    another operation x5 -> x0, other arithmetic: 4.8 us -> none  [the longest x2 2.67 us: update_h(): return hfield - DT * jnp.stack([curl_x, curl_y, curl_z])]
  transfers between devices with their start and end apart: 3 -> 3, of which waited for: 1 -> 1; matrix products, arithmetic and copies ran while one was open for 24% -> 16% of each run, Pallas kernels for 0% -> 0%
where the time goes in v2:
time: 61.7 us; the launch traced here: 61.2 us
  blocking collectives  19.1 us (31%)
  starting transfers between devices  12.5 us (20%)
  local copies, waits for them, and re-layouts  9.92 us (16%)
  waiting for transfers between devices  5.96 us (10%)
  Pallas kernels  5.56 us (9%)
  matrix products  4.1 us (7%)
  between operations  2.15 us (3%)
  other arithmetic  1.87 us (3%)
    all_to_all x1, blocking collectives, body(): lax.all_to_all(returned, 'gx', split_axis=0, concat_axis=0, tiled=True)  19.1 us
    all_to_all x1, starting transfers between devices, body(): lax.all_to_all(slots, 'gx', split_axis=0, concat_axis=0, tiled=True)  8.95 us
    unnamed x30, local copies, waits for them, and re-layouts  7.34 us
    all_to_all x1, waiting for transfers between devices, body(): lax.all_to_all(slots, 'gx', split_axis=0, concat_axis=0, tiled=True)  5.95 us
    pallas_call x1, Pallas kernels, fields(): pl.pallas_call(field_kernel, out_shape=(field, field, field, field, jax.S...  5.56 us
    ppermute x2, starting transfers between devices, passed_along(): return lax.ppermute(block, axis, route)  3.55 us
    dot_general x1, matrix products, body(): density = jnp.einsum('lo,oxy->lxy', select, arrived, precision=HIGH)  1.7 us
    another operation x2, local copies, waits for them, and re-layouts, body(): jnp.stack([e_forward[0, 0], e_forward[1, 0], e_adjoint[0, 0], e_adjoint[1...  1.57 us
  transfers between devices with their start and end apart: 3, of which 1 were waited for; matrix products, arithmetic and copies ran while one was open for 16% of the time, Pallas kernels for 0%

profile of v2, /device:TPU:0, one launch (start us, length us, event | category | flops | bytes accessed | tf_op | source)
XLA Modules:
  0.0 61.2 jit_solution(18440181491225977242)
XLA Ops:
  0.6 0.8 %slice_bitcast_fusion.3 = (f32[1,32,256]{2,1,0:T(8,128)S(1)}, f32[1,32,256]{2,1,0:T(8,128)S(1)}) fusion(f32[3,8,32,256]{3,2,1,0:T(8,128)} %ef.1), kind=kLoop, calls=%fused_computation.33 | loop fusion | bytes 131072 | tf_op jit(solution)/shard_map/stack;squeeze | solution.py:192
  1.4 0.8 %slice_bitcast_fusion.1 = (f32[1,32,256]{2,1,0:T(8,128)S(1)}, f32[1,32,256]{2,1,0:T(8,128)S(1)}) fusion(f32[3,8,32,256]{3,2,1,0:T(8,128)} %ea.1), kind=kLoop, calls=%fused_computation.31 | loop fusion | bytes 131072 | tf_op jit(solution)/shard_map/stack;squeeze | solution.py:192
  2.2 0.7 %pad_maximum_fusion = f32[4,32,256]{2,1,0:T(8,128)} fusion(f32[1,32,256]{2,1,0:T(8,128)S(1)} %get-tuple-element.18, f32[1,32,256]{2,1,0:T(8,128)S(1)} %get-tuple-element.17, f32[1,32,256]{2,1,0:T(8,128)S(1)} %get-tuple-element.16, f32[1,32,256]{2,1,0:T(8,128)S(1)} %get-tuple-element.15), kind=kLoop, calls=%fused_computation.11 | loop fusion | flops 98304 | bytes 262144 | tf_op jit(solution)/shard_map/stack | solution.py:192
  2.9 1.3 %collective-permute-start = (f32[4,32,256]{2,1,0:T(8,128)}, f32[4,32,256]{2,1,0:T(8,128)}, u32[]{:S(2)}, u32[]{:S(2)}) collective-permute-start(f32[4,32,256]{2,1,0:T(8,128)} %pad_maximum_fusion), channel_id=1, source_target_pairs={{1,0},{2,1},{3,2},{4,3},{5,4},{6,5},{7,6},{8,7},{9,8},{10,9},{11,1... | collective-permute-start | bytes 393224 | tf_op jit(solution)/shard_map/ppermute | solution.py:24
  6.5 0.9 %broadcast_multiply_fusion = f32[16,32,256]{2,1,0:T(8,128)} fusion(f32[32,256]{1,0:T(8,128)S(1)} %fusion.4, f32[16]{0:T(128)S(1)} %compare_convert_fusion), kind=kLoop, calls=%fused_computation.6 | loop fusion | flops 131072 | bytes 557120 | tf_op jit(solution)/shard_map/mul | solution.py:205
  7.4 8.9 %all-to-all-start = ((f32[16,32,256]{2,1,0:T(8,128)}), f32[16,32,256]{2,1,0:T(8,128)}, u32[]{:S(2)}, u32[]{:S(2)}) async-start(f32[16,32,256]{2,1,0:T(8,128)} %broadcast_multiply_fusion), calls=%async_computation | async-start | bytes 1048576 | tf_op jit(solution)/shard_map/all_to_all | solution.py:206
  16.3 0.6 %bitcast_dynamic-update-slice_fusion.9 = f32[10,32,256]{2,1,0:T(8,128)} fusion(f32[3,8,32,256]{3,2,1,0:T(8,128)S(1)} %copy-done.3), kind=kLoop, calls=%fused_computation.27 | loop fusion | bytes 65536
  17.0 0.6 %bitcast_dynamic-update-slice_fusion.8 = f32[10,32,256]{2,1,0:T(8,128)} fusion(f32[10,32,256]{2,1,0:T(8,128)} %bitcast_dynamic-update-slice_fusion.9, f32[3,8,32,256]{3,2,1,0:T(8,128)S(1)} %copy-done.3), kind=kLoop, calls=%fused_computation.26 | loop fusion | bytes 65536
  17.6 0.6 %bitcast_dynamic-update-slice_fusion.7 = f32[10,32,256]{2,1,0:T(8,128)} fusion(f32[10,32,256]{2,1,0:T(8,128)} %bitcast_dynamic-update-slice_fusion.8, f32[3,8,32,256]{3,2,1,0:T(8,128)S(1)} %copy-done.1), kind=kLoop, calls=%fused_computation.25 | loop fusion | bytes 65536
  18.2 0.6 %bitcast_dynamic-update-slice_fusion.6 = f32[10,32,256]{2,1,0:T(8,128)} fusion(f32[10,32,256]{2,1,0:T(8,128)} %bitcast_dynamic-update-slice_fusion.7, f32[3,8,32,256]{3,2,1,0:T(8,128)S(1)} %copy-done.1), kind=kLoop, calls=%fused_computation.24 | loop fusion | bytes 65536
  18.8 0.6 %bitcast_dynamic-update-slice_fusion.5 = f32[10,32,256]{2,1,0:T(8,128)} fusion(f32[10,32,256]{2,1,0:T(8,128)} %bitcast_dynamic-update-slice_fusion.6, f32[3,8,32,256]{3,2,1,0:T(8,128)S(1)} %copy-done.1), kind=kLoop, calls=%fused_computation.23 | loop fusion | bytes 65536
  19.4 0.6 %bitcast_dynamic-update-slice_fusion.4 = f32[10,32,256]{2,1,0:T(8,128)} fusion(f32[10,32,256]{2,1,0:T(8,128)} %bitcast_dynamic-update-slice_fusion.5, f32[3,8,32,256]{3,2,1,0:T(8,128)S(1)} %copy-done.4), kind=kLoop, calls=%fused_computation.22 | loop fusion | bytes 65536
  20.1 0.6 %bitcast_dynamic-update-slice_fusion.3 = f32[10,32,256]{2,1,0:T(8,128)} fusion(f32[10,32,256]{2,1,0:T(8,128)} %bitcast_dynamic-update-slice_fusion.4, f32[3,8,32,256]{3,2,1,0:T(8,128)S(1)} %copy-done.4), kind=kLoop, calls=%fused_computation.21 | loop fusion | bytes 65536
  20.7 0.6 %bitcast_dynamic-update-slice_fusion.2 = f32[10,32,256]{2,1,0:T(8,128)} fusion(f32[10,32,256]{2,1,0:T(8,128)} %bitcast_dynamic-update-slice_fusion.3, f32[3,8,32,256]{3,2,1,0:T(8,128)S(1)} %copy-done.2), kind=kLoop, calls=%fused_computation.20 | loop fusion | bytes 65536
  21.3 0.6 %bitcast_dynamic-update-slice_fusion.1 = f32[10,32,256]{2,1,0:T(8,128)} fusion(f32[10,32,256]{2,1,0:T(8,128)} %bitcast_dynamic-update-slice_fusion.2, f32[3,8,32,256]{3,2,1,0:T(8,128)S(1)} %copy-done.2), kind=kLoop, calls=%fused_computation.19 | loop fusion | bytes 65536
  21.9 0.6 %bitcast_dynamic-update-slice_fusion = f32[10,32,256]{2,1,0:T(8,128)} fusion(f32[10,32,256]{2,1,0:T(8,128)} %bitcast_dynamic-update-slice_fusion.1, f32[3,8,32,256]{3,2,1,0:T(8,128)S(1)} %copy-done.2), kind=kLoop, calls=%fused_computation.18 | loop fusion | bytes 65536 | tf_op jit(solution)/shard_map/stack | solution.py:195
  22.5 2.3 %collective-permute-start.1 = (f32[10,32,256]{2,1,0:T(8,128)}, f32[10,32,256]{2,1,0:T(8,128)S(1)}, u32[]{:S(2)}, u32[]{:S(2)}) collective-permute-start(f32[10,32,256]{2,1,0:T(8,128)} %bitcast_dynamic-update-slice_fusion), channel_id=1, source_target_pairs={{0,1},{1,2},{2,3},{3,4},{4,5},{5,6},{6,7},{7,8},{8,9},{9,10},{10,1... | collective-permute-start | bytes 983048 | tf_op jit(solution)/shard_map/ppermute | solution.py:24
  24.9 6.0 %all-to-all-done = f32[16,32,256]{2,1,0:T(8,128)} async-done(((f32[16,32,256]{2,1,0:T(8,128)}), f32[16,32,256]{2,1,0:T(8,128)}, u32[]{:S(2)}, u32[]{:S(2)}) %all-to-all-start) | async-done | bytes 524320 | tf_op jit(solution)/shard_map/all_to_all | solution.py:206
  30.9 1.7 %fusion = f32[8,32,256]{2,0,1:T(8,128)S(1)} fusion(f32[16,32,256]{2,1,0:T(8,128)} %all-to-all-done, s32[8]{0:T(128)S(1)} %add_subtract_fusion), kind=kOutput, calls=%fused_computation.2 | convolution fusion | flops 12583040 | bytes 786464 | tf_op jit(solution)/shard_map/lo,oxy->lxy/dot_general | solution.py:207
  33.2 1.1 %copy-done.6 = f32[3,8,32,256]{3,2,1,0:T(8,128)S(1)} copy-done((f32[3,8,32,256]{3,2,1,0:T(8,128)S(1)}, f32[3,8,32,256]{3,2,1,0:T(8,128)}, u32[]{:S(2)}) %copy-start.6) | copy-done | bytes 786456
  34.4 5.6 %shard_map.173 = (f32[3,8,32,256]{3,2,1,0:T(8,128)}, f32[3,8,32,256]{3,2,1,0:T(8,128)}, f32[3,8,32,256]{3,2,1,0:T(8,128)}, f32[3,8,32,256]{3,2,1,0:T(8,128)}, f32[8,32,256]{2,1,0:T(8,128)S(1)}) custom-call(f32[3,8,32,256]{3,2,1,0:T(8,128)S(1)} %copy-done.1, f32[3,8,32,256]{3,2,1,0:T(8,128)S(1)} %copy-done.3, f32[3,8,32,256]{3,2,1,0:T(8,128)S(1)} %copy-done.5, ...), custom_call_target="tpu_custom_call" | custom-call | flops 13107200 | bytes 10485760 | tf_op jit(solution)/shard_map/pallas_call | solution.py:154
  39.9 0.5 fusion.2
  40.8 19.1 %all_to_all.10 = f32[16,32,256]{2,1,0:T(8,128)S(1)} all-to-all(f32[16,32,256]{2,1,0:T(8,128)S(1)} %copy.33), channel_id=1, replica_groups=mesh['grp'=2,'gx'=16] {'gx'}, dimensions={0} | all-to-all | bytes 1048576 | tf_op jit(solution)/shard_map/all_to_all | solution.py:213
  60.2 0.9 %convolution_bitcast_fusion = f32[1,32,256]{2,1,0:T(8,128)} fusion(f32[32,256]{1,0:T(8,128)S(1)} %convolution_bitcast_fusion.1, f32[256]{0:T(256)S(1)} %convert_reduce_fusion, s32[]{:T(128)} %bitcast.2), kind=kOutput, calls=%fused_computation | convolution fusion | flops 25559040 | bytes 66564 | tf_op jit(solution)/shard_map/zxb,by->zxy/dot_general | solution.py:41
  (32 shorter events, 2.3 us)
Async XLA Ops:
  0.6 5.1 %copy-start = (f32[1,32,256]{2,1,0:T(8,128)S(1)}, f32[1,32,256]{2,1,0:T(8,128)}, u32[]{:S(2)}) copy-start(f32[1,32,256]{2,1,0:T(8,128)} %param.22) | copy-start | bytes 98308
  2.9 29.8 %collective-permute-start = (f32[4,32,256]{2,1,0:T(8,128)}, f32[4,32,256]{2,1,0:T(8,128)}, u32[]{:S(2)}, u32[]{:S(2)}) collective-permute-start(f32[4,32,256]{2,1,0:T(8,128)} %pad_maximum_fusion), channel_id=1, source_target_pairs={{1,0},{2,1},{3,2},{4,3},{5,4},{6,5},{7,6},{8,7},{9,8},{10,9},{11,1... | collective-permute-start | bytes 393224 | tf_op jit(solution)/shard_map/ppermute | solution.py:24
  6.0 10.3 %copy-start.3 = (f32[3,8,32,256]{3,2,1,0:T(8,128)S(1)}, f32[3,8,32,256]{3,2,1,0:T(8,128)}, u32[]{:S(2)}) copy-start(f32[3,8,32,256]{3,2,1,0:T(8,128)} %hf.1) | copy-start | bytes 2359300
  6.0 13.4 %copy-start.4 = (f32[3,8,32,256]{3,2,1,0:T(8,128)S(1)}, f32[3,8,32,256]{3,2,1,0:T(8,128)}, u32[]{:S(2)}) copy-start(f32[3,8,32,256]{3,2,1,0:T(8,128)} %ha.1) | copy-start | bytes 2359300
  6.5 11.1 %copy-start.1 = (f32[3,8,32,256]{3,2,1,0:T(8,128)S(1)}, f32[3,8,32,256]{3,2,1,0:T(8,128)}, u32[]{:S(2)}) copy-start(f32[3,8,32,256]{3,2,1,0:T(8,128)} %ef.1) | copy-start | bytes 2359300
  7.4 13.3 %copy-start.2 = (f32[3,8,32,256]{3,2,1,0:T(8,128)S(1)}, f32[3,8,32,256]{3,2,1,0:T(8,128)}, u32[]{:S(2)}) copy-start(f32[3,8,32,256]{3,2,1,0:T(8,128)} %ea.1) | copy-start | bytes 2359300
  7.4 23.5 %all-to-all-start = ((f32[16,32,256]{2,1,0:T(8,128)}), f32[16,32,256]{2,1,0:T(8,128)}, u32[]{:S(2)}, u32[]{:S(2)}) async-start(f32[16,32,256]{2,1,0:T(8,128)} %broadcast_multiply_fusion), calls=%async_computation | async-start | bytes 1048576 | tf_op jit(solution)/shard_map/all_to_all | solution.py:206
  21.9 2.9 %copy-start.9 = (f32[16,3]{0,1:T(4,128)S(1)}, f32[16,3]{0,1:T(4,128)}, u32[]{:S(2)}) copy-start(f32[16,3]{0,1:T(4,128)} %param.23) | copy-start | bytes 580
  22.5 10.2 %collective-permute-start.1 = (f32[10,32,256]{2,1,0:T(8,128)}, f32[10,32,256]{2,1,0:T(8,128)S(1)}, u32[]{:S(2)}, u32[]{:S(2)}) collective-permute-start(f32[10,32,256]{2,1,0:T(8,128)} %bitcast_dynamic-update-slice_fusion), channel_id=1, source_target_pairs={{0,1},{1,2},{2,3},{3,4},{4,5},{5,6},{6,7},{7,8},{8,9},{9,10},{10,1... | collective-permute-start | bytes 983048 | tf_op jit(solution)/shard_map/ppermute | solution.py:24
  30.9 1.8 %copy-start.5 = (f32[3,8,32,256]{3,2,1,0:T(8,128)S(1)}, f32[3,8,32,256]{3,2,1,0:T(8,128)}, u32[]{:S(2)}) copy-start(f32[3,8,32,256]{3,2,1,0:T(8,128)} %pf.1) | copy-start | bytes 2359300
  32.6 0.7 %copy-start.7 = (s32[16]{0:T(128)S(1)}, s32[16]{0:T(128)}, u32[]{:S(2)}) copy-start(s32[16]{0:T(128)} %src.1) | copy-start | bytes 196
  32.6 0.7 %copy-start.8 = (s32[16]{0:T(128)S(1)}, s32[16]{0:T(128)}, u32[]{:S(2)}) copy-start(s32[16]{0:T(128)} %mon.1) | copy-start | bytes 196
  33.2 1.1 %copy-start.6 = (f32[3,8,32,256]{3,2,1,0:T(8,128)S(1)}, f32[3,8,32,256]{3,2,1,0:T(8,128)}, u32[]{:S(2)}) copy-start(f32[3,8,32,256]{3,2,1,0:T(8,128)} %jf.1) | copy-start | bytes 2359300

commit v3 on v2

--- a/solution.py
+++ b/solution.py
@@ -42,11 +42,17 @@
 
 
 def field_kernel(
-    ef, hf, pf, jf, ea, ha, pa, ja, rho, upper, below, src, mon, amp,
-    ef_o, hf_o, ea_o, ha_o, inter_o,
+    ef, hf, pf, jf, ea, ha, pa, ja, arrived, upper, below, src, mon, amp, first,
+    ef_o, hf_o, ea_o, ha_o, ret_o, rho,
 ):
     depth, width_x, width_y = rho.shape
+    slab = arrived.shape[0]
     index = lax.axis_index("gx")
+    start = first[0]
+    for z in range(depth):
+        p = index * depth + z - start
+        inside = (p >= 0) & (p < slab)
+        rho[z] = jnp.where(inside, arrived[jnp.clip(p, 0, slab - 1)], 0.0)
     row = lax.broadcasted_iota(jnp.int32, (width_x, width_y), 0)
     lane = lax.broadcasted_iota(jnp.int32, (width_x, width_y), 1)
 
@@ -134,17 +140,23 @@
     for m in range(mon.shape[0]):
         add_at(mon[m], ea_o, lambda c, local, rows: ef[c, local, rows, :])
 
+    for g in range(slab):
+        ret_o[g] = jnp.zeros((width_x, width_y), jnp.float32)
     for z in range(depth):
         total = None
         for c in range(3):
             fwd = ef_o[c, z]
             term = ea_o[c, z] * (fwd - ef[c, z] + GAIN_FIELD * fwd)
             total = term if total is None else total + term
-        inter_o[z] = total
+        p = index * depth + z - start
+
+        @pl.when((p >= 0) & (p < slab))
+        def _():
+            ret_o[jnp.clip(p, 0, slab - 1)] = total
 
 
 def fields(e_forward, h_forward, p_forward, j_forward, e_adjoint, h_adjoint, p_adjoint, j_adjoint,
-           density, upper, below, source_cell, monitor_cell, source_amp):
+           arrived, upper, below, source_cell, monitor_cell, source_amp, slab_start):
     shape = e_forward.shape
     depth = shape[1]
     field = jax.ShapeDtypeStruct(shape, jnp.float32)
@@ -153,15 +165,16 @@
     cells = shape[1] * shape[2] * shape[3]
     return pl.pallas_call(
         field_kernel,
-        out_shape=(field, field, field, field, jax.ShapeDtypeStruct(shape[1:], jnp.float32)),
-        in_specs=[vmem] * 11 + [smem] * 3,
+        out_shape=(field, field, field, field, jax.ShapeDtypeStruct(arrived.shape, jnp.float32)),
+        in_specs=[vmem] * 11 + [smem] * 4,
         out_specs=(vmem,) * 5,
+        scratch_shapes=[pltpu.VMEM(shape[1:], jnp.float32)],
         compiler_params=pltpu.CompilerParams(vmem_limit_bytes=48 * 1024 * 1024),
         cost_estimate=pl.CostEstimate(
             flops=200 * cells, bytes_accessed=4 * cells * 40, transcendentals=0
         ),
     )(e_forward, h_forward, p_forward, j_forward, e_adjoint, h_adjoint, p_adjoint, j_adjoint,
-      density, upper, below, source_cell, monitor_cell, source_amp)
+      arrived, upper, below, source_cell, monitor_cell, source_amp, slab_start)
 
 
 def body(
@@ -186,15 +199,10 @@
     start = slab_start[0]
     wx = band_matrix(width_x, radius[0])
     wy = band_matrix(width_y, radius[0])
-    planes = index * depth + jnp.arange(depth, dtype=jnp.int32) - start
-    select = (planes[:, None] == jnp.arange(count, dtype=jnp.int32)[None, :]).astype(jnp.float32)
-    upper = passed_along(
-        jnp.stack([e_forward[0, 0], e_forward[1, 0], e_adjoint[0, 0], e_adjoint[1, 0]]), "gx", -1
-    )
+    upper = passed_along(jnp.concatenate([e_forward[0:2, 0], e_adjoint[0:2, 0]], 0), "gx", -1)
     below = passed_along(
-        jnp.stack(
-            [h_forward[0, -1], h_forward[1, -1], e_forward[0, -1], e_forward[1, -1], e_forward[2, -1],
-             h_adjoint[0, -1], h_adjoint[1, -1], e_adjoint[0, -1], e_adjoint[1, -1], e_adjoint[2, -1]]
+        jnp.concatenate(
+            [h_forward[0:2, -1], e_forward[:, -1], h_adjoint[0:2, -1], e_adjoint[:, -1]], 0
         ),
         "gx",
         1,
@@ -204,15 +212,13 @@
     target = (jnp.arange(count, dtype=jnp.int32) == holder).astype(jnp.float32)
     slots = target[:, None, None] * owned
     arrived = lax.all_to_all(slots, "gx", split_axis=0, concat_axis=0, tiled=True)
-    density = jnp.einsum("lo,oxy->lxy", select, arrived, precision=HIGH)
-    ef, hf, ea, ha, intersection = fields(
+    ef, hf, ea, ha, returned = fields(
         e_forward, h_forward, p_forward, j_forward, e_adjoint, h_adjoint, p_adjoint, j_adjoint,
-        density, upper, below, source_cell, monitor_cell, source_amp,
+        arrived, upper, below, source_cell, monitor_cell, source_amp, slab_start,
     )
-    returned = jnp.einsum("lo,lxy->oxy", select, intersection, precision=HIGH)
     arrived_back = lax.all_to_all(returned, "gx", split_axis=0, concat_axis=0, tiled=True)
-    own_intersection = jnp.sum(arrived_back, axis=0, keepdims=True)
-    design_grad = smooth_adjoint(wx, wy, own_intersection)
+    inner = jnp.einsum("ax,jab->xb", wx, arrived_back, precision=HIGH)
+    design_grad = jnp.einsum("xb,by->xy", inner, wy, precision=HIGH)[None]
     return (ef, hf, ea, ha, design_grad)
 
 

time: 61.7 us -> 57.3 us (0.929)
  local copies, waits for them, and re-layouts: 9.92 us -> 3.28 us
  waiting for transfers between devices: 5.96 us -> 9.01 us
  blocking collectives: 19.1 us -> 21.4 us
  matrix products: 4.1 us -> 1.88 us
  starting transfers between devices: 12.5 us -> 11.1 us
    unnamed x30 -> x19, local copies, waits for them, and re-layouts: 7.34 us -> 2.4 us
    ppermute x2, waiting for transfers between devices: 0.01 us -> 2.97 us  [passed_along(): return lax.ppermute(block, axis, route)]
    all_to_all x1, blocking collectives: 19.1 us -> 21.4 us  [body(): lax.all_to_all(returned, 'gx', split_axis=0, concat_axis=0, tiled=True)]
    dot_general x4 -> x2, matrix products: 3.45 us -> 1.23 us  [the longest x1 0.93 us: body(): design_grad = jnp.einsum('xb,by->xy', inner, wy, precision=HIGH)[None]]
    another operation x3 -> x0, local copies, waits for them, and re-layouts: 2.18 us -> none  [the longest x2 1.57 us: body(): jnp.stack([e_forward[0, 0], e_forward[1, 0], e_adjoint[0, 0], e_adjoint[1...]
    all_to_all x1, starting transfers between devices: 8.95 us -> 7.52 us  [body(): lax.all_to_all(slots, 'gx', split_axis=0, concat_axis=0, tiled=True)]
    squeeze x0 -> x3, local copies, waits for them, and re-layouts: none -> 0.88 us  [the longest x1 0.86 us: body(): h_adjoint[0:2, -1]]
    concatenate x0 -> x2, other arithmetic: none -> 0.76 us  [the longest x1 0.75 us: body(): jnp.concatenate([h_forward[0:2, -1], e_forward[:, -1], h_adjoint[0:2, -1]...]
  transfers between devices with their start and end apart: 3 -> 3, of which waited for: 1 -> 2; matrix products, arithmetic and copies ran while one was open for 16% -> 3% of each run, Pallas kernels for 0% -> 0%
where the time goes in v3:
time: 57.3 us; the launch traced here: 56.7 us
  blocking collectives  21.4 us (37%)
  starting transfers between devices  11.1 us (19%)
  waiting for transfers between devices  9.01 us (16%)
  Pallas kernels  5.97 us (10%)
  local copies, waits for them, and re-layouts  3.28 us (6%)
  between operations  2.14 us (4%)
  other arithmetic  1.96 us (3%)
  matrix products  1.88 us (3%)
    all_to_all x1, blocking collectives, body(): lax.all_to_all(returned, 'gx', split_axis=0, concat_axis=0, tiled=True)  21.4 us
    all_to_all x1, starting transfers between devices, body(): lax.all_to_all(slots, 'gx', split_axis=0, concat_axis=0, tiled=True)  7.52 us
    all_to_all x1, waiting for transfers between devices, body(): lax.all_to_all(slots, 'gx', split_axis=0, concat_axis=0, tiled=True)  6.04 us
    pallas_call x1, Pallas kernels, fields(): pl.pallas_call(field_kernel, out_shape=(field, field, field, field, jax.S...  5.97 us
    ppermute x2, starting transfers between devices, passed_along(): return lax.ppermute(block, axis, route)  3.61 us
    ppermute x2, waiting for transfers between devices, passed_along(): return lax.ppermute(block, axis, route)  2.97 us
    unnamed x19, local copies, waits for them, and re-layouts  2.4 us
  transfers between devices with their start and end apart: 3, of which 2 were waited for; matrix products, arithmetic and copies ran while one was open for 3% of the time, Pallas kernels for 0%

profile of v3, /device:TPU:0, one launch (start us, length us, event | category | flops | bytes accessed | tf_op | source)
XLA Modules:
  0.0 56.7 jit_solution(3640974716722854410)
XLA Ops:
  0.6 0.0 copy-start
  2.0 0.1 convert_reduce_fusion.1
  2.1 0.2 convert_reduce_fusion
  2.3 0.2 fusion.7
  2.5 0.0 copy-start.3
  2.5 0.4 fusion
  2.9 0.0 copy-start.2
  3.0 0.9 %broadcast_multiply_fusion = f32[16,32,256]{2,1,0:T(8,128)} fusion(f32[32,256]{1,0:T(8,128)S(1)} %fusion, f32[16]{0:T(128)S(1)} %compare_convert_fusion), kind=kLoop, calls=%fused_computation.2 | loop fusion | flops 131072 | bytes 557120 | tf_op jit(solution)/shard_map/mul | solution.py:213
  3.9 7.5 %all-to-all-start = ((f32[16,32,256]{2,1,0:T(8,128)}), f32[16,32,256]{2,1,0:T(8,128)S(1)}, u32[]{:S(2)}, u32[]{:S(2)}) async-start(f32[16,32,256]{2,1,0:T(8,128)} %broadcast_multiply_fusion), calls=%async_computation | async-start | bytes 1048576 | tf_op jit(solution)/shard_map/all_to_all | solution.py:214
  11.4 0.9 %slice_bitcast_fusion.2 = (f32[2,32,256]{2,1,0:T(8,128)S(1)}, f32[2,32,256]{2,1,0:T(8,128)S(1)}) fusion(f32[3,8,32,256]{3,2,1,0:T(8,128)} %ha.1, f32[3,8,32,256]{3,2,1,0:T(8,128)S(1)} %copy-done.3), kind=kLoop, calls=%fused_computation.16 | loop fusion | bytes 262144 | tf_op jit(solution)/shard_map/squeeze | solution.py:205
  12.3 0.7 %pad_maximum_fusion = f32[10,32,256]{2,1,0:T(8,128)} fusion(f32[3,32,256]{2,1,0:T(8,128)S(1)} %get-tuple-element.17, f32[2,32,256]{2,1,0:T(8,128)S(1)} %get-tuple-element.19, f32[3,32,256]{2,1,0:T(8,128)S(1)} %get-tuple-element.18, f32[2,32,256]{2,1,0:T(8,128)S(1)} %get-tuple-element.20), kind=kLoop, calls=%fused_computation.1 | loop fusion | flops 245760 | bytes 655360 | tf_op jit(solution)/shard_map/concatenate | solution.py:204
  13.0 2.3 %collective-permute-start.1 = (f32[10,32,256]{2,1,0:T(8,128)}, f32[10,32,256]{2,1,0:T(8,128)S(1)}, u32[]{:S(2)}, u32[]{:S(2)}) collective-permute-start(f32[10,32,256]{2,1,0:T(8,128)} %pad_maximum_fusion), channel_id=1, source_target_pairs={{0,1},{1,2},{2,3},{3,4},{4,5},{5,6},{6,7},{7,8},{8,9},{9,10},{10,1... | collective-permute-start | bytes 983048 | tf_op jit(solution)/shard_map/ppermute | solution.py:24
  15.4 0.0 copy-start.8
  15.4 0.0 copy-start.6
  15.4 1.3 %collective-permute-start = (f32[4,32,256]{2,1,0:T(8,128)S(1)}, f32[4,32,256]{2,1,0:T(8,128)S(1)}, u32[]{:S(2)}, u32[]{:S(2)}) collective-permute-start(f32[4,32,256]{2,1,0:T(8,128)S(1)} %pad_maximum_fusion.1), channel_id=1, source_target_pairs={{1,0},{2,1},{3,2},{4,3},{5,4},{6,5},{7,6},{8,7},{9,8},{10,9},{11,1... | collective-permute-start | bytes 393224 | tf_op jit(solution)/shard_map/ppermute | solution.py:24
  16.8 0.1 copy.32.amp
  16.8 3.0 %collective-permute-done.upper = f32[4,32,256]{2,1,0:T(8,128)S(1)} collective-permute-done((f32[4,32,256]{2,1,0:T(8,128)S(1)}, f32[4,32,256]{2,1,0:T(8,128)S(1)}, u32[]{:S(2)}, u32[]{:S(2)}) %collective-permute-start) | collective-permute-done | bytes 131104 | tf_op jit(solution)/shard_map/ppermute | solution.py:24
  19.8 6.0 %all-to-all-done.arrived = f32[16,32,256]{2,1,0:T(8,128)S(1)} async-done(((f32[16,32,256]{2,1,0:T(8,128)}), f32[16,32,256]{2,1,0:T(8,128)S(1)}, u32[]{:S(2)}, u32[]{:S(2)}) %all-to-all-start) | async-done | bytes 524320 | tf_op jit(solution)/shard_map/all_to_all | solution.py:214
  25.9 1.1 %copy-done.4 = f32[3,8,32,256]{3,2,1,0:T(8,128)S(1)} copy-done((f32[3,8,32,256]{3,2,1,0:T(8,128)S(1)}, f32[3,8,32,256]{3,2,1,0:T(8,128)}, u32[]{:S(2)}) %copy-start.4) | copy-done | bytes 786456
  27.0 1.1 %copy-done.5 = f32[3,8,32,256]{3,2,1,0:T(8,128)S(1)} copy-done((f32[3,8,32,256]{3,2,1,0:T(8,128)S(1)}, f32[3,8,32,256]{3,2,1,0:T(8,128)}, u32[]{:S(2)}) %copy-start.5) | copy-done | bytes 786456
  28.1 6.0 %shard_map.173 = (f32[3,8,32,256]{3,2,1,0:T(8,128)}, f32[3,8,32,256]{3,2,1,0:T(8,128)}, f32[3,8,32,256]{3,2,1,0:T(8,128)}, f32[3,8,32,256]{3,2,1,0:T(8,128)}, f32[16,32,256]{2,1,0:T(8,128)S(1)}) custom-call(f32[3,8,32,256]{3,2,1,0:T(8,128)S(1)} %copy-done.1, f32[3,8,32,256]{3,2,1,0:T(8,128)S(1)} %copy-done.3, f32[3,8,32,256]{3,2,1,0:T(8,128)S(1)} %copy-done.4, ...), custom_call_target="tpu_custom_call" | custom-call | flops 13107200 | bytes 10485760 | tf_op jit(solution)/shard_map/pallas_call | solution.py:166
  34.1 21.4 %all_to_all.10 = f32[16,32,256]{2,1,0:T(8,128)S(1)} all-to-all(f32[16,32,256]{2,1,0:T(8,128)S(1)} %get-tuple-element.14), channel_id=1, replica_groups=mesh['grp'=2,'gx'=16] {'gx'}, dimensions={0} | all-to-all | bytes 1048576 | tf_op jit(solution)/shard_map/all_to_all | solution.py:219
  55.5 0.3 fusion.9
  55.8 0.9 %convolution_bitcast_fusion = f32[1,32,256]{2,1,0:T(8,128)} fusion(f32[32,256]{1,0:T(8,128)S(1)} %fusion.9, f32[256]{0:T(256)S(1)} %convert_reduce_fusion, s32[]{:T(128)} %bitcast.1), kind=kOutput, calls=%fused_computation | convolution fusion | flops 25559040 | bytes 66564 | tf_op jit(solution)/shard_map/xb,by->xy/dot_general | solution.py:221
  (17 shorter events, 0.1 us)
Async XLA Ops:
  0.6 1.6 %copy-start = (f32[1,32,256]{2,1,0:T(8,128)S(1)}, f32[1,32,256]{2,1,0:T(8,128)}, u32[]{:S(2)}) copy-start(f32[1,32,256]{2,1,0:T(8,128)} %param.22) | copy-start | bytes 98308
  2.5 8.9 %copy-start.3 = (f32[3,8,32,256]{3,2,1,0:T(8,128)S(1)}, f32[3,8,32,256]{3,2,1,0:T(8,128)}, u32[]{:S(2)}) copy-start(f32[3,8,32,256]{3,2,1,0:T(8,128)} %hf.1) | copy-start | bytes 2359300
  2.9 9.3 %copy-start.2 = (f32[3,8,32,256]{3,2,1,0:T(8,128)S(1)}, f32[3,8,32,256]{3,2,1,0:T(8,128)}, u32[]{:S(2)}) copy-start(f32[3,8,32,256]{3,2,1,0:T(8,128)} %ea.1) | copy-start | bytes 2359300
  3.9 8.4 %copy-start.1 = (f32[3,8,32,256]{3,2,1,0:T(8,128)S(1)}, f32[3,8,32,256]{3,2,1,0:T(8,128)}, u32[]{:S(2)}) copy-start(f32[3,8,32,256]{3,2,1,0:T(8,128)} %ef.1) | copy-start | bytes 2359300
  3.9 22.0 %all-to-all-start = ((f32[16,32,256]{2,1,0:T(8,128)}), f32[16,32,256]{2,1,0:T(8,128)S(1)}, u32[]{:S(2)}, u32[]{:S(2)}) async-start(f32[16,32,256]{2,1,0:T(8,128)} %broadcast_multiply_fusion), calls=%async_computation | async-start | bytes 1048576 | tf_op jit(solution)/shard_map/all_to_all | solution.py:214
  13.0 6.8 %collective-permute-start.1 = (f32[10,32,256]{2,1,0:T(8,128)}, f32[10,32,256]{2,1,0:T(8,128)S(1)}, u32[]{:S(2)}, u32[]{:S(2)}) collective-permute-start(f32[10,32,256]{2,1,0:T(8,128)} %pad_maximum_fusion), channel_id=1, source_target_pairs={{0,1},{1,2},{2,3},{3,4},{4,5},{5,6},{6,7},{7,8},{8,9},{9,10},{10,1... | collective-permute-start | bytes 983048 | tf_op jit(solution)/shard_map/ppermute | solution.py:24
  15.4 1.4 %copy-start.8 = (f32[16,3]{0,1:T(4,128)S(1)}, f32[16,3]{0,1:T(4,128)}, u32[]{:S(2)}) copy-start(f32[16,3]{0,1:T(4,128)} %param.23) | copy-start | bytes 580
  15.4 10.4 %copy-start.6 = (s32[16]{0:T(128)S(1)}, s32[16]{0:T(128)}, u32[]{:S(2)}) copy-start(s32[16]{0:T(128)} %src.1) | copy-start | bytes 196
  15.4 10.4 %copy-start.7 = (s32[16]{0:T(128)S(1)}, s32[16]{0:T(128)}, u32[]{:S(2)}) copy-start(s32[16]{0:T(128)} %mon.1) | copy-start | bytes 196
  15.4 4.4 %collective-permute-start = (f32[4,32,256]{2,1,0:T(8,128)S(1)}, f32[4,32,256]{2,1,0:T(8,128)S(1)}, u32[]{:S(2)}, u32[]{:S(2)}) collective-permute-start(f32[4,32,256]{2,1,0:T(8,128)S(1)} %pad_maximum_fusion.1), channel_id=1, source_target_pairs={{1,0},{2,1},{3,2},{4,3},{5,4},{6,5},{7,6},{8,7},{9,8},{10,9},{11,1... | collective-permute-start | bytes 393224 | tf_op jit(solution)/shard_map/ppermute | solution.py:24
  25.9 1.1 %copy-start.4 = (f32[3,8,32,256]{3,2,1,0:T(8,128)S(1)}, f32[3,8,32,256]{3,2,1,0:T(8,128)}, u32[]{:S(2)}) copy-start(f32[3,8,32,256]{3,2,1,0:T(8,128)} %pf.1) | copy-start | bytes 2359300
  27.0 1.1 %copy-start.5 = (f32[3,8,32,256]{3,2,1,0:T(8,128)S(1)}, f32[3,8,32,256]{3,2,1,0:T(8,128)}, u32[]{:S(2)}) copy-start(f32[3,8,32,256]{3,2,1,0:T(8,128)} %jf.1) | copy-start | bytes 2359300

commit v4 on v3

--- a/solution.py
+++ b/solution.py
@@ -42,17 +42,15 @@
 
 
 def field_kernel(
-    ef, hf, pf, jf, ea, ha, pa, ja, arrived, upper, below, src, mon, amp, first,
-    ef_o, hf_o, ea_o, ha_o, ret_o, rho,
+    ef, hf, pf, jf, ea, ha, pa, ja, ef_up, ea_up, arrived, upper, below, src, mon, amp, first,
+    ef_o, hf_o, ea_o, ha_o, ret_o, prev, rho,
 ):
-    depth, width_x, width_y = rho.shape
+    _, _, width_x, width_y = ef.shape
+    depth = pl.num_programs(0)
+    z = pl.program_id(0)
     slab = arrived.shape[0]
     index = lax.axis_index("gx")
     start = first[0]
-    for z in range(depth):
-        p = index * depth + z - start
-        inside = (p >= 0) & (p < slab)
-        rho[z] = jnp.where(inside, arrived[jnp.clip(p, 0, slab - 1)], 0.0)
     row = lax.broadcasted_iota(jnp.int32, (width_x, width_y), 0)
     lane = lax.broadcasted_iota(jnp.int32, (width_x, width_y), 1)
 
@@ -68,51 +66,49 @@
     def behind_x(f):
         return jnp.where(row == 0, 0.0, pltpu.roll(f, 1, 0))
 
-    def new_h(e, h, z, ex_up, ey_up):
-        ex, ey, ez = e[0, z], e[1, z], e[2, z]
-        curl_x = ahead_y(ez) - ez - (ey_up - ey)
-        curl_y = ex_up - ex - (ahead_x(ez) - ez)
-        curl_z = ahead_x(ey) - ey - (ahead_y(ex) - ex)
-        return (h[0, z] - DT * curl_x, h[1, z] - DT * curl_y, h[2, z] - DT * curl_z)
-
-    def lower_h(e, base):
-        hx, hy, ex, ey, ez = (below[base + i] for i in range(5))
-        curl_x = ahead_y(ez) - ez - (e[1, 0] - ey)
-        curl_y = e[0, 0] - ex - (ahead_x(ez) - ez)
+    p_here = index * depth + z - start
+    inside = (p_here >= 0) & (p_here < slab)
+    density = jnp.where(inside, arrived[jnp.clip(p_here, 0, slab - 1)], 0.0)
+    rho[...] = density
+    step = DT / (1.0 + EPS_RANGE * density)
+    strength = STRENGTH_BASE + STRENGTH_RANGE * density
+    last = z == depth - 1
+
+    @pl.when(z == 0)
+    def _():
         keep = index > 0
-        return (
-            jnp.where(keep, hx - DT * curl_x, 0.0),
-            jnp.where(keep, hy - DT * curl_y, 0.0),
-        )
-
-    def new_e(e, p, j, out, z, hn, hn_dn, step, strength):
-        hx, hy, hz = hn
-        hx_dn, hy_dn = hn_dn
+        for r, e in enumerate((ef, ea)):
+            hx, hy, ex, ey, ez = (below[5 * r + i] for i in range(5))
+            curl_x = ahead_y(ez) - ez - (e[1, 0] - ey)
+            curl_y = e[0, 0] - ex - (ahead_x(ez) - ez)
+            prev[2 * r] = jnp.where(keep, hx - DT * curl_x, 0.0)
+            prev[2 * r + 1] = jnp.where(keep, hy - DT * curl_y, 0.0)
+        for g in range(slab):
+            ret_o[g] = jnp.zeros((width_x, width_y), jnp.float32)
+
+    runs = ((ef, hf, pf, jf, ef_up, hf_o, ef_o), (ea, ha, pa, ja, ea_up, ha_o, ea_o))
+    for r, (e, h, p, j, e_up, h_out, e_out) in enumerate(runs):
+        ex, ey, ez = e[0, 0], e[1, 0], e[2, 0]
+        ex_up = jnp.where(last, upper[2 * r], e_up[0, 0])
+        ey_up = jnp.where(last, upper[2 * r + 1], e_up[1, 0])
+        hx = h[0, 0] - DT * (ahead_y(ez) - ez - (ey_up - ey))
+        hy = h[1, 0] - DT * (ex_up - ex - (ahead_x(ez) - ez))
+        hz = h[2, 0] - DT * (ahead_x(ey) - ey - (ahead_y(ex) - ex))
+        h_out[0, 0] = hx
+        h_out[1, 0] = hy
+        h_out[2, 0] = hz
+        hx_dn = prev[2 * r]
+        hy_dn = prev[2 * r + 1]
         curl = (
             hz - behind_y(hz) - (hy - hy_dn),
             hx - hx_dn - (hz - behind_x(hz)),
             hy - behind_x(hy) - (hx - behind_y(hx)),
         )
         for c in range(3):
-            j_next = (KEEP * j[c, z] + DT * (strength * e[c, z] - p[c, z])) / LOSS
-            out[c, z] = e[c, z] + step * (curl[c] - j_next)
-
-    runs = ((ef, hf, pf, jf, hf_o, ef_o, 0), (ea, ha, pa, ja, ha_o, ea_o, 2))
-    prev = [lower_h(ef, 0), lower_h(ea, 5)]
-    for z in range(depth):
-        density = rho[z]
-        step = DT / (1.0 + EPS_RANGE * density)
-        strength = STRENGTH_BASE + STRENGTH_RANGE * density
-        for r, (e, h, p, j, h_out, e_out, up) in enumerate(runs):
-            if z + 1 < depth:
-                ex_up, ey_up = e[0, z + 1], e[1, z + 1]
-            else:
-                ex_up, ey_up = upper[up], upper[up + 1]
-            hn = new_h(e, h, z, ex_up, ey_up)
-            for c in range(3):
-                h_out[c, z] = hn[c]
-            new_e(e, p, j, e_out, z, hn, prev[r], step, strength)
-            prev[r] = (hn[0], hn[1])
+            j_next = (KEEP * j[c, 0] + DT * (strength * e[c, 0] - p[c, 0])) / LOSS
+            e_out[c, 0] = e[c, 0] + step * (curl[c] - j_next)
+        prev[2 * r] = hx
+        prev[2 * r + 1] = hy
 
     plane = width_x * width_y
     tile_row = lax.broadcasted_iota(jnp.int32, (8, width_y), 0)
@@ -120,61 +116,62 @@
 
     def add_at(cell, out, value_of):
         zz = cell // plane
-        local = zz - index * depth
         rest = cell - zz * plane
         x = rest // width_y
         y = rest - x * width_y
         x0 = pl.multiple_of((x // 8) * 8, 8)
 
-        @pl.when((local >= 0) & (local < depth))
+        @pl.when(zz - index * depth == z)
         def _():
             rows = pl.ds(x0, 8)
             hit = (tile_row == x - x0) & (tile_lane == y)
-            step = DT / (1.0 + EPS_RANGE * rho[local, rows, :])
+            gain = DT / (1.0 + EPS_RANGE * rho[rows, :])
             for c in range(3):
-                held = out[c, local, rows, :]
-                out[c, local, rows, :] = held + jnp.where(hit, step * value_of(c, local, rows), 0.0)
-
-    for s in range(src.shape[0]):
-        add_at(src[s], ef_o, lambda c, local, rows, s=s: amp[s, c])
+                held = out[c, 0, rows, :]
+                out[c, 0, rows, :] = held + jnp.where(hit, gain * value_of(c, rows), 0.0)
+
+    for s_ in range(src.shape[0]):
+        add_at(src[s_], ef_o, lambda c, rows, s_=s_: amp[s_, c])
     for m in range(mon.shape[0]):
-        add_at(mon[m], ea_o, lambda c, local, rows: ef[c, local, rows, :])
-
-    for g in range(slab):
-        ret_o[g] = jnp.zeros((width_x, width_y), jnp.float32)
-    for z in range(depth):
-        total = None
-        for c in range(3):
-            fwd = ef_o[c, z]
-            term = ea_o[c, z] * (fwd - ef[c, z] + GAIN_FIELD * fwd)
-            total = term if total is None else total + term
-        p = index * depth + z - start
-
-        @pl.when((p >= 0) & (p < slab))
-        def _():
-            ret_o[jnp.clip(p, 0, slab - 1)] = total
+        add_at(mon[m], ea_o, lambda c, rows: ef[c, 0, rows, :])
+
+    total = None
+    for c in range(3):
+        fwd = ef_o[c, 0]
+        term = ea_o[c, 0] * (fwd - ef[c, 0] + GAIN_FIELD * fwd)
+        total = term if total is None else total + term
+
+    @pl.when(inside)
+    def _():
+        ret_o[jnp.clip(p_here, 0, slab - 1)] = total
 
 
 def fields(e_forward, h_forward, p_forward, j_forward, e_adjoint, h_adjoint, p_adjoint, j_adjoint,
            arrived, upper, below, source_cell, monitor_cell, source_amp, slab_start):
     shape = e_forward.shape
-    depth = shape[1]
+    depth, width_x, width_y = shape[1], shape[2], shape[3]
     field = jax.ShapeDtypeStruct(shape, jnp.float32)
-    vmem = pl.BlockSpec(memory_space=pltpu.VMEM)
+    block = pl.BlockSpec((3, 1, width_x, width_y), lambda z: (0, z, 0, 0))
+    ahead = pl.BlockSpec((2, 1, width_x, width_y), lambda z: (0, jnp.minimum(z + 1, depth - 1), 0, 0))
+    whole = lambda a: pl.BlockSpec(a.shape, lambda z: (0,) * a.ndim)
     smem = pl.BlockSpec(memory_space=pltpu.SMEM)
-    cells = shape[1] * shape[2] * shape[3]
+    cells = depth * width_x * width_y
     return pl.pallas_call(
         field_kernel,
+        grid=(depth,),
         out_shape=(field, field, field, field, jax.ShapeDtypeStruct(arrived.shape, jnp.float32)),
-        in_specs=[vmem] * 11 + [smem] * 4,
-        out_specs=(vmem,) * 5,
-        scratch_shapes=[pltpu.VMEM(shape[1:], jnp.float32)],
-        compiler_params=pltpu.CompilerParams(vmem_limit_bytes=48 * 1024 * 1024),
+        in_specs=[block] * 8 + [ahead] * 2 + [whole(arrived), whole(upper), whole(below)] + [smem] * 4,
+        out_specs=(block,) * 4 + (whole(arrived),),
+        scratch_shapes=[
+            pltpu.VMEM((4, width_x, width_y), jnp.float32),
+            pltpu.VMEM((width_x, width_y), jnp.float32),
+        ],
+        compiler_params=pltpu.CompilerParams(dimension_semantics=("arbitrary",)),
         cost_estimate=pl.CostEstimate(
             flops=200 * cells, bytes_accessed=4 * cells * 40, transcendentals=0
         ),
     )(e_forward, h_forward, p_forward, j_forward, e_adjoint, h_adjoint, p_adjoint, j_adjoint,
-      arrived, upper, below, source_cell, monitor_cell, source_amp, slab_start)
+      e_forward, e_adjoint, arrived, upper, below, source_cell, monitor_cell, source_amp, slab_start)
 
 
 def body(

time: 57.3 us -> 63.1 us (1.10)
  Pallas kernels: 5.97 us -> 12.1 us
  waiting for transfers between devices: 9.01 us -> 7.36 us
  local copies, waits for them, and re-layouts: 3.28 us -> 4.24 us
  blocking collectives: 21.4 us -> 22.3 us
  other arithmetic: 1.96 us -> 1.24 us
    pallas_call x1, Pallas kernels: 5.97 us -> 12.1 us  [fields(): pl.pallas_call(field_kernel, grid=(depth,), out_shape=(field, field, fiel...]
    all_to_all x1, waiting for transfers between devices: 6.04 us -> 4.99 us  [body(): lax.all_to_all(slots, 'gx', split_axis=0, concat_axis=0, tiled=True)]
    squeeze x1, local copies, waits for them, and re-layouts: 0.02 us -> 0.96 us  [body(): e_adjoint[:, -1]]
    all_to_all x1, blocking collectives: 21.4 us -> 22.3 us  [body(): lax.all_to_all(returned, 'gx', split_axis=0, concat_axis=0, tiled=True)]
    unnamed x19 -> x11, local copies, waits for them, and re-layouts: 2.4 us -> 1.5 us
    squeeze x1, local copies, waits for them, and re-layouts: 0.01 us -> 0.89 us  [body(): e_adjoint[0:2, 0]]
    concatenate x1, other arithmetic: 0.75 us -> 0.02 us  [body(): jnp.concatenate([h_forward[0:2, -1], e_forward[:, -1], h_adjoint[0:2, -1]...]
  transfers between devices with their start and end apart: 3 -> 3, of which waited for: 2 -> 2; matrix products, arithmetic and copies ran while one was open for 3% -> 6% of each run, Pallas kernels for 0% -> 0%
where the time goes in v4:
time: 63.1 us; the launch traced here: 62.2 us
  blocking collectives  22.3 us (35%)
  Pallas kernels  12.1 us (19%)
  starting transfers between devices  11 us (17%)
  waiting for transfers between devices  7.36 us (12%)
  local copies, waits for them, and re-layouts  4.24 us (7%)
  between operations  2.09 us (3%)
  matrix products  1.88 us (3%)
  other arithmetic  1.24 us (2%)
    all_to_all x1, blocking collectives, body(): lax.all_to_all(returned, 'gx', split_axis=0, concat_axis=0, tiled=True)  22.3 us
    pallas_call x1, Pallas kernels, fields(): pl.pallas_call(field_kernel, grid=(depth,), out_shape=(field, field, fiel...  12.1 us
    all_to_all x1, starting transfers between devices, body(): lax.all_to_all(slots, 'gx', split_axis=0, concat_axis=0, tiled=True)  7.38 us
    all_to_all x1, waiting for transfers between devices, body(): lax.all_to_all(slots, 'gx', split_axis=0, concat_axis=0, tiled=True)  4.99 us
    ppermute x2, starting transfers between devices, passed_along(): return lax.ppermute(block, axis, route)  3.62 us
    ppermute x2, waiting for transfers between devices, passed_along(): return lax.ppermute(block, axis, route)  2.37 us
    unnamed x11, local copies, waits for them, and re-layouts  1.5 us
  transfers between devices with their start and end apart: 3, of which 2 were waited for; matrix products, arithmetic and copies ran while one was open for 6% of the time, Pallas kernels for 0%

profile of v4, /device:TPU:0, one launch (start us, length us, event | category | flops | bytes accessed | tf_op | source)
XLA Modules:
  0.0 62.2 jit_solution(10637315869772226050)
XLA Ops:
  0.6 0.0 copy-start
  2.0 0.1 convert_reduce_fusion.1
  2.1 0.2 convert_reduce_fusion
  2.3 0.0 copy-done
  2.3 0.2 fusion.7
  2.5 0.4 fusion
  2.9 0.9 %broadcast_multiply_fusion = f32[16,32,256]{2,1,0:T(8,128)} fusion(f32[32,256]{1,0:T(8,128)S(1)} %fusion, f32[16]{0:T(128)S(1)} %compare_convert_fusion), kind=kLoop, calls=%fused_computation.2 | loop fusion | flops 131072 | bytes 557120 | tf_op jit(solution)/shard_map/mul | solution.py:210
  3.8 7.4 %all-to-all-start = ((f32[16,32,256]{2,1,0:T(8,128)}), f32[16,32,256]{2,1,0:T(8,128)S(1)}, u32[]{:S(2)}, u32[]{:S(2)}) async-start(f32[16,32,256]{2,1,0:T(8,128)} %broadcast_multiply_fusion), calls=%async_computation | async-start | bytes 1048576 | tf_op jit(solution)/shard_map/all_to_all | solution.py:211
  11.2 0.9 %slice_bitcast_fusion.2 = (f32[2,32,256]{2,1,0:T(8,128)S(1)}, f32[2,32,256]{2,1,0:T(8,128)S(1)}) fusion(f32[3,8,32,256]{3,2,1,0:T(8,128)} %ha.1, f32[3,8,32,256]{3,2,1,0:T(8,128)} %hf.1), kind=kLoop, calls=%fused_computation.16 | loop fusion | bytes 262144 | tf_op jit(solution)/shard_map/squeeze | solution.py:202
  12.1 1.0 %slice_bitcast_fusion = (f32[3,32,256]{2,1,0:T(8,128)S(1)}, f32[3,32,256]{2,1,0:T(8,128)S(1)}) fusion(f32[3,8,32,256]{3,2,1,0:T(8,128)} %ea_up.1, f32[3,8,32,256]{3,2,1,0:T(8,128)} %ef_up.1), kind=kLoop, calls=%fused_computation.14 | loop fusion | bytes 393216 | tf_op jit(solution)/shard_map/squeeze | solution.py:202
  13.1 2.3 %collective-permute-start.1 = (f32[10,32,256]{2,1,0:T(8,128)S(1)}, f32[10,32,256]{2,1,0:T(8,128)S(1)}, u32[]{:S(2)}, u32[]{:S(2)}) collective-permute-start(f32[10,32,256]{2,1,0:T(8,128)S(1)} %pad_maximum_fusion), channel_id=1, source_target_pairs={{0,1},{1,2},{2,3},{3,4},{4,5},{5,6},{6,7},{7,8},{8,9},{9,10},{10,1... | collective-permute-start | bytes 983048 | tf_op jit(solution)/shard_map/ppermute | solution.py:24
  15.4 0.9 %slice_bitcast_fusion.4 = (f32[2,32,256]{2,1,0:T(8,128)S(1)}, f32[2,32,256]{2,1,0:T(8,128)S(1)}) fusion(f32[3,8,32,256]{3,2,1,0:T(8,128)} %ea_up.1, f32[3,8,32,256]{3,2,1,0:T(8,128)} %ef_up.1), kind=kLoop, calls=%fused_computation.18 | loop fusion | bytes 262144 | tf_op jit(solution)/shard_map/squeeze | solution.py:199
  16.3 0.0 copy-start.4
  16.4 1.3 %collective-permute-start = (f32[4,32,256]{2,1,0:T(8,128)S(1)}, f32[4,32,256]{2,1,0:T(8,128)S(1)}, u32[]{:S(2)}, u32[]{:S(2)}) collective-permute-start(f32[4,32,256]{2,1,0:T(8,128)S(1)} %pad_maximum_fusion.1), channel_id=1, source_target_pairs={{1,0},{2,1},{3,2},{4,3},{5,4},{6,5},{7,6},{8,7},{9,8},{10,9},{11,1... | collective-permute-start | bytes 393224 | tf_op jit(solution)/shard_map/ppermute | solution.py:24
  17.7 0.7 %copy.32.amp = f32[16,3]{1,0:T(8,128)} copy(f32[16,3]{0,1:T(4,128)S(1)} %copy-done.4) | data formatting | bytes 384 | tf_op args[9]
  18.4 2.4 %collective-permute-done.upper = f32[4,32,256]{2,1,0:T(8,128)S(1)} collective-permute-done((f32[4,32,256]{2,1,0:T(8,128)S(1)}, f32[4,32,256]{2,1,0:T(8,128)S(1)}, u32[]{:S(2)}, u32[]{:S(2)}) %collective-permute-start) | collective-permute-done | bytes 131104 | tf_op jit(solution)/shard_map/ppermute | solution.py:24
  20.7 0.0 collective-permute-done.1.below
  20.7 5.0 %all-to-all-done.arrived = f32[16,32,256]{2,1,0:T(8,128)S(1)} async-done(((f32[16,32,256]{2,1,0:T(8,128)}), f32[16,32,256]{2,1,0:T(8,128)S(1)}, u32[]{:S(2)}, u32[]{:S(2)}) %all-to-all-start) | async-done | bytes 524320 | tf_op jit(solution)/shard_map/all_to_all | solution.py:211
  25.7 0.0 copy-done.2
  25.7 0.8 %copy-done.1 = f32[16,32,256]{2,1,0:T(8,128)} copy-done((f32[16,32,256]{2,1,0:T(8,128)}, f32[16,32,256]{2,1,0:T(8,128)S(1)}, u32[]{:S(2)}) %copy-start.1) | copy-done | bytes 524312
  26.5 12.1 %shard_map.173 = (f32[3,8,32,256]{3,2,1,0:T(8,128)}, f32[3,8,32,256]{3,2,1,0:T(8,128)}, f32[3,8,32,256]{3,2,1,0:T(8,128)}, f32[3,8,32,256]{3,2,1,0:T(8,128)}, f32[16,32,256]{2,1,0:T(8,128)}) custom-call(f32[3,8,32,256]{3,2,1,0:T(8,128)} %ef_up.1, f32[3,8,32,256]{3,2,1,0:T(8,128)} %hf.1, f32[3,8,32,256]{3,2,1,0:T(8,128)} %pf.1, f32[3,8,32,256]{3,2,1,0:T(8,128)} %jf.1, ...), custom_call_target="tpu_custom_call" | custom-call | flops 13107200 | bytes 10485760 | tf_op jit(solution)/shard_map/pallas_call | solution.py:159
  38.6 22.3 %all_to_all.10 = f32[16,32,256]{2,1,0:T(8,128)S(1)} all-to-all(f32[16,32,256]{2,1,0:T(8,128)} %get-tuple-element.14), channel_id=1, replica_groups=mesh['grp'=2,'gx'=16] {'gx'}, dimensions={0} | all-to-all | bytes 1048576 | tf_op jit(solution)/shard_map/all_to_all | solution.py:216
  60.9 0.3 fusion.9
  61.3 0.9 %convolution_bitcast_fusion = f32[1,32,256]{2,1,0:T(8,128)} fusion(f32[32,256]{1,0:T(8,128)S(1)} %fusion.9, f32[256]{0:T(256)S(1)} %convert_reduce_fusion, s32[]{:T(128)} %bitcast.1), kind=kOutput, calls=%fused_computation | convolution fusion | flops 25559040 | bytes 66564 | tf_op jit(solution)/shard_map/xb,by->xy/dot_general | solution.py:218
  (9 shorter events, 0.1 us)
Async XLA Ops:
  0.6 1.6 %copy-start = (f32[1,32,256]{2,1,0:T(8,128)S(1)}, f32[1,32,256]{2,1,0:T(8,128)}, u32[]{:S(2)}) copy-start(f32[1,32,256]{2,1,0:T(8,128)} %param.22) | copy-start | bytes 98308
  3.8 21.9 %all-to-all-start = ((f32[16,32,256]{2,1,0:T(8,128)}), f32[16,32,256]{2,1,0:T(8,128)S(1)}, u32[]{:S(2)}, u32[]{:S(2)}) async-start(f32[16,32,256]{2,1,0:T(8,128)} %broadcast_multiply_fusion), calls=%async_computation | async-start | bytes 1048576 | tf_op jit(solution)/shard_map/all_to_all | solution.py:211
  13.1 7.6 %collective-permute-start.1 = (f32[10,32,256]{2,1,0:T(8,128)S(1)}, f32[10,32,256]{2,1,0:T(8,128)S(1)}, u32[]{:S(2)}, u32[]{:S(2)}) collective-permute-start(f32[10,32,256]{2,1,0:T(8,128)S(1)} %pad_maximum_fusion), channel_id=1, source_target_pairs={{0,1},{1,2},{2,3},{3,4},{4,5},{5,6},{6,7},{7,8},{8,9},{9,10},{10,1... | collective-permute-start | bytes 983048 | tf_op jit(solution)/shard_map/ppermute | solution.py:24
  16.3 1.3 %copy-start.4 = (f32[16,3]{0,1:T(4,128)S(1)}, f32[16,3]{0,1:T(4,128)}, u32[]{:S(2)}) copy-start(f32[16,3]{0,1:T(4,128)} %param.23) | copy-start | bytes 580
  16.4 4.4 %collective-permute-start = (f32[4,32,256]{2,1,0:T(8,128)S(1)}, f32[4,32,256]{2,1,0:T(8,128)S(1)}, u32[]{:S(2)}, u32[]{:S(2)}) collective-permute-start(f32[4,32,256]{2,1,0:T(8,128)S(1)} %pad_maximum_fusion.1), channel_id=1, source_target_pairs={{1,0},{2,1},{3,2},{4,3},{5,4},{6,5},{7,6},{8,7},{9,8},{10,9},{11,1... | collective-permute-start | bytes 393224 | tf_op jit(solution)/shard_map/ppermute | solution.py:24
  20.7 5.0 %copy-start.3 = (f32[4,32,256]{2,1,0:T(8,128)}, f32[4,32,256]{2,1,0:T(8,128)S(1)}, u32[]{:S(2)}) copy-start(f32[4,32,256]{2,1,0:T(8,128)S(1)} %collective-permute-done.upper) | copy-start | bytes 393220
  20.7 5.0 %copy-start.2 = (f32[10,32,256]{2,1,0:T(8,128)}, f32[10,32,256]{2,1,0:T(8,128)S(1)}, u32[]{:S(2)}) copy-start(f32[10,32,256]{2,1,0:T(8,128)S(1)} %collective-permute-done.1.below) | copy-start | bytes 983044
  25.7 0.8 %copy-start.1 = (f32[16,32,256]{2,1,0:T(8,128)}, f32[16,32,256]{2,1,0:T(8,128)S(1)}, u32[]{:S(2)}) copy-start(f32[16,32,256]{2,1,0:T(8,128)S(1)} %all-to-all-done.arrived) | copy-start | bytes 1572868

commit v5 on v3

--- a/solution.py
+++ b/solution.py
@@ -42,17 +42,38 @@
 
 
 def field_kernel(
-    ef, hf, pf, jf, ea, ha, pa, ja, arrived, upper, below, src, mon, amp, first,
-    ef_o, hf_o, ea_o, ha_o, ret_o, rho,
+    ef_h, hf_h, pf_h, jf_h, ea_h, ha_h, pa_h, ja_h, arrived, upper, below, src, mon, amp, first,
+    ef_oh, hf_oh, ea_oh, ha_oh, ret_o,
+    ins, outs, rho, in_sem, out_sem,
 ):
     depth, width_x, width_y = rho.shape
     slab = arrived.shape[0]
     index = lax.axis_index("gx")
     start = first[0]
+    sources = (ef_h, hf_h, pf_h, jf_h, ea_h, ha_h, pa_h, ja_h)
+    targets = (ef_oh, hf_oh, ea_oh, ha_oh)
+
+    def fetch(a, z):
+        return pltpu.make_async_copy(
+            sources[a].at[:, pl.ds(z, 1)], ins.at[a, :, pl.ds(z, 1)], in_sem.at[a, z]
+        )
+
+    def store(a, z):
+        return pltpu.make_async_copy(
+            outs.at[a, :, pl.ds(z, 1)], targets[a].at[:, pl.ds(z, 1)], out_sem.at[a, z]
+        )
+
+    for z in range(depth):
+        for a in range(8):
+            fetch(a, z).start()
+
     for z in range(depth):
         p = index * depth + z - start
         inside = (p >= 0) & (p < slab)
         rho[z] = jnp.where(inside, arrived[jnp.clip(p, 0, slab - 1)], 0.0)
+    for g in range(slab):
+        ret_o[g] = jnp.zeros((width_x, width_y), jnp.float32)
+
     row = lax.broadcasted_iota(jnp.int32, (width_x, width_y), 0)
     lane = lax.broadcasted_iota(jnp.int32, (width_x, width_y), 1)
 
@@ -68,91 +89,100 @@
     def behind_x(f):
         return jnp.where(row == 0, 0.0, pltpu.roll(f, 1, 0))
 
-    def new_h(e, h, z, ex_up, ey_up):
-        ex, ey, ez = e[0, z], e[1, z], e[2, z]
-        curl_x = ahead_y(ez) - ez - (ey_up - ey)
-        curl_y = ex_up - ex - (ahead_x(ez) - ez)
-        curl_z = ahead_x(ey) - ey - (ahead_y(ex) - ex)
-        return (h[0, z] - DT * curl_x, h[1, z] - DT * curl_y, h[2, z] - DT * curl_z)
-
-    def lower_h(e, base):
-        hx, hy, ex, ey, ez = (below[base + i] for i in range(5))
+    plane = width_x * width_y
+    tile_row = lax.broadcasted_iota(jnp.int32, (8, width_y), 0)
+    tile_lane = lax.broadcasted_iota(jnp.int32, (8, width_y), 1)
+
+    def locate(cell):
+        zz = cell // plane
+        rest = cell - zz * plane
+        x = rest // width_y
+        y = rest - x * width_y
+        return zz - index * depth, x, y
+
+    src_at = [locate(src[s]) for s in range(src.shape[0])]
+    mon_at = [locate(mon[m]) for m in range(mon.shape[0])]
+
+    def add_at(where_, z, out, value_of):
+        local, x, y = where_
+        x0 = pl.multiple_of((x // 8) * 8, 8)
+
+        @pl.when(local == z)
+        def _():
+            rows = pl.ds(x0, 8)
+            hit = (tile_row == x - x0) & (tile_lane == y)
+            gain = DT / (1.0 + EPS_RANGE * rho[z, rows, :])
+            for c in range(3):
+                held = outs[out, c, z, rows, :]
+                outs[out, c, z, rows, :] = held + jnp.where(hit, gain * value_of(c, z, rows), 0.0)
+
+    keep = index > 0
+    prev = []
+    for r in range(2):
+        fetch(4 * r, 0).wait()
+        fetch(4 * r + 1, 0).wait()
+        hx, hy, ex, ey, ez = (below[5 * r + i] for i in range(5))
+        e = ins.at[4 * r]
         curl_x = ahead_y(ez) - ez - (e[1, 0] - ey)
         curl_y = e[0, 0] - ex - (ahead_x(ez) - ez)
-        keep = index > 0
-        return (
-            jnp.where(keep, hx - DT * curl_x, 0.0),
-            jnp.where(keep, hy - DT * curl_y, 0.0),
-        )
-
-    def new_e(e, p, j, out, z, hn, hn_dn, step, strength):
-        hx, hy, hz = hn
-        hx_dn, hy_dn = hn_dn
-        curl = (
-            hz - behind_y(hz) - (hy - hy_dn),
-            hx - hx_dn - (hz - behind_x(hz)),
-            hy - behind_x(hy) - (hx - behind_y(hx)),
-        )
-        for c in range(3):
-            j_next = (KEEP * j[c, z] + DT * (strength * e[c, z] - p[c, z])) / LOSS
-            out[c, z] = e[c, z] + step * (curl[c] - j_next)
-
-    runs = ((ef, hf, pf, jf, hf_o, ef_o, 0), (ea, ha, pa, ja, ha_o, ea_o, 2))
-    prev = [lower_h(ef, 0), lower_h(ea, 5)]
-    for z in range(depth):
+        prev.append((jnp.where(keep, hx - DT * curl_x, 0.0), jnp.where(keep, hy - DT * curl_y, 0.0)))
+    for r in range(2):
+        fetch(4 * r + 2, 0).wait()
+        fetch(4 * r + 3, 0).wait()
+
+    for z in range(depth):
+        if z + 1 < depth:
+            for a in range(8):
+                fetch(a, z + 1).wait()
         density = rho[z]
         step = DT / (1.0 + EPS_RANGE * density)
         strength = STRENGTH_BASE + STRENGTH_RANGE * density
-        for r, (e, h, p, j, h_out, e_out, up) in enumerate(runs):
+        for r in range(2):
+            e, h, p, j = (ins.at[4 * r + i] for i in range(4))
             if z + 1 < depth:
                 ex_up, ey_up = e[0, z + 1], e[1, z + 1]
             else:
-                ex_up, ey_up = upper[up], upper[up + 1]
-            hn = new_h(e, h, z, ex_up, ey_up)
+                ex_up, ey_up = upper[2 * r], upper[2 * r + 1]
+            ex, ey, ez = e[0, z], e[1, z], e[2, z]
+            hx = h[0, z] - DT * (ahead_y(ez) - ez - (ey_up - ey))
+            hy = h[1, z] - DT * (ex_up - ex - (ahead_x(ez) - ez))
+            hz = h[2, z] - DT * (ahead_x(ey) - ey - (ahead_y(ex) - ex))
+            outs[2 * r + 1, 0, z] = hx
+            outs[2 * r + 1, 1, z] = hy
+            outs[2 * r + 1, 2, z] = hz
+            hx_dn, hy_dn = prev[r]
+            curl = (
+                hz - behind_y(hz) - (hy - hy_dn),
+                hx - hx_dn - (hz - behind_x(hz)),
+                hy - behind_x(hy) - (hx - behind_y(hx)),
+            )
             for c in range(3):
-                h_out[c, z] = hn[c]
-            new_e(e, p, j, e_out, z, hn, prev[r], step, strength)
-            prev[r] = (hn[0], hn[1])
-
-    plane = width_x * width_y
-    tile_row = lax.broadcasted_iota(jnp.int32, (8, width_y), 0)
-    tile_lane = lax.broadcasted_iota(jnp.int32, (8, width_y), 1)
-
-    def add_at(cell, out, value_of):
-        zz = cell // plane
-        local = zz - index * depth
-        rest = cell - zz * plane
-        x = rest // width_y
-        y = rest - x * width_y
-        x0 = pl.multiple_of((x // 8) * 8, 8)
-
-        @pl.when((local >= 0) & (local < depth))
-        def _():
-            rows = pl.ds(x0, 8)
-            hit = (tile_row == x - x0) & (tile_lane == y)
-            step = DT / (1.0 + EPS_RANGE * rho[local, rows, :])
-            for c in range(3):
-                held = out[c, local, rows, :]
-                out[c, local, rows, :] = held + jnp.where(hit, step * value_of(c, local, rows), 0.0)
-
-    for s in range(src.shape[0]):
-        add_at(src[s], ef_o, lambda c, local, rows, s=s: amp[s, c])
-    for m in range(mon.shape[0]):
-        add_at(mon[m], ea_o, lambda c, local, rows: ef[c, local, rows, :])
-
-    for g in range(slab):
-        ret_o[g] = jnp.zeros((width_x, width_y), jnp.float32)
-    for z in range(depth):
+                j_next = (KEEP * j[c, z] + DT * (strength * e[c, z] - p[c, z])) / LOSS
+                outs[2 * r, c, z] = e[c, z] + step * (curl[c] - j_next)
+            prev[r] = (hx, hy)
+            store(2 * r + 1, z).start()
+
+        for s in range(src.shape[0]):
+            add_at(src_at[s], z, 0, lambda c, zz, rows, s=s: amp[s, c])
+        for m in range(mon.shape[0]):
+            add_at(mon_at[m], z, 2, lambda c, zz, rows: ins[0, c, zz, rows, :])
+        store(0, z).start()
+        store(2, z).start()
+
         total = None
         for c in range(3):
-            fwd = ef_o[c, z]
-            term = ea_o[c, z] * (fwd - ef[c, z] + GAIN_FIELD * fwd)
+            fwd = outs[0, c, z]
+            term = outs[2, c, z] * (fwd - ins[0, c, z] + GAIN_FIELD * fwd)
             total = term if total is None else total + term
         p = index * depth + z - start
 
         @pl.when((p >= 0) & (p < slab))
         def _():
             ret_o[jnp.clip(p, 0, slab - 1)] = total
+
+    for z in range(depth):
+        for a in range(4):
+            store(a, z).wait()
 
 
 def fields(e_forward, h_forward, p_forward, j_forward, e_adjoint, h_adjoint, p_adjoint, j_adjoint,
@@ -160,15 +190,22 @@
     shape = e_forward.shape
     depth = shape[1]
     field = jax.ShapeDtypeStruct(shape, jnp.float32)
+    hbm = pl.BlockSpec(memory_space=pltpu.HBM)
     vmem = pl.BlockSpec(memory_space=pltpu.VMEM)
     smem = pl.BlockSpec(memory_space=pltpu.SMEM)
     cells = shape[1] * shape[2] * shape[3]
     return pl.pallas_call(
         field_kernel,
         out_shape=(field, field, field, field, jax.ShapeDtypeStruct(arrived.shape, jnp.float32)),
-        in_specs=[vmem] * 11 + [smem] * 4,
-        out_specs=(vmem,) * 5,
-        scratch_shapes=[pltpu.VMEM(shape[1:], jnp.float32)],
+        in_specs=[hbm] * 8 + [vmem] * 3 + [smem] * 4,
+        out_specs=(hbm,) * 4 + (vmem,),
+        scratch_shapes=[
+            pltpu.VMEM((8,) + shape, jnp.float32),
+            pltpu.VMEM((4,) + shape, jnp.float32),
+            pltpu.VMEM(shape[1:], jnp.float32),
+            pltpu.SemaphoreType.DMA((8, depth)),
+            pltpu.SemaphoreType.DMA((4, depth)),
+        ],
         compiler_params=pltpu.CompilerParams(vmem_limit_bytes=48 * 1024 * 1024),
         cost_estimate=pl.CostEstimate(
             flops=200 * cells, bytes_accessed=4 * cells * 40, transcendentals=0

time: 57.3 us -> 60.4 us (1.054)
  Pallas kernels: 5.97 us -> 9.04 us
    pallas_call x1, Pallas kernels: 5.97 us -> 9.04 us  [fields(): pl.pallas_call(field_kernel, out_shape=(field, field, field, field, jax.S...]
where the time goes in v5:
time: 60.4 us; the launch traced here: 59.9 us
  blocking collectives  21.4 us (35%)
  starting transfers between devices  11.1 us (18%)
  Pallas kernels  9.04 us (15%)
  waiting for transfers between devices  9.01 us (15%)
  local copies, waits for them, and re-layouts  3.28 us (5%)
  between operations  2.15 us (4%)
  other arithmetic  1.96 us (3%)
  matrix products  1.88 us (3%)
    all_to_all x1, blocking collectives, body(): lax.all_to_all(returned, 'gx', split_axis=0, concat_axis=0, tiled=True)  21.4 us
    pallas_call x1, Pallas kernels, fields(): pl.pallas_call(field_kernel, out_shape=(field, field, field, field, jax.S...  9.04 us
    all_to_all x1, starting transfers between devices, body(): lax.all_to_all(slots, 'gx', split_axis=0, concat_axis=0, tiled=True)  7.52 us
    all_to_all x1, waiting for transfers between devices, body(): lax.all_to_all(slots, 'gx', split_axis=0, concat_axis=0, tiled=True)  6.04 us
    ppermute x2, starting transfers between devices, passed_along(): return lax.ppermute(block, axis, route)  3.61 us
    ppermute x2, waiting for transfers between devices, passed_along(): return lax.ppermute(block, axis, route)  2.97 us
    unnamed x19, local copies, waits for them, and re-layouts  2.4 us
  transfers between devices with their start and end apart: 3, of which 2 were waited for; matrix products, arithmetic and copies ran while one was open for 3% of the time, Pallas kernels for 0%

profile of v5, /device:TPU:0, one launch (start us, length us, event | category | flops | bytes accessed | tf_op | source)
XLA Modules:
  0.0 59.9 jit_solution(6048607340589694714)
XLA Ops:
  0.6 0.0 copy-start
  2.0 0.1 convert_reduce_fusion.1
  2.1 0.2 convert_reduce_fusion
  2.3 0.2 fusion.7
  2.5 0.0 copy-start.3
  2.5 0.4 fusion
  2.9 0.0 copy-start.2
  3.0 0.9 %broadcast_multiply_fusion = f32[16,32,256]{2,1,0:T(8,128)} fusion(f32[32,256]{1,0:T(8,128)S(1)} %fusion, f32[16]{0:T(128)S(1)} %compare_convert_fusion), kind=kLoop, calls=%fused_computation.2 | loop fusion | flops 131072 | bytes 557120 | tf_op jit(solution)/shard_map/mul | solution.py:250
  3.9 7.5 %all-to-all-start = ((f32[16,32,256]{2,1,0:T(8,128)}), f32[16,32,256]{2,1,0:T(8,128)S(1)}, u32[]{:S(2)}, u32[]{:S(2)}) async-start(f32[16,32,256]{2,1,0:T(8,128)} %broadcast_multiply_fusion), calls=%async_computation | async-start | bytes 1048576 | tf_op jit(solution)/shard_map/all_to_all | solution.py:251
  11.4 0.9 %slice_bitcast_fusion.2 = (f32[2,32,256]{2,1,0:T(8,128)S(1)}, f32[2,32,256]{2,1,0:T(8,128)S(1)}) fusion(f32[3,8,32,256]{3,2,1,0:T(8,128)} %ha_h.1, f32[3,8,32,256]{3,2,1,0:T(8,128)S(1)} %copy-done.3), kind=kLoop, calls=%fused_computation.16 | loop fusion | bytes 262144 | tf_op jit(solution)/shard_map/squeeze | solution.py:242
  12.3 0.7 %pad_maximum_fusion = f32[10,32,256]{2,1,0:T(8,128)} fusion(f32[3,32,256]{2,1,0:T(8,128)S(1)} %get-tuple-element.17, f32[2,32,256]{2,1,0:T(8,128)S(1)} %get-tuple-element.19, f32[3,32,256]{2,1,0:T(8,128)S(1)} %get-tuple-element.18, f32[2,32,256]{2,1,0:T(8,128)S(1)} %get-tuple-element.20), kind=kLoop, calls=%fused_computation.1 | loop fusion | flops 245760 | bytes 655360 | tf_op jit(solution)/shard_map/concatenate | solution.py:241
  13.0 2.3 %collective-permute-start.1 = (f32[10,32,256]{2,1,0:T(8,128)}, f32[10,32,256]{2,1,0:T(8,128)S(1)}, u32[]{:S(2)}, u32[]{:S(2)}) collective-permute-start(f32[10,32,256]{2,1,0:T(8,128)} %pad_maximum_fusion), channel_id=1, source_target_pairs={{0,1},{1,2},{2,3},{3,4},{4,5},{5,6},{6,7},{7,8},{8,9},{9,10},{10,1... | collective-permute-start | bytes 983048 | tf_op jit(solution)/shard_map/ppermute | solution.py:24
  15.4 0.0 copy-start.8
  15.4 0.0 copy-start.6
  15.4 1.3 %collective-permute-start = (f32[4,32,256]{2,1,0:T(8,128)S(1)}, f32[4,32,256]{2,1,0:T(8,128)S(1)}, u32[]{:S(2)}, u32[]{:S(2)}) collective-permute-start(f32[4,32,256]{2,1,0:T(8,128)S(1)} %pad_maximum_fusion.1), channel_id=1, source_target_pairs={{1,0},{2,1},{3,2},{4,3},{5,4},{6,5},{7,6},{8,7},{9,8},{10,9},{11,1... | collective-permute-start | bytes 393224 | tf_op jit(solution)/shard_map/ppermute | solution.py:24
  16.8 0.1 copy.32.amp
  16.8 3.0 %collective-permute-done.upper = f32[4,32,256]{2,1,0:T(8,128)S(1)} collective-permute-done((f32[4,32,256]{2,1,0:T(8,128)S(1)}, f32[4,32,256]{2,1,0:T(8,128)S(1)}, u32[]{:S(2)}, u32[]{:S(2)}) %collective-permute-start) | collective-permute-done | bytes 131104 | tf_op jit(solution)/shard_map/ppermute | solution.py:24
  19.8 6.0 %all-to-all-done.arrived = f32[16,32,256]{2,1,0:T(8,128)S(1)} async-done(((f32[16,32,256]{2,1,0:T(8,128)}), f32[16,32,256]{2,1,0:T(8,128)S(1)}, u32[]{:S(2)}, u32[]{:S(2)}) %all-to-all-start) | async-done | bytes 524320 | tf_op jit(solution)/shard_map/all_to_all | solution.py:251
  25.9 1.1 %copy-done.4 = f32[3,8,32,256]{3,2,1,0:T(8,128)S(1)} copy-done((f32[3,8,32,256]{3,2,1,0:T(8,128)S(1)}, f32[3,8,32,256]{3,2,1,0:T(8,128)}, u32[]{:S(2)}) %copy-start.4) | copy-done | bytes 786456
  27.0 1.1 %copy-done.5 = f32[3,8,32,256]{3,2,1,0:T(8,128)S(1)} copy-done((f32[3,8,32,256]{3,2,1,0:T(8,128)S(1)}, f32[3,8,32,256]{3,2,1,0:T(8,128)}, u32[]{:S(2)}) %copy-start.5) | copy-done | bytes 786456
  28.1 9.0 %shard_map.173 = (f32[3,8,32,256]{3,2,1,0:T(8,128)}, f32[3,8,32,256]{3,2,1,0:T(8,128)}, f32[3,8,32,256]{3,2,1,0:T(8,128)}, f32[3,8,32,256]{3,2,1,0:T(8,128)}, f32[16,32,256]{2,1,0:T(8,128)S(1)}) custom-call(f32[3,8,32,256]{3,2,1,0:T(8,128)S(1)} %copy-done.1, f32[3,8,32,256]{3,2,1,0:T(8,128)S(1)} %copy-done.3, f32[3,8,32,256]{3,2,1,0:T(8,128)S(1)} %copy-done.4, ...), custom_call_target="tpu_custom_call" | custom-call | flops 13107200 | bytes 10485760 | tf_op jit(solution)/shard_map/pallas_call | solution.py:197
  37.2 21.4 %all_to_all.10 = f32[16,32,256]{2,1,0:T(8,128)S(1)} all-to-all(f32[16,32,256]{2,1,0:T(8,128)S(1)} %get-tuple-element.14), channel_id=1, replica_groups=mesh['grp'=2,'gx'=16] {'gx'}, dimensions={0} | all-to-all | bytes 1048576 | tf_op jit(solution)/shard_map/all_to_all | solution.py:256
  58.6 0.3 fusion.9
  58.9 0.9 %convolution_bitcast_fusion = f32[1,32,256]{2,1,0:T(8,128)} fusion(f32[32,256]{1,0:T(8,128)S(1)} %fusion.9, f32[256]{0:T(256)S(1)} %convert_reduce_fusion, s32[]{:T(128)} %bitcast.1), kind=kOutput, calls=%fused_computation | convolution fusion | flops 25559040 | bytes 66564 | tf_op jit(solution)/shard_map/xb,by->xy/dot_general | solution.py:258
  (17 shorter events, 0.1 us)
Async XLA Ops:
  0.6 1.6 %copy-start = (f32[1,32,256]{2,1,0:T(8,128)S(1)}, f32[1,32,256]{2,1,0:T(8,128)}, u32[]{:S(2)}) copy-start(f32[1,32,256]{2,1,0:T(8,128)} %param.22) | copy-start | bytes 98308
  2.5 8.9 %copy-start.3 = (f32[3,8,32,256]{3,2,1,0:T(8,128)S(1)}, f32[3,8,32,256]{3,2,1,0:T(8,128)}, u32[]{:S(2)}) copy-start(f32[3,8,32,256]{3,2,1,0:T(8,128)} %hf_h.1) | copy-start | bytes 2359300
  2.9 9.3 %copy-start.2 = (f32[3,8,32,256]{3,2,1,0:T(8,128)S(1)}, f32[3,8,32,256]{3,2,1,0:T(8,128)}, u32[]{:S(2)}) copy-start(f32[3,8,32,256]{3,2,1,0:T(8,128)} %ea_h.1) | copy-start | bytes 2359300
  3.9 8.4 %copy-start.1 = (f32[3,8,32,256]{3,2,1,0:T(8,128)S(1)}, f32[3,8,32,256]{3,2,1,0:T(8,128)}, u32[]{:S(2)}) copy-start(f32[3,8,32,256]{3,2,1,0:T(8,128)} %ef_h.1) | copy-start | bytes 2359300
  3.9 22.0 %all-to-all-start = ((f32[16,32,256]{2,1,0:T(8,128)}), f32[16,32,256]{2,1,0:T(8,128)S(1)}, u32[]{:S(2)}, u32[]{:S(2)}) async-start(f32[16,32,256]{2,1,0:T(8,128)} %broadcast_multiply_fusion), calls=%async_computation | async-start | bytes 1048576 | tf_op jit(solution)/shard_map/all_to_all | solution.py:251
  13.0 6.8 %collective-permute-start.1 = (f32[10,32,256]{2,1,0:T(8,128)}, f32[10,32,256]{2,1,0:T(8,128)S(1)}, u32[]{:S(2)}, u32[]{:S(2)}) collective-permute-start(f32[10,32,256]{2,1,0:T(8,128)} %pad_maximum_fusion), channel_id=1, source_target_pairs={{0,1},{1,2},{2,3},{3,4},{4,5},{5,6},{6,7},{7,8},{8,9},{9,10},{10,1... | collective-permute-start | bytes 983048 | tf_op jit(solution)/shard_map/ppermute | solution.py:24
  15.4 1.4 %copy-start.8 = (f32[16,3]{0,1:T(4,128)S(1)}, f32[16,3]{0,1:T(4,128)}, u32[]{:S(2)}) copy-start(f32[16,3]{0,1:T(4,128)} %param.23) | copy-start | bytes 580
  15.4 10.4 %copy-start.6 = (s32[16]{0:T(128)S(1)}, s32[16]{0:T(128)}, u32[]{:S(2)}) copy-start(s32[16]{0:T(128)} %src.1) | copy-start | bytes 196
  15.4 10.4 %copy-start.7 = (s32[16]{0:T(128)S(1)}, s32[16]{0:T(128)}, u32[]{:S(2)}) copy-start(s32[16]{0:T(128)} %mon.1) | copy-start | bytes 196
  15.4 4.4 %collective-permute-start = (f32[4,32,256]{2,1,0:T(8,128)S(1)}, f32[4,32,256]{2,1,0:T(8,128)S(1)}, u32[]{:S(2)}, u32[]{:S(2)}) collective-permute-start(f32[4,32,256]{2,1,0:T(8,128)S(1)} %pad_maximum_fusion.1), channel_id=1, source_target_pairs={{1,0},{2,1},{3,2},{4,3},{5,4},{6,5},{7,6},{8,7},{9,8},{10,9},{11,1... | collective-permute-start | bytes 393224 | tf_op jit(solution)/shard_map/ppermute | solution.py:24
  25.9 1.1 %copy-start.4 = (f32[3,8,32,256]{3,2,1,0:T(8,128)S(1)}, f32[3,8,32,256]{3,2,1,0:T(8,128)}, u32[]{:S(2)}) copy-start(f32[3,8,32,256]{3,2,1,0:T(8,128)} %pf_h.1) | copy-start | bytes 2359300
  27.0 1.1 %copy-start.5 = (f32[3,8,32,256]{3,2,1,0:T(8,128)S(1)}, f32[3,8,32,256]{3,2,1,0:T(8,128)}, u32[]{:S(2)}) copy-start(f32[3,8,32,256]{3,2,1,0:T(8,128)} %jf_h.1) | copy-start | bytes 2359300

commit v6 on v3

--- a/solution.py
+++ b/solution.py
@@ -16,6 +16,7 @@
 HIGH = lax.Precision.HIGHEST
 KEEP = 1.0 - DAMPING * DT / 2.0
 LOSS = 1.0 + DAMPING * DT / 2.0
+SHRINK = 1.0 / LOSS
 
 
 def passed_along(block, axis, distance):
@@ -42,7 +43,7 @@
 
 
 def field_kernel(
-    ef, hf, pf, jf, ea, ha, pa, ja, arrived, upper, below, src, mon, amp, first,
+    ef, hf, ea, ha, pa, ja, pf, jf, arrived, upper, below, src, mon, amp, first,
     ef_o, hf_o, ea_o, ha_o, ret_o, rho,
 ):
     depth, width_x, width_y = rho.shape
@@ -94,7 +95,7 @@
             hy - behind_x(hy) - (hx - behind_y(hx)),
         )
         for c in range(3):
-            j_next = (KEEP * j[c, z] + DT * (strength * e[c, z] - p[c, z])) / LOSS
+            j_next = (KEEP * j[c, z] + DT * (strength * e[c, z] - p[c, z])) * SHRINK
             out[c, z] = e[c, z] + step * (curl[c] - j_next)
 
     runs = ((ef, hf, pf, jf, hf_o, ef_o, 0), (ea, ha, pa, ja, ha_o, ea_o, 2))
@@ -169,11 +170,11 @@
         in_specs=[vmem] * 11 + [smem] * 4,
         out_specs=(vmem,) * 5,
         scratch_shapes=[pltpu.VMEM(shape[1:], jnp.float32)],
-        compiler_params=pltpu.CompilerParams(vmem_limit_bytes=48 * 1024 * 1024),
+        compiler_params=pltpu.CompilerParams(vmem_limit_bytes=56 * 1024 * 1024),
         cost_estimate=pl.CostEstimate(
             flops=200 * cells, bytes_accessed=4 * cells * 40, transcendentals=0
         ),
-    )(e_forward, h_forward, p_forward, j_forward, e_adjoint, h_adjoint, p_adjoint, j_adjoint,
+    )(e_forward, h_forward, e_adjoint, h_adjoint, p_adjoint, j_adjoint, p_forward, j_forward,
       arrived, upper, below, source_cell, monitor_cell, source_amp, slab_start)
 
 

time: 57.3 us -> 58.2 us (1.016)
  waiting for transfers between devices: 9.01 us -> 7.36 us
  Pallas kernels: 5.97 us -> 7.53 us
  local copies, waits for them, and re-layouts: 3.28 us -> 4.24 us
  blocking collectives: 21.4 us -> 22.3 us
  other arithmetic: 1.96 us -> 1.24 us
    pallas_call x1, Pallas kernels: 5.97 us -> 7.53 us  [fields(): pl.pallas_call(field_kernel, out_shape=(field, field, field, field, jax.S...]
    all_to_all x1, waiting for transfers between devices: 6.04 us -> 4.99 us  [body(): lax.all_to_all(slots, 'gx', split_axis=0, concat_axis=0, tiled=True)]
    squeeze x1, local copies, waits for them, and re-layouts: 0.02 us -> 0.96 us  [body(): e_adjoint[:, -1]]
    all_to_all x1, blocking collectives: 21.4 us -> 22.3 us  [body(): lax.all_to_all(returned, 'gx', split_axis=0, concat_axis=0, tiled=True)]
    unnamed x19 -> x11, local copies, waits for them, and re-layouts: 2.4 us -> 1.5 us
    squeeze x1, local copies, waits for them, and re-layouts: 0.01 us -> 0.89 us  [body(): e_adjoint[0:2, 0]]
    concatenate x1, other arithmetic: 0.75 us -> 0.02 us  [body(): jnp.concatenate([h_forward[0:2, -1], e_forward[:, -1], h_adjoint[0:2, -1]...]
    ppermute x2, waiting for transfers between devices: 2.97 us -> 2.37 us  [passed_along(): return lax.ppermute(block, axis, route)]
  transfers between devices with their start and end apart: 3 -> 3, of which waited for: 2 -> 2; matrix products, arithmetic and copies ran while one was open for 3% -> 6% of each run, Pallas kernels for 0% -> 0%
where the time goes in v6:
time: 58.2 us; the launch traced here: 57.6 us
  blocking collectives  22.3 us (38%)
  starting transfers between devices  11 us (19%)
  Pallas kernels  7.53 us (13%)
  waiting for transfers between devices  7.36 us (13%)
  local copies, waits for them, and re-layouts  4.24 us (7%)
  between operations  2.08 us (4%)
  matrix products  1.88 us (3%)
  other arithmetic  1.24 us (2%)
    all_to_all x1, blocking collectives, body(): lax.all_to_all(returned, 'gx', split_axis=0, concat_axis=0, tiled=True)  22.3 us
    pallas_call x1, Pallas kernels, fields(): pl.pallas_call(field_kernel, out_shape=(field, field, field, field, jax.S...  7.53 us
    all_to_all x1, starting transfers between devices, body(): lax.all_to_all(slots, 'gx', split_axis=0, concat_axis=0, tiled=True)  7.38 us
    all_to_all x1, waiting for transfers between devices, body(): lax.all_to_all(slots, 'gx', split_axis=0, concat_axis=0, tiled=True)  4.99 us
    ppermute x2, starting transfers between devices, passed_along(): return lax.ppermute(block, axis, route)  3.62 us
    ppermute x2, waiting for transfers between devices, passed_along(): return lax.ppermute(block, axis, route)  2.37 us
    unnamed x11, local copies, waits for them, and re-layouts  1.5 us
  transfers between devices with their start and end apart: 3, of which 2 were waited for; matrix products, arithmetic and copies ran while one was open for 6% of the time, Pallas kernels for 0%

profile of v6, /device:TPU:0, one launch (start us, length us, event | category | flops | bytes accessed | tf_op | source)
XLA Modules:
  0.0 57.6 jit_solution(10850470981219565518)
XLA Ops:
  0.6 0.0 copy-start
  2.0 0.1 convert_reduce_fusion.1
  2.1 0.2 convert_reduce_fusion
  2.3 0.2 fusion.7
  2.5 0.4 fusion
  2.9 0.9 %broadcast_multiply_fusion = f32[16,32,256]{2,1,0:T(8,128)} fusion(f32[32,256]{1,0:T(8,128)S(1)} %fusion, f32[16]{0:T(128)S(1)} %compare_convert_fusion), kind=kLoop, calls=%fused_computation.2 | loop fusion | flops 131072 | bytes 557120 | tf_op jit(solution)/shard_map/mul | solution.py:214
  3.8 7.4 %all-to-all-start = ((f32[16,32,256]{2,1,0:T(8,128)}), f32[16,32,256]{2,1,0:T(8,128)S(1)}, u32[]{:S(2)}, u32[]{:S(2)}) async-start(f32[16,32,256]{2,1,0:T(8,128)} %broadcast_multiply_fusion), calls=%async_computation | async-start | bytes 1048576 | tf_op jit(solution)/shard_map/all_to_all | solution.py:215
  11.2 0.9 %slice_bitcast_fusion.2 = (f32[2,32,256]{2,1,0:T(8,128)S(1)}, f32[2,32,256]{2,1,0:T(8,128)S(1)}) fusion(f32[3,8,32,256]{3,2,1,0:T(8,128)} %ha.1, f32[3,8,32,256]{3,2,1,0:T(8,128)} %hf.1), kind=kLoop, calls=%fused_computation.16 | loop fusion | bytes 262144 | tf_op jit(solution)/shard_map/squeeze | solution.py:206
  12.1 1.0 %slice_bitcast_fusion = (f32[3,32,256]{2,1,0:T(8,128)S(1)}, f32[3,32,256]{2,1,0:T(8,128)S(1)}) fusion(f32[3,8,32,256]{3,2,1,0:T(8,128)} %ea.1, f32[3,8,32,256]{3,2,1,0:T(8,128)} %ef.1), kind=kLoop, calls=%fused_computation.14 | loop fusion | bytes 393216 | tf_op jit(solution)/shard_map/squeeze | solution.py:206
  13.1 2.3 %collective-permute-start.1 = (f32[10,32,256]{2,1,0:T(8,128)S(1)}, f32[10,32,256]{2,1,0:T(8,128)S(1)}, u32[]{:S(2)}, u32[]{:S(2)}) collective-permute-start(f32[10,32,256]{2,1,0:T(8,128)S(1)} %pad_maximum_fusion), channel_id=1, source_target_pairs={{0,1},{1,2},{2,3},{3,4},{4,5},{5,6},{6,7},{7,8},{8,9},{9,10},{10,1... | collective-permute-start | bytes 983048 | tf_op jit(solution)/shard_map/ppermute | solution.py:25
  15.4 0.9 %slice_bitcast_fusion.4 = (f32[2,32,256]{2,1,0:T(8,128)S(1)}, f32[2,32,256]{2,1,0:T(8,128)S(1)}) fusion(f32[3,8,32,256]{3,2,1,0:T(8,128)} %ea.1, f32[3,8,32,256]{3,2,1,0:T(8,128)} %ef.1), kind=kLoop, calls=%fused_computation.18 | loop fusion | bytes 262144 | tf_op jit(solution)/shard_map/squeeze | solution.py:203
  16.3 0.0 copy-start.4
  16.4 1.3 %collective-permute-start = (f32[4,32,256]{2,1,0:T(8,128)S(1)}, f32[4,32,256]{2,1,0:T(8,128)S(1)}, u32[]{:S(2)}, u32[]{:S(2)}) collective-permute-start(f32[4,32,256]{2,1,0:T(8,128)S(1)} %pad_maximum_fusion.1), channel_id=1, source_target_pairs={{1,0},{2,1},{3,2},{4,3},{5,4},{6,5},{7,6},{8,7},{9,8},{10,9},{11,1... | collective-permute-start | bytes 393224 | tf_op jit(solution)/shard_map/ppermute | solution.py:25
  17.7 0.0 copy-done.4
  17.7 0.7 %copy.32.amp = f32[16,3]{1,0:T(8,128)} copy(f32[16,3]{0,1:T(4,128)S(1)} %copy-done.4) | data formatting | bytes 384 | tf_op args[9]
  18.4 2.4 %collective-permute-done.upper = f32[4,32,256]{2,1,0:T(8,128)S(1)} collective-permute-done((f32[4,32,256]{2,1,0:T(8,128)S(1)}, f32[4,32,256]{2,1,0:T(8,128)S(1)}, u32[]{:S(2)}, u32[]{:S(2)}) %collective-permute-start) | collective-permute-done | bytes 131104 | tf_op jit(solution)/shard_map/ppermute | solution.py:25
  20.7 0.0 collective-permute-done.1.below
  20.7 5.0 %all-to-all-done.arrived = f32[16,32,256]{2,1,0:T(8,128)S(1)} async-done(((f32[16,32,256]{2,1,0:T(8,128)}), f32[16,32,256]{2,1,0:T(8,128)S(1)}, u32[]{:S(2)}, u32[]{:S(2)}) %all-to-all-start) | async-done | bytes 524320 | tf_op jit(solution)/shard_map/all_to_all | solution.py:215
  25.7 0.0 copy-done.3
  25.7 0.8 %copy-done.1 = f32[16,32,256]{2,1,0:T(8,128)} copy-done((f32[16,32,256]{2,1,0:T(8,128)}, f32[16,32,256]{2,1,0:T(8,128)S(1)}, u32[]{:S(2)}) %copy-start.1) | copy-done | bytes 524312
  26.5 7.5 %shard_map.173 = (f32[3,8,32,256]{3,2,1,0:T(8,128)}, f32[3,8,32,256]{3,2,1,0:T(8,128)}, f32[3,8,32,256]{3,2,1,0:T(8,128)}, f32[3,8,32,256]{3,2,1,0:T(8,128)}, f32[16,32,256]{2,1,0:T(8,128)}) custom-call(f32[3,8,32,256]{3,2,1,0:T(8,128)} %ef.1, f32[3,8,32,256]{3,2,1,0:T(8,128)} %hf.1, f32[3,8,32,256]{3,2,1,0:T(8,128)} %ea.1, f32[3,8,32,256]{3,2,1,0:T(8,128)} %ha.1, ...), custom_call_target="tpu_custom_call" | custom-call | flops 13107200 | bytes 10485760 | tf_op jit(solution)/shard_map/pallas_call | solution.py:167
  34.1 22.3 %all_to_all.10 = f32[16,32,256]{2,1,0:T(8,128)S(1)} all-to-all(f32[16,32,256]{2,1,0:T(8,128)} %get-tuple-element.14), channel_id=1, replica_groups=mesh['grp'=2,'gx'=16] {'gx'}, dimensions={0} | all-to-all | bytes 1048576 | tf_op jit(solution)/shard_map/all_to_all | solution.py:220
  56.4 0.3 fusion.9
  56.7 0.9 %convolution_bitcast_fusion = f32[1,32,256]{2,1,0:T(8,128)} fusion(f32[32,256]{1,0:T(8,128)S(1)} %fusion.9, f32[256]{0:T(256)S(1)} %convert_reduce_fusion, s32[]{:T(128)} %bitcast.1), kind=kOutput, calls=%fused_computation | convolution fusion | flops 25559040 | bytes 66564 | tf_op jit(solution)/shard_map/xb,by->xy/dot_general | solution.py:222
  (9 shorter events, 0.1 us)
Async XLA Ops:
  0.6 1.6 %copy-start = (f32[1,32,256]{2,1,0:T(8,128)S(1)}, f32[1,32,256]{2,1,0:T(8,128)}, u32[]{:S(2)}) copy-start(f32[1,32,256]{2,1,0:T(8,128)} %param.22) | copy-start | bytes 98308
  3.8 21.9 %all-to-all-start = ((f32[16,32,256]{2,1,0:T(8,128)}), f32[16,32,256]{2,1,0:T(8,128)S(1)}, u32[]{:S(2)}, u32[]{:S(2)}) async-start(f32[16,32,256]{2,1,0:T(8,128)} %broadcast_multiply_fusion), calls=%async_computation | async-start | bytes 1048576 | tf_op jit(solution)/shard_map/all_to_all | solution.py:215
  13.1 7.6 %collective-permute-start.1 = (f32[10,32,256]{2,1,0:T(8,128)S(1)}, f32[10,32,256]{2,1,0:T(8,128)S(1)}, u32[]{:S(2)}, u32[]{:S(2)}) collective-permute-start(f32[10,32,256]{2,1,0:T(8,128)S(1)} %pad_maximum_fusion), channel_id=1, source_target_pairs={{0,1},{1,2},{2,3},{3,4},{4,5},{5,6},{6,7},{7,8},{8,9},{9,10},{10,1... | collective-permute-start | bytes 983048 | tf_op jit(solution)/shard_map/ppermute | solution.py:25
  16.3 1.3 %copy-start.4 = (f32[16,3]{0,1:T(4,128)S(1)}, f32[16,3]{0,1:T(4,128)}, u32[]{:S(2)}) copy-start(f32[16,3]{0,1:T(4,128)} %param.23) | copy-start | bytes 580
  16.4 4.4 %collective-permute-start = (f32[4,32,256]{2,1,0:T(8,128)S(1)}, f32[4,32,256]{2,1,0:T(8,128)S(1)}, u32[]{:S(2)}, u32[]{:S(2)}) collective-permute-start(f32[4,32,256]{2,1,0:T(8,128)S(1)} %pad_maximum_fusion.1), channel_id=1, source_target_pairs={{1,0},{2,1},{3,2},{4,3},{5,4},{6,5},{7,6},{8,7},{9,8},{10,9},{11,1... | collective-permute-start | bytes 393224 | tf_op jit(solution)/shard_map/ppermute | solution.py:25
  20.7 5.0 %copy-start.3 = (f32[4,32,256]{2,1,0:T(8,128)}, f32[4,32,256]{2,1,0:T(8,128)S(1)}, u32[]{:S(2)}) copy-start(f32[4,32,256]{2,1,0:T(8,128)S(1)} %collective-permute-done.upper) | copy-start | bytes 393220
  20.7 5.0 %copy-start.2 = (f32[10,32,256]{2,1,0:T(8,128)}, f32[10,32,256]{2,1,0:T(8,128)S(1)}, u32[]{:S(2)}) copy-start(f32[10,32,256]{2,1,0:T(8,128)S(1)} %collective-permute-done.1.below) | copy-start | bytes 983044
  25.7 0.8 %copy-start.1 = (f32[16,32,256]{2,1,0:T(8,128)}, f32[16,32,256]{2,1,0:T(8,128)S(1)}, u32[]{:S(2)}) copy-start(f32[16,32,256]{2,1,0:T(8,128)S(1)} %all-to-all-done.arrived) | copy-start | bytes 1572868

commit v7 on v3

--- a/solution.py
+++ b/solution.py
@@ -16,6 +16,7 @@
 HIGH = lax.Precision.HIGHEST
 KEEP = 1.0 - DAMPING * DT / 2.0
 LOSS = 1.0 + DAMPING * DT / 2.0
+SHRINK = 1.0 / LOSS
 
 
 def passed_along(block, axis, distance):
@@ -94,7 +95,7 @@
             hy - behind_x(hy) - (hx - behind_y(hx)),
         )
         for c in range(3):
-            j_next = (KEEP * j[c, z] + DT * (strength * e[c, z] - p[c, z])) / LOSS
+            j_next = (KEEP * j[c, z] + DT * (strength * e[c, z] - p[c, z])) * SHRINK
             out[c, z] = e[c, z] + step * (curl[c] - j_next)
 
     runs = ((ef, hf, pf, jf, hf_o, ef_o, 0), (ea, ha, pa, ja, ha_o, ea_o, 2))
@@ -208,9 +209,7 @@
         1,
     )
     owned = smooth(wx, wy, design)
-    holder = (start + index) // depth
-    target = (jnp.arange(count, dtype=jnp.int32) == holder).astype(jnp.float32)
-    slots = target[:, None, None] * owned
+    slots = jnp.broadcast_to(owned, (count,) + owned.shape[1:])
     arrived = lax.all_to_all(slots, "gx", split_axis=0, concat_axis=0, tiled=True)
     ef, hf, ea, ha, returned = fields(
         e_forward, h_forward, p_forward, j_forward, e_adjoint, h_adjoint, p_adjoint, j_adjoint,

time: 57.3 us -> 56.5 us (0.986)
  other arithmetic: 1.96 us -> 1.06 us
  local copies, waits for them, and re-layouts: 3.28 us -> 4.12 us
  waiting for transfers between devices: 9.01 us -> 8.36 us
    mul x1 -> x0, other arithmetic: 0.9 us -> none  [body(): slots = target[:, None, None] * owned]
    broadcast_in_dim x0 -> x1, local copies, waits for them, and re-layouts: none -> 0.84 us  [body(): slots = jnp.broadcast_to(owned, (count,) + owned.shape[1:])]
    ppermute x2, waiting for transfers between devices: 2.97 us -> 2.3 us  [passed_along(): return lax.ppermute(block, axis, route)]
where the time goes in v7:
time: 56.5 us; the launch traced here: 56 us
  blocking collectives  21.4 us (38%)
  starting transfers between devices  11.1 us (20%)
  waiting for transfers between devices  8.36 us (15%)
  Pallas kernels  5.94 us (11%)
  local copies, waits for them, and re-layouts  4.12 us (7%)
  between operations  2.1 us (4%)
  matrix products  1.88 us (3%)
  other arithmetic  1.06 us (2%)
    all_to_all x1, blocking collectives, body(): lax.all_to_all(returned, 'gx', split_axis=0, concat_axis=0, tiled=True)  21.4 us
    all_to_all x1, starting transfers between devices, body(): lax.all_to_all(slots, 'gx', split_axis=0, concat_axis=0, tiled=True)  7.52 us
    all_to_all x1, waiting for transfers between devices, body(): lax.all_to_all(slots, 'gx', split_axis=0, concat_axis=0, tiled=True)  6.07 us
    pallas_call x1, Pallas kernels, fields(): pl.pallas_call(field_kernel, out_shape=(field, field, field, field, jax.S...  5.94 us
    ppermute x2, starting transfers between devices, passed_along(): return lax.ppermute(block, axis, route)  3.61 us
    unnamed x19, local copies, waits for them, and re-layouts  2.4 us
    ppermute x2, waiting for transfers between devices, passed_along(): return lax.ppermute(block, axis, route)  2.3 us
  transfers between devices with their start and end apart: 3, of which 2 were waited for; matrix products, arithmetic and copies ran while one was open for 3% of the time, Pallas kernels for 0%

profile of v7, /device:TPU:0, one launch (start us, length us, event | category | flops | bytes accessed | tf_op | source)
XLA Modules:
  0.0 56.0 jit_solution(12456813577747542836)
XLA Ops:
  0.6 0.0 copy-start
  1.3 0.1 convert_reduce_fusion.1
  1.4 0.2 convert_reduce_fusion
  1.6 0.2 fusion.7
  1.8 0.0 copy-start.3
  1.8 0.4 fusion
  2.3 0.0 copy-start.2
  2.3 0.8 %broadcast_in_dim.4 = f32[16,32,256]{2,1,0:T(8,128)} broadcast(f32[32,256]{1,0:T(8,128)S(1)} %fusion), dimensions={1,2} | broadcast | bytes 557056 | tf_op jit(solution)/shard_map/broadcast_in_dim | solution.py:212
  3.1 7.5 %all-to-all-start = ((f32[16,32,256]{2,1,0:T(8,128)}), f32[16,32,256]{2,1,0:T(8,128)S(1)}, u32[]{:S(2)}, u32[]{:S(2)}) async-start(f32[16,32,256]{2,1,0:T(8,128)} %broadcast_in_dim.4), calls=%async_computation | async-start | bytes 1048576 | tf_op jit(solution)/shard_map/all_to_all | solution.py:213
  10.6 0.9 %slice_bitcast_fusion.2 = (f32[2,32,256]{2,1,0:T(8,128)S(1)}, f32[2,32,256]{2,1,0:T(8,128)S(1)}) fusion(f32[3,8,32,256]{3,2,1,0:T(8,128)} %ha.1, f32[3,8,32,256]{3,2,1,0:T(8,128)S(1)} %copy-done.3), kind=kLoop, calls=%fused_computation.15 | loop fusion | bytes 262144 | tf_op jit(solution)/shard_map/squeeze | solution.py:206
  11.6 0.7 %pad_maximum_fusion = f32[10,32,256]{2,1,0:T(8,128)} fusion(f32[3,32,256]{2,1,0:T(8,128)S(1)} %get-tuple-element.17, f32[2,32,256]{2,1,0:T(8,128)S(1)} %get-tuple-element.19, f32[3,32,256]{2,1,0:T(8,128)S(1)} %get-tuple-element.18, f32[2,32,256]{2,1,0:T(8,128)S(1)} %get-tuple-element.20), kind=kLoop, calls=%fused_computation.1 | loop fusion | flops 245760 | bytes 655360 | tf_op jit(solution)/shard_map/concatenate | solution.py:205
  12.3 2.3 %collective-permute-start.1 = (f32[10,32,256]{2,1,0:T(8,128)}, f32[10,32,256]{2,1,0:T(8,128)S(1)}, u32[]{:S(2)}, u32[]{:S(2)}) collective-permute-start(f32[10,32,256]{2,1,0:T(8,128)} %pad_maximum_fusion), channel_id=1, source_target_pairs={{0,1},{1,2},{2,3},{3,4},{4,5},{5,6},{6,7},{7,8},{8,9},{9,10},{10,1... | collective-permute-start | bytes 983048 | tf_op jit(solution)/shard_map/ppermute | solution.py:25
  14.6 0.0 copy-start.8
  14.7 1.3 %collective-permute-start = (f32[4,32,256]{2,1,0:T(8,128)S(1)}, f32[4,32,256]{2,1,0:T(8,128)S(1)}, u32[]{:S(2)}, u32[]{:S(2)}) collective-permute-start(f32[4,32,256]{2,1,0:T(8,128)S(1)} %pad_maximum_fusion.1), channel_id=1, source_target_pairs={{1,0},{2,1},{3,2},{4,3},{5,4},{6,5},{7,6},{8,7},{9,8},{10,9},{11,1... | collective-permute-start | bytes 393224 | tf_op jit(solution)/shard_map/ppermute | solution.py:25
  16.6 0.0 copy-start.7
  16.7 0.1 copy.32.amp
  16.7 2.3 %collective-permute-done.upper = f32[4,32,256]{2,1,0:T(8,128)S(1)} collective-permute-done((f32[4,32,256]{2,1,0:T(8,128)S(1)}, f32[4,32,256]{2,1,0:T(8,128)S(1)}, u32[]{:S(2)}, u32[]{:S(2)}) %collective-permute-start) | collective-permute-done | bytes 131104 | tf_op jit(solution)/shard_map/ppermute | solution.py:25
  19.0 6.1 %all-to-all-done.arrived = f32[16,32,256]{2,1,0:T(8,128)S(1)} async-done(((f32[16,32,256]{2,1,0:T(8,128)}), f32[16,32,256]{2,1,0:T(8,128)S(1)}, u32[]{:S(2)}, u32[]{:S(2)}) %all-to-all-start) | async-done | bytes 524320 | tf_op jit(solution)/shard_map/all_to_all | solution.py:213
  25.1 1.1 %copy-done.4 = f32[3,8,32,256]{3,2,1,0:T(8,128)S(1)} copy-done((f32[3,8,32,256]{3,2,1,0:T(8,128)S(1)}, f32[3,8,32,256]{3,2,1,0:T(8,128)}, u32[]{:S(2)}) %copy-start.4) | copy-done | bytes 786456
  26.2 1.1 %copy-done.5 = f32[3,8,32,256]{3,2,1,0:T(8,128)S(1)} copy-done((f32[3,8,32,256]{3,2,1,0:T(8,128)S(1)}, f32[3,8,32,256]{3,2,1,0:T(8,128)}, u32[]{:S(2)}) %copy-start.5) | copy-done | bytes 786456
  27.4 5.9 %shard_map.173 = (f32[3,8,32,256]{3,2,1,0:T(8,128)}, f32[3,8,32,256]{3,2,1,0:T(8,128)}, f32[3,8,32,256]{3,2,1,0:T(8,128)}, f32[3,8,32,256]{3,2,1,0:T(8,128)}, f32[16,32,256]{2,1,0:T(8,128)S(1)}) custom-call(f32[3,8,32,256]{3,2,1,0:T(8,128)S(1)} %copy-done.1, f32[3,8,32,256]{3,2,1,0:T(8,128)S(1)} %copy-done.3, f32[3,8,32,256]{3,2,1,0:T(8,128)S(1)} %copy-done.4, ...), custom_call_target="tpu_custom_call" | custom-call | flops 13107200 | bytes 10485760 | tf_op jit(solution)/shard_map/pallas_call | solution.py:167
  33.3 21.4 %all_to_all.10 = f32[16,32,256]{2,1,0:T(8,128)S(1)} all-to-all(f32[16,32,256]{2,1,0:T(8,128)S(1)} %get-tuple-element.14), channel_id=1, replica_groups=mesh['grp'=2,'gx'=16] {'gx'}, dimensions={0} | all-to-all | bytes 1048576 | tf_op jit(solution)/shard_map/all_to_all | solution.py:218
  54.8 0.3 fusion.9
  55.1 0.9 %convolution_bitcast_fusion = f32[1,32,256]{2,1,0:T(8,128)} fusion(f32[32,256]{1,0:T(8,128)S(1)} %fusion.9, f32[256]{0:T(256)S(1)} %convert_reduce_fusion, s32[]{:T(128)} %bitcast), kind=kOutput, calls=%fused_computation | convolution fusion | flops 25559040 | bytes 66564 | tf_op jit(solution)/shard_map/xb,by->xy/dot_general | solution.py:220
  (16 shorter events, 0.1 us)
Async XLA Ops:
  0.6 0.9 %copy-start = (f32[1,32,256]{2,1,0:T(8,128)S(1)}, f32[1,32,256]{2,1,0:T(8,128)}, u32[]{:S(2)}) copy-start(f32[1,32,256]{2,1,0:T(8,128)} %param.22) | copy-start | bytes 98308
  1.8 8.8 %copy-start.3 = (f32[3,8,32,256]{3,2,1,0:T(8,128)S(1)}, f32[3,8,32,256]{3,2,1,0:T(8,128)}, u32[]{:S(2)}) copy-start(f32[3,8,32,256]{3,2,1,0:T(8,128)} %hf.1) | copy-start | bytes 2359300
  2.3 9.3 %copy-start.2 = (f32[3,8,32,256]{3,2,1,0:T(8,128)S(1)}, f32[3,8,32,256]{3,2,1,0:T(8,128)}, u32[]{:S(2)}) copy-start(f32[3,8,32,256]{3,2,1,0:T(8,128)} %ea.1) | copy-start | bytes 2359300
  3.1 8.4 %copy-start.1 = (f32[3,8,32,256]{3,2,1,0:T(8,128)S(1)}, f32[3,8,32,256]{3,2,1,0:T(8,128)}, u32[]{:S(2)}) copy-start(f32[3,8,32,256]{3,2,1,0:T(8,128)} %ef.1) | copy-start | bytes 2359300
  3.1 22.0 %all-to-all-start = ((f32[16,32,256]{2,1,0:T(8,128)}), f32[16,32,256]{2,1,0:T(8,128)S(1)}, u32[]{:S(2)}, u32[]{:S(2)}) async-start(f32[16,32,256]{2,1,0:T(8,128)} %broadcast_in_dim.4), calls=%async_computation | async-start | bytes 1048576 | tf_op jit(solution)/shard_map/all_to_all | solution.py:213
  12.3 6.7 %collective-permute-start.1 = (f32[10,32,256]{2,1,0:T(8,128)}, f32[10,32,256]{2,1,0:T(8,128)S(1)}, u32[]{:S(2)}, u32[]{:S(2)}) collective-permute-start(f32[10,32,256]{2,1,0:T(8,128)} %pad_maximum_fusion), channel_id=1, source_target_pairs={{0,1},{1,2},{2,3},{3,4},{4,5},{5,6},{6,7},{7,8},{8,9},{9,10},{10,1... | collective-permute-start | bytes 983048 | tf_op jit(solution)/shard_map/ppermute | solution.py:25
  14.6 2.0 %copy-start.8 = (f32[16,3]{0,1:T(4,128)S(1)}, f32[16,3]{0,1:T(4,128)}, u32[]{:S(2)}) copy-start(f32[16,3]{0,1:T(4,128)} %param.23) | copy-start | bytes 580
  14.7 4.4 %collective-permute-start = (f32[4,32,256]{2,1,0:T(8,128)S(1)}, f32[4,32,256]{2,1,0:T(8,128)S(1)}, u32[]{:S(2)}, u32[]{:S(2)}) collective-permute-start(f32[4,32,256]{2,1,0:T(8,128)S(1)} %pad_maximum_fusion.1), channel_id=1, source_target_pairs={{1,0},{2,1},{3,2},{4,3},{5,4},{6,5},{7,6},{8,7},{9,8},{10,9},{11,1... | collective-permute-start | bytes 393224 | tf_op jit(solution)/shard_map/ppermute | solution.py:25
  16.6 8.5 %copy-start.6 = (s32[16]{0:T(128)S(1)}, s32[16]{0:T(128)}, u32[]{:S(2)}) copy-start(s32[16]{0:T(128)} %src.1) | copy-start | bytes 196
  16.6 8.5 %copy-start.7 = (s32[16]{0:T(128)S(1)}, s32[16]{0:T(128)}, u32[]{:S(2)}) copy-start(s32[16]{0:T(128)} %mon.1) | copy-start | bytes 196
  25.1 1.1 %copy-start.4 = (f32[3,8,32,256]{3,2,1,0:T(8,128)S(1)}, f32[3,8,32,256]{3,2,1,0:T(8,128)}, u32[]{:S(2)}) copy-start(f32[3,8,32,256]{3,2,1,0:T(8,128)} %pf.1) | copy-start | bytes 2359300
  26.2 1.1 %copy-start.5 = (f32[3,8,32,256]{3,2,1,0:T(8,128)S(1)}, f32[3,8,32,256]{3,2,1,0:T(8,128)}, u32[]{:S(2)}) copy-start(f32[3,8,32,256]{3,2,1,0:T(8,128)} %jf.1) | copy-start | bytes 2359300

commit v8 on v7

--- a/solution.py
+++ b/solution.py
@@ -42,9 +42,49 @@
     return jnp.einsum("zxb,by->zxy", inner, wy, precision=HIGH)
 
 
-def field_kernel(
-    ef, hf, pf, jf, ea, ha, pa, ja, arrived, upper, below, src, mon, amp, first,
-    ef_o, hf_o, ea_o, ha_o, ret_o, rho,
+def shifts(width_x, width_y):
+    row = lax.broadcasted_iota(jnp.int32, (width_x, width_y), 0)
+    lane = lax.broadcasted_iota(jnp.int32, (width_x, width_y), 1)
+
+    def ahead_y(f):
+        return jnp.where(lane == width_y - 1, 0.0, pltpu.roll(f, width_y - 1, 1))
+
+    def ahead_x(f):
+        return jnp.where(row == width_x - 1, 0.0, pltpu.roll(f, width_x - 1, 0))
+
+    def behind_y(f):
+        return jnp.where(lane == 0, 0.0, pltpu.roll(f, 1, 1))
+
+    def behind_x(f):
+        return jnp.where(row == 0, 0.0, pltpu.roll(f, 1, 0))
+
+    return ahead_y, ahead_x, behind_y, behind_x
+
+
+def h_kernel(ef, hf, ea, ha, upper, below, hf_o, ha_o, lower):
+    _, depth, width_x, width_y = ef.shape
+    ahead_y, ahead_x, _, _ = shifts(width_x, width_y)
+    keep = lax.axis_index("gx") > 0
+    for r, (e, h, h_out) in enumerate(((ef, hf, hf_o), (ea, ha, ha_o))):
+        hx, hy, ex, ey, ez = (below[5 * r + i] for i in range(5))
+        curl_x = ahead_y(ez) - ez - (e[1, 0] - ey)
+        curl_y = e[0, 0] - ex - (ahead_x(ez) - ez)
+        lower[2 * r] = jnp.where(keep, hx - DT * curl_x, 0.0)
+        lower[2 * r + 1] = jnp.where(keep, hy - DT * curl_y, 0.0)
+        for z in range(depth):
+            if z + 1 < depth:
+                ex_up, ey_up = e[0, z + 1], e[1, z + 1]
+            else:
+                ex_up, ey_up = upper[2 * r], upper[2 * r + 1]
+            ex, ey, ez = e[0, z], e[1, z], e[2, z]
+            h_out[0, z] = h[0, z] - DT * (ahead_y(ez) - ez - (ey_up - ey))
+            h_out[1, z] = h[1, z] - DT * (ex_up - ex - (ahead_x(ez) - ez))
+            h_out[2, z] = h[2, z] - DT * (ahead_x(ey) - ey - (ahead_y(ex) - ex))
+
+
+def e_kernel(
+    ef, pf, jf, ea, pa, ja, hfn, han, lower, arrived, src, mon, amp, first,
+    ef_o, ea_o, ret_o, rho,
 ):
     depth, width_x, width_y = rho.shape
     slab = arrived.shape[0]
@@ -54,66 +94,27 @@
         p = index * depth + z - start
         inside = (p >= 0) & (p < slab)
         rho[z] = jnp.where(inside, arrived[jnp.clip(p, 0, slab - 1)], 0.0)
-    row = lax.broadcasted_iota(jnp.int32, (width_x, width_y), 0)
-    lane = lax.broadcasted_iota(jnp.int32, (width_x, width_y), 1)
-
-    def ahead_y(f):
-        return jnp.where(lane == width_y - 1, 0.0, pltpu.roll(f, width_y - 1, 1))
-
-    def ahead_x(f):
-        return jnp.where(row == width_x - 1, 0.0, pltpu.roll(f, width_x - 1, 0))
-
-    def behind_y(f):
-        return jnp.where(lane == 0, 0.0, pltpu.roll(f, 1, 1))
-
-    def behind_x(f):
-        return jnp.where(row == 0, 0.0, pltpu.roll(f, 1, 0))
-
-    def new_h(e, h, z, ex_up, ey_up):
-        ex, ey, ez = e[0, z], e[1, z], e[2, z]
-        curl_x = ahead_y(ez) - ez - (ey_up - ey)
-        curl_y = ex_up - ex - (ahead_x(ez) - ez)
-        curl_z = ahead_x(ey) - ey - (ahead_y(ex) - ex)
-        return (h[0, z] - DT * curl_x, h[1, z] - DT * curl_y, h[2, z] - DT * curl_z)
-
-    def lower_h(e, base):
-        hx, hy, ex, ey, ez = (below[base + i] for i in range(5))
-        curl_x = ahead_y(ez) - ez - (e[1, 0] - ey)
-        curl_y = e[0, 0] - ex - (ahead_x(ez) - ez)
-        keep = index > 0
-        return (
-            jnp.where(keep, hx - DT * curl_x, 0.0),
-            jnp.where(keep, hy - DT * curl_y, 0.0),
-        )
-
-    def new_e(e, p, j, out, z, hn, hn_dn, step, strength):
-        hx, hy, hz = hn
-        hx_dn, hy_dn = hn_dn
-        curl = (
-            hz - behind_y(hz) - (hy - hy_dn),
-            hx - hx_dn - (hz - behind_x(hz)),
-            hy - behind_x(hy) - (hx - behind_y(hx)),
-        )
-        for c in range(3):
-            j_next = (KEEP * j[c, z] + DT * (strength * e[c, z] - p[c, z])) * SHRINK
-            out[c, z] = e[c, z] + step * (curl[c] - j_next)
-
-    runs = ((ef, hf, pf, jf, hf_o, ef_o, 0), (ea, ha, pa, ja, ha_o, ea_o, 2))
-    prev = [lower_h(ef, 0), lower_h(ea, 5)]
+    _, _, behind_y, behind_x = shifts(width_x, width_y)
+
+    runs = ((ef, pf, jf, hfn, ef_o), (ea, pa, ja, han, ea_o))
     for z in range(depth):
         density = rho[z]
         step = DT / (1.0 + EPS_RANGE * density)
         strength = STRENGTH_BASE + STRENGTH_RANGE * density
-        for r, (e, h, p, j, h_out, e_out, up) in enumerate(runs):
-            if z + 1 < depth:
-                ex_up, ey_up = e[0, z + 1], e[1, z + 1]
+        for r, (e, p, j, hn, e_out) in enumerate(runs):
+            hx, hy, hz = hn[0, z], hn[1, z], hn[2, z]
+            if z > 0:
+                hx_dn, hy_dn = hn[0, z - 1], hn[1, z - 1]
             else:
-                ex_up, ey_up = upper[up], upper[up + 1]
-            hn = new_h(e, h, z, ex_up, ey_up)
+                hx_dn, hy_dn = lower[2 * r], lower[2 * r + 1]
+            curl = (
+                hz - behind_y(hz) - (hy - hy_dn),
+                hx - hx_dn - (hz - behind_x(hz)),
+                hy - behind_x(hy) - (hx - behind_y(hx)),
+            )
             for c in range(3):
-                h_out[c, z] = hn[c]
-            new_e(e, p, j, e_out, z, hn, prev[r], step, strength)
-            prev[r] = (hn[0], hn[1])
+                j_next = (KEEP * j[c, z] + DT * (strength * e[c, z] - p[c, z])) * SHRINK
+                e_out[c, z] = e[c, z] + step * (curl[c] - j_next)
 
     plane = width_x * width_y
     tile_row = lax.broadcasted_iota(jnp.int32, (8, width_y), 0)
@@ -131,10 +132,10 @@
         def _():
             rows = pl.ds(x0, 8)
             hit = (tile_row == x - x0) & (tile_lane == y)
-            step = DT / (1.0 + EPS_RANGE * rho[local, rows, :])
+            gain = DT / (1.0 + EPS_RANGE * rho[local, rows, :])
             for c in range(3):
                 held = out[c, local, rows, :]
-                out[c, local, rows, :] = held + jnp.where(hit, step * value_of(c, local, rows), 0.0)
+                out[c, local, rows, :] = held + jnp.where(hit, gain * value_of(c, local, rows), 0.0)
 
     for s in range(src.shape[0]):
         add_at(src[s], ef_o, lambda c, local, rows, s=s: amp[s, c])
@@ -159,23 +160,33 @@
 def fields(e_forward, h_forward, p_forward, j_forward, e_adjoint, h_adjoint, p_adjoint, j_adjoint,
            arrived, upper, below, source_cell, monitor_cell, source_amp, slab_start):
     shape = e_forward.shape
-    depth = shape[1]
     field = jax.ShapeDtypeStruct(shape, jnp.float32)
     vmem = pl.BlockSpec(memory_space=pltpu.VMEM)
     smem = pl.BlockSpec(memory_space=pltpu.SMEM)
     cells = shape[1] * shape[2] * shape[3]
-    return pl.pallas_call(
-        field_kernel,
-        out_shape=(field, field, field, field, jax.ShapeDtypeStruct(arrived.shape, jnp.float32)),
-        in_specs=[vmem] * 11 + [smem] * 4,
-        out_specs=(vmem,) * 5,
+    hf, ha, lower = pl.pallas_call(
+        h_kernel,
+        out_shape=(field, field, jax.ShapeDtypeStruct((4,) + shape[2:], jnp.float32)),
+        in_specs=[vmem] * 6,
+        out_specs=(vmem,) * 3,
+        compiler_params=pltpu.CompilerParams(vmem_limit_bytes=12 * 1024 * 1024),
+        cost_estimate=pl.CostEstimate(
+            flops=60 * cells, bytes_accessed=4 * cells * 18, transcendentals=0
+        ),
+    )(e_forward, h_forward, e_adjoint, h_adjoint, upper, below)
+    ef, ea, returned = pl.pallas_call(
+        e_kernel,
+        out_shape=(field, field, jax.ShapeDtypeStruct(arrived.shape, jnp.float32)),
+        in_specs=[vmem] * 10 + [smem] * 4,
+        out_specs=(vmem,) * 3,
         scratch_shapes=[pltpu.VMEM(shape[1:], jnp.float32)],
-        compiler_params=pltpu.CompilerParams(vmem_limit_bytes=48 * 1024 * 1024),
+        compiler_params=pltpu.CompilerParams(vmem_limit_bytes=56 * 1024 * 1024),
         cost_estimate=pl.CostEstimate(
-            flops=200 * cells, bytes_accessed=4 * cells * 40, transcendentals=0
-        ),
-    )(e_forward, h_forward, p_forward, j_forward, e_adjoint, h_adjoint, p_adjoint, j_adjoint,
-      arrived, upper, below, source_cell, monitor_cell, source_amp, slab_start)
+            flops=140 * cells, bytes_accessed=4 * cells * 30, transcendentals=0
+        ),
+    )(e_forward, p_forward, j_forward, e_adjoint, p_adjoint, j_adjoint, hf, ha, lower, arrived,
+      source_cell, monitor_cell, source_amp, slab_start)
+    return ef, hf, ea, ha, returned
 
 
 def body(

time: 56.5 us -> 57.6 us (1.019)
  waiting for transfers between devices: 8.36 us -> 4.26 us
  blocking collectives: 21.4 us -> 24.5 us
  Pallas kernels: 5.94 us -> 8.47 us
  local copies, waits for them, and re-layouts: 4.12 us -> 3.1 us
  other arithmetic: 1.06 us -> 1.72 us
    all_to_all x1, waiting for transfers between devices: 6.07 us -> 2.19 us  [body(): lax.all_to_all(slots, 'gx', split_axis=0, concat_axis=0, tiled=True)]
    all_to_all x1, blocking collectives: 21.4 us -> 24.5 us  [body(): lax.all_to_all(returned, 'gx', split_axis=0, concat_axis=0, tiled=True)]
    pallas_call x1 -> x2, Pallas kernels: 5.94 us -> 8.47 us  [the longest x1 6.14 us: fields(): pl.pallas_call(e_kernel, out_shape=(field, field, jax.ShapeDtypeStruct(ar...]
    unnamed x19 -> x15, local copies, waits for them, and re-layouts: 2.4 us -> 1.37 us
    concatenate x1, other arithmetic: 0.01 us -> 0.67 us  [body(): jnp.concatenate([e_forward[0:2, 0], e_adjoint[0:2, 0]], 0)]
  transfers between devices with their start and end apart: 3 -> 3, of which waited for: 2 -> 2; matrix products, arithmetic and copies ran while one was open for 3% -> 5% of each run, Pallas kernels for 0% -> 4%
where the time goes in v8:
time: 57.6 us; the launch traced here: 57.1 us
  blocking collectives  24.5 us (43%)
  starting transfers between devices  11.1 us (19%)
  Pallas kernels  8.47 us (15%)
  waiting for transfers between devices  4.26 us (7%)
  local copies, waits for them, and re-layouts  3.1 us (5%)
  between operations  2.08 us (4%)
  matrix products  1.88 us (3%)
  other arithmetic  1.72 us (3%)
    all_to_all x1, blocking collectives, body(): lax.all_to_all(returned, 'gx', split_axis=0, concat_axis=0, tiled=True)  24.5 us
    all_to_all x1, starting transfers between devices, body(): lax.all_to_all(slots, 'gx', split_axis=0, concat_axis=0, tiled=True)  7.57 us
    pallas_call x1, Pallas kernels, fields(): pl.pallas_call(e_kernel, out_shape=(field, field, jax.ShapeDtypeStruct(ar...  6.14 us
    ppermute x2, starting transfers between devices, passed_along(): return lax.ppermute(block, axis, route)  3.55 us
    pallas_call x1, Pallas kernels, fields(): pl.pallas_call(h_kernel, out_shape=(field, field, jax.ShapeDtypeStruct((4...  2.33 us
    all_to_all x1, waiting for transfers between devices, body(): lax.all_to_all(slots, 'gx', split_axis=0, concat_axis=0, tiled=True)  2.19 us
    ppermute x2, waiting for transfers between devices, passed_along(): return lax.ppermute(block, axis, route)  2.07 us
    unnamed x15, local copies, waits for them, and re-layouts  1.37 us
  transfers between devices with their start and end apart: 3, of which 2 were waited for; matrix products, arithmetic and copies ran while one was open for 5% of the time, Pallas kernels for 4%

profile of v8, /device:TPU:0, one launch (start us, length us, event | category | flops | bytes accessed | tf_op | source)
XLA Modules:
  0.0 57.1 jit_solution(16534819959563625415)
XLA Ops:
  0.6 0.0 copy-start
  1.3 0.1 convert_reduce_fusion.1
  1.4 0.2 convert_reduce_fusion
  1.6 0.2 fusion.7
  1.8 0.0 copy-start.3
  1.8 0.4 fusion
  2.3 0.0 copy-start.2
  2.3 0.8 %broadcast_in_dim.4 = f32[16,32,256]{2,1,0:T(8,128)} broadcast(f32[32,256]{1,0:T(8,128)S(1)} %fusion), dimensions={1,2} | broadcast | bytes 557056 | tf_op jit(solution)/shard_map/broadcast_in_dim | solution.py:223
  3.1 7.6 %all-to-all-start = ((f32[16,32,256]{2,1,0:T(8,128)}), f32[16,32,256]{2,1,0:T(8,128)}, u32[]{:S(2)}, u32[]{:S(2)}) async-start(f32[16,32,256]{2,1,0:T(8,128)} %broadcast_in_dim.4), calls=%async_computation | async-start | bytes 1048576 | tf_op jit(solution)/shard_map/all_to_all | solution.py:224
  10.7 0.9 %slice_bitcast_fusion.2 = (f32[2,32,256]{2,1,0:T(8,128)S(1)}, f32[2,32,256]{2,1,0:T(8,128)S(1)}) fusion(f32[3,8,32,256]{3,2,1,0:T(8,128)} %ha.1, f32[3,8,32,256]{3,2,1,0:T(8,128)S(1)} %copy-done.3), kind=kLoop, calls=%fused_computation.15 | loop fusion | bytes 262144 | tf_op jit(solution)/shard_map/squeeze | solution.py:217
  11.6 0.0 copy-start.4
  11.6 0.7 %pad_maximum_fusion = f32[10,32,256]{2,1,0:T(8,128)} fusion(f32[3,32,256]{2,1,0:T(8,128)S(1)} %get-tuple-element.19, f32[2,32,256]{2,1,0:T(8,128)S(1)} %get-tuple-element.21, f32[3,32,256]{2,1,0:T(8,128)S(1)} %get-tuple-element.20, f32[2,32,256]{2,1,0:T(8,128)S(1)} %get-tuple-element.22), kind=kLoop, calls=%fused_computation.1 | loop fusion | flops 245760 | bytes 655360 | tf_op jit(solution)/shard_map/concatenate | solution.py:216
  12.4 2.3 %collective-permute-start.1 = (f32[10,32,256]{2,1,0:T(8,128)}, f32[10,32,256]{2,1,0:T(8,128)S(1)}, u32[]{:S(2)}, u32[]{:S(2)}) collective-permute-start(f32[10,32,256]{2,1,0:T(8,128)} %pad_maximum_fusion), channel_id=1, source_target_pairs={{0,1},{1,2},{2,3},{3,4},{4,5},{5,6},{6,7},{7,8},{8,9},{9,10},{10,1... | collective-permute-start | bytes 983048 | tf_op jit(solution)/shard_map/ppermute | solution.py:25
  14.7 0.7 %pad_maximum_fusion.1 = f32[4,32,256]{2,1,0:T(8,128)} fusion(f32[2,32,256]{2,1,0:T(8,128)S(1)} %get-tuple-element.17, f32[2,32,256]{2,1,0:T(8,128)S(1)} %get-tuple-element.18), kind=kLoop, calls=%fused_computation.6 | loop fusion | flops 32768 | bytes 262144 | tf_op jit(solution)/shard_map/concatenate | solution.py:214
  15.3 1.3 %collective-permute-start = (f32[4,32,256]{2,1,0:T(8,128)}, f32[4,32,256]{2,1,0:T(8,128)}, u32[]{:S(2)}, u32[]{:S(2)}) collective-permute-start(f32[4,32,256]{2,1,0:T(8,128)} %pad_maximum_fusion.1), channel_id=1, source_target_pairs={{1,0},{2,1},{3,2},{4,3},{5,4},{6,5},{7,6},{8,7},{9,8},{10,9},{11,1... | collective-permute-start | bytes 393224 | tf_op jit(solution)/shard_map/ppermute | solution.py:25
  17.3 0.7 %copy.32.amp = f32[16,3]{1,0:T(8,128)} copy(f32[16,3]{0,1:T(4,128)S(1)} %copy-done.6) | data formatting | bytes 384 | tf_op args[9]
  18.0 2.1 %collective-permute-done.upper = f32[4,32,256]{2,1,0:T(8,128)} collective-permute-done((f32[4,32,256]{2,1,0:T(8,128)}, f32[4,32,256]{2,1,0:T(8,128)}, u32[]{:S(2)}, u32[]{:S(2)}) %collective-permute-start) | collective-permute-done | bytes 131104 | tf_op jit(solution)/shard_map/ppermute | solution.py:25
  20.0 2.3 %shard_map.173 = (f32[3,8,32,256]{3,2,1,0:T(8,128)}, f32[3,8,32,256]{3,2,1,0:T(8,128)}, f32[4,32,256]{2,1,0:T(8,128)S(1)}) custom-call(f32[3,8,32,256]{3,2,1,0:T(8,128)S(1)} %copy-done.1, f32[3,8,32,256]{3,2,1,0:T(8,128)S(1)} %copy-done.3, f32[3,8,32,256]{3,2,1,0:T(8,128)S(1)} %copy-done.2, f32[3,8,32,256]{3,2,1,0:T(8,128)S(1)} %copy-done.4, ...), custom_call_target="tpu_custom_call" | custom-call | flops 3932160 | bytes 4718592 | tf_op jit(solution)/shard_map/pallas_call | solution.py:167
  22.4 0.7 %copy-done.5 = f32[4,32,256]{2,1,0:T(8,128)} copy-done((f32[4,32,256]{2,1,0:T(8,128)}, f32[4,32,256]{2,1,0:T(8,128)S(1)}, u32[]{:S(2)}) %copy-start.5) | copy-done | bytes 131096
  23.0 2.2 %all-to-all-done.arrived = f32[16,32,256]{2,1,0:T(8,128)} async-done(((f32[16,32,256]{2,1,0:T(8,128)}), f32[16,32,256]{2,1,0:T(8,128)}, u32[]{:S(2)}, u32[]{:S(2)}) %all-to-all-start) | async-done | bytes 524320 | tf_op jit(solution)/shard_map/all_to_all | solution.py:224
  25.2 6.1 %shard_map.174 = (f32[3,8,32,256]{3,2,1,0:T(8,128)}, f32[3,8,32,256]{3,2,1,0:T(8,128)}, f32[16,32,256]{2,1,0:T(8,128)}) custom-call(f32[3,8,32,256]{3,2,1,0:T(8,128)} %ef.3, f32[3,8,32,256]{3,2,1,0:T(8,128)} %pf.1, f32[3,8,32,256]{3,2,1,0:T(8,128)} %jf.1, f32[3,8,32,256]{3,2,1,0:T(8,128)} %ea.3, f32[3,8,32,256]{3,2,1,0:T(8,128)} %pa.1, ...), custom_call_target="tpu_custom_call" | custom-call | flops 9175040 | bytes 7864320 | tf_op jit(solution)/shard_map/pallas_call | solution.py:177
  31.4 24.5 %all_to_all.10 = f32[16,32,256]{2,1,0:T(8,128)S(1)} all-to-all(f32[16,32,256]{2,1,0:T(8,128)} %get-tuple-element.16), channel_id=1, replica_groups=mesh['grp'=2,'gx'=16] {'gx'}, dimensions={0} | all-to-all | bytes 1048576 | tf_op jit(solution)/shard_map/all_to_all | solution.py:229
  55.8 0.3 fusion.9
  56.1 0.9 %convolution_bitcast_fusion = f32[1,32,256]{2,1,0:T(8,128)} fusion(f32[32,256]{1,0:T(8,128)S(1)} %fusion.9, f32[256]{0:T(256)S(1)} %convert_reduce_fusion, s32[]{:T(128)} %bitcast.6), kind=kOutput, calls=%fused_computation | convolution fusion | flops 25559040 | bytes 66564 | tf_op jit(solution)/shard_map/xb,by->xy/dot_general | solution.py:231
  (13 shorter events, 0.1 us)
Async XLA Ops:
  0.6 0.9 %copy-start = (f32[1,32,256]{2,1,0:T(8,128)S(1)}, f32[1,32,256]{2,1,0:T(8,128)}, u32[]{:S(2)}) copy-start(f32[1,32,256]{2,1,0:T(8,128)} %param.22) | copy-start | bytes 98308
  1.8 8.9 %copy-start.3 = (f32[3,8,32,256]{3,2,1,0:T(8,128)S(1)}, f32[3,8,32,256]{3,2,1,0:T(8,128)}, u32[]{:S(2)}) copy-start(f32[3,8,32,256]{3,2,1,0:T(8,128)} %hf.1) | copy-start | bytes 2359300
  2.3 9.3 %copy-start.2 = (f32[3,8,32,256]{3,2,1,0:T(8,128)S(1)}, f32[3,8,32,256]{3,2,1,0:T(8,128)}, u32[]{:S(2)}) copy-start(f32[3,8,32,256]{3,2,1,0:T(8,128)} %ea.3) | copy-start | bytes 2359300
  3.1 8.5 %copy-start.1 = (f32[3,8,32,256]{3,2,1,0:T(8,128)S(1)}, f32[3,8,32,256]{3,2,1,0:T(8,128)}, u32[]{:S(2)}) copy-start(f32[3,8,32,256]{3,2,1,0:T(8,128)} %ef.3) | copy-start | bytes 2359300
  3.1 22.1 %all-to-all-start = ((f32[16,32,256]{2,1,0:T(8,128)}), f32[16,32,256]{2,1,0:T(8,128)}, u32[]{:S(2)}, u32[]{:S(2)}) async-start(f32[16,32,256]{2,1,0:T(8,128)} %broadcast_in_dim.4), calls=%async_computation | async-start | bytes 1048576 | tf_op jit(solution)/shard_map/all_to_all | solution.py:224
  11.6 8.5 %copy-start.4 = (f32[3,8,32,256]{3,2,1,0:T(8,128)S(1)}, f32[3,8,32,256]{3,2,1,0:T(8,128)}, u32[]{:S(2)}) copy-start(f32[3,8,32,256]{3,2,1,0:T(8,128)} %ha.1) | copy-start | bytes 2359300
  12.4 7.7 %collective-permute-start.1 = (f32[10,32,256]{2,1,0:T(8,128)}, f32[10,32,256]{2,1,0:T(8,128)S(1)}, u32[]{:S(2)}, u32[]{:S(2)}) collective-permute-start(f32[10,32,256]{2,1,0:T(8,128)} %pad_maximum_fusion), channel_id=1, source_target_pairs={{0,1},{1,2},{2,3},{3,4},{4,5},{5,6},{6,7},{7,8},{8,9},{9,10},{10,1... | collective-permute-start | bytes 983048 | tf_op jit(solution)/shard_map/ppermute | solution.py:25
  14.7 2.6 %copy-start.6 = (f32[16,3]{0,1:T(4,128)S(1)}, f32[16,3]{0,1:T(4,128)}, u32[]{:S(2)}) copy-start(f32[16,3]{0,1:T(4,128)} %param.23) | copy-start | bytes 580
  15.3 4.7 %collective-permute-start = (f32[4,32,256]{2,1,0:T(8,128)}, f32[4,32,256]{2,1,0:T(8,128)}, u32[]{:S(2)}, u32[]{:S(2)}) collective-permute-start(f32[4,32,256]{2,1,0:T(8,128)} %pad_maximum_fusion.1), channel_id=1, source_target_pairs={{1,0},{2,1},{3,2},{4,3},{5,4},{6,5},{7,6},{8,7},{9,8},{10,9},{11,1... | collective-permute-start | bytes 393224 | tf_op jit(solution)/shard_map/ppermute | solution.py:25
  22.4 0.7 %copy-start.5 = (f32[4,32,256]{2,1,0:T(8,128)}, f32[4,32,256]{2,1,0:T(8,128)S(1)}, u32[]{:S(2)}) copy-start(f32[4,32,256]{2,1,0:T(8,128)S(1)} %get-tuple-element.13.lower) | copy-start | bytes 393220

commit v9 on v8

--- a/solution.py
+++ b/solution.py
@@ -61,31 +61,40 @@
     return ahead_y, ahead_x, behind_y, behind_x
 
 
-def h_kernel(ef, hf, ea, ha, upper, below, hf_o, ha_o, lower):
+def h_kernel(ef, hf, pf, jf, ea, ha, pa, ja, upper, below, hf_o, ha_o, qf_o, qa_o):
     _, depth, width_x, width_y = ef.shape
-    ahead_y, ahead_x, _, _ = shifts(width_x, width_y)
+    ahead_y, ahead_x, behind_y, behind_x = shifts(width_x, width_y)
     keep = lax.axis_index("gx") > 0
-    for r, (e, h, h_out) in enumerate(((ef, hf, hf_o), (ea, ha, ha_o))):
+    runs = ((ef, hf, pf, jf, hf_o, qf_o), (ea, ha, pa, ja, ha_o, qa_o))
+    for r, (e, h, p, j, h_out, q_out) in enumerate(runs):
         hx, hy, ex, ey, ez = (below[5 * r + i] for i in range(5))
         curl_x = ahead_y(ez) - ez - (e[1, 0] - ey)
         curl_y = e[0, 0] - ex - (ahead_x(ez) - ez)
-        lower[2 * r] = jnp.where(keep, hx - DT * curl_x, 0.0)
-        lower[2 * r + 1] = jnp.where(keep, hy - DT * curl_y, 0.0)
+        hx_dn = jnp.where(keep, hx - DT * curl_x, 0.0)
+        hy_dn = jnp.where(keep, hy - DT * curl_y, 0.0)
         for z in range(depth):
             if z + 1 < depth:
                 ex_up, ey_up = e[0, z + 1], e[1, z + 1]
             else:
                 ex_up, ey_up = upper[2 * r], upper[2 * r + 1]
             ex, ey, ez = e[0, z], e[1, z], e[2, z]
-            h_out[0, z] = h[0, z] - DT * (ahead_y(ez) - ez - (ey_up - ey))
-            h_out[1, z] = h[1, z] - DT * (ex_up - ex - (ahead_x(ez) - ez))
-            h_out[2, z] = h[2, z] - DT * (ahead_x(ey) - ey - (ahead_y(ex) - ex))
-
-
-def e_kernel(
-    ef, pf, jf, ea, pa, ja, hfn, han, lower, arrived, src, mon, amp, first,
-    ef_o, ea_o, ret_o, rho,
-):
+            hx = h[0, z] - DT * (ahead_y(ez) - ez - (ey_up - ey))
+            hy = h[1, z] - DT * (ex_up - ex - (ahead_x(ez) - ez))
+            hz = h[2, z] - DT * (ahead_x(ey) - ey - (ahead_y(ex) - ex))
+            h_out[0, z] = hx
+            h_out[1, z] = hy
+            h_out[2, z] = hz
+            curl = (
+                hz - behind_y(hz) - (hy - hy_dn),
+                hx - hx_dn - (hz - behind_x(hz)),
+                hy - behind_x(hy) - (hx - behind_y(hx)),
+            )
+            for c in range(3):
+                q_out[c, z] = curl[c] - (KEEP * j[c, z] - DT * p[c, z]) * SHRINK
+            hx_dn, hy_dn = hx, hy
+
+
+def e_kernel(ef, qf, ea, qa, arrived, src, mon, amp, first, ef_o, ea_o, ret_o, rho):
     depth, width_x, width_y = rho.shape
     slab = arrived.shape[0]
     index = lax.axis_index("gx")
@@ -94,27 +103,14 @@
         p = index * depth + z - start
         inside = (p >= 0) & (p < slab)
         rho[z] = jnp.where(inside, arrived[jnp.clip(p, 0, slab - 1)], 0.0)
-    _, _, behind_y, behind_x = shifts(width_x, width_y)
-
-    runs = ((ef, pf, jf, hfn, ef_o), (ea, pa, ja, han, ea_o))
+
     for z in range(depth):
         density = rho[z]
         step = DT / (1.0 + EPS_RANGE * density)
         strength = STRENGTH_BASE + STRENGTH_RANGE * density
-        for r, (e, p, j, hn, e_out) in enumerate(runs):
-            hx, hy, hz = hn[0, z], hn[1, z], hn[2, z]
-            if z > 0:
-                hx_dn, hy_dn = hn[0, z - 1], hn[1, z - 1]
-            else:
-                hx_dn, hy_dn = lower[2 * r], lower[2 * r + 1]
-            curl = (
-                hz - behind_y(hz) - (hy - hy_dn),
-                hx - hx_dn - (hz - behind_x(hz)),
-                hy - behind_x(hy) - (hx - behind_y(hx)),
-            )
+        for e, q, e_out in ((ef, qf, ef_o), (ea, qa, ea_o)):
             for c in range(3):
-                j_next = (KEEP * j[c, z] + DT * (strength * e[c, z] - p[c, z])) * SHRINK
-                e_out[c, z] = e[c, z] + step * (curl[c] - j_next)
+                e_out[c, z] = e[c, z] + step * (q[c, z] - DT * SHRINK * (strength * e[c, z]))
 
     plane = width_x * width_y
     tile_row = lax.broadcasted_iota(jnp.int32, (8, width_y), 0)
@@ -164,28 +160,28 @@
     vmem = pl.BlockSpec(memory_space=pltpu.VMEM)
     smem = pl.BlockSpec(memory_space=pltpu.SMEM)
     cells = shape[1] * shape[2] * shape[3]
-    hf, ha, lower = pl.pallas_call(
+    hf, ha, qf, qa = pl.pallas_call(
         h_kernel,
-        out_shape=(field, field, jax.ShapeDtypeStruct((4,) + shape[2:], jnp.float32)),
-        in_specs=[vmem] * 6,
-        out_specs=(vmem,) * 3,
-        compiler_params=pltpu.CompilerParams(vmem_limit_bytes=12 * 1024 * 1024),
+        out_shape=(field,) * 4,
+        in_specs=[vmem] * 10,
+        out_specs=(vmem,) * 4,
+        compiler_params=pltpu.CompilerParams(vmem_limit_bytes=24 * 1024 * 1024),
         cost_estimate=pl.CostEstimate(
-            flops=60 * cells, bytes_accessed=4 * cells * 18, transcendentals=0
-        ),
-    )(e_forward, h_forward, e_adjoint, h_adjoint, upper, below)
+            flops=120 * cells, bytes_accessed=4 * cells * 36, transcendentals=0
+        ),
+    )(e_forward, h_forward, p_forward, j_forward, e_adjoint, h_adjoint, p_adjoint, j_adjoint,
+      upper, below)
     ef, ea, returned = pl.pallas_call(
         e_kernel,
         out_shape=(field, field, jax.ShapeDtypeStruct(arrived.shape, jnp.float32)),
-        in_specs=[vmem] * 10 + [smem] * 4,
+        in_specs=[vmem] * 5 + [smem] * 4,
         out_specs=(vmem,) * 3,
         scratch_shapes=[pltpu.VMEM(shape[1:], jnp.float32)],
         compiler_params=pltpu.CompilerParams(vmem_limit_bytes=56 * 1024 * 1024),
         cost_estimate=pl.CostEstimate(
-            flops=140 * cells, bytes_accessed=4 * cells * 30, transcendentals=0
-        ),
-    )(e_forward, p_forward, j_forward, e_adjoint, p_adjoint, j_adjoint, hf, ha, lower, arrived,
-      source_cell, monitor_cell, source_amp, slab_start)
+            flops=40 * cells, bytes_accessed=4 * cells * 20, transcendentals=0
+        ),
+    )(e_forward, qf, e_adjoint, qa, arrived, source_cell, monitor_cell, source_amp, slab_start)
     return ef, hf, ea, ha, returned
 
 

time: 57.6 us -> 63 us (1.094)
  local copies, waits for them, and re-layouts: 3.1 us -> 8.76 us
  blocking collectives: 24.5 us -> 26.7 us
  waiting for transfers between devices: 4.26 us -> 2.07 us
    unnamed x15 -> x25, local copies, waits for them, and re-layouts: 1.37 us -> 7.04 us
    all_to_all x1, blocking collectives: 24.5 us -> 26.7 us  [body(): lax.all_to_all(returned, 'gx', split_axis=0, concat_axis=0, tiled=True)]
    all_to_all x1, waiting for transfers between devices: 2.19 us -> 0.01 us  [body(): lax.all_to_all(slots, 'gx', split_axis=0, concat_axis=0, tiled=True)]
    pallas_call x1, Pallas kernels: 6.14 us -> 4.61 us  [fields(): pl.pallas_call(e_kernel, out_shape=(field, field, jax.ShapeDtypeStruct(ar...]
    pallas_call x1, Pallas kernels: 2.33 us -> 3.34 us  [fields(): pl.pallas_call(h_kernel, out_shape=(field,) * 4, in_specs=[vmem] * 10, ou...]
  transfers between devices with their start and end apart: 3 -> 3, of which waited for: 2 -> 1; matrix products, arithmetic and copies ran while one was open for 5% -> 5% of each run, Pallas kernels for 4% -> 5%
where the time goes in v9:
time: 63 us; the launch traced here: 62.3 us
  blocking collectives  26.7 us (42%)
  starting transfers between devices  11.1 us (18%)
  local copies, waits for them, and re-layouts  8.76 us (14%)
  Pallas kernels  7.95 us (13%)
  between operations  2.09 us (3%)
  waiting for transfers between devices  2.07 us (3%)
  matrix products  1.88 us (3%)
  other arithmetic  1.72 us (3%)
    all_to_all x1, blocking collectives, body(): lax.all_to_all(returned, 'gx', split_axis=0, concat_axis=0, tiled=True)  26.7 us
    all_to_all x1, starting transfers between devices, body(): lax.all_to_all(slots, 'gx', split_axis=0, concat_axis=0, tiled=True)  7.57 us
    unnamed x25, local copies, waits for them, and re-layouts  7.04 us
    pallas_call x1, Pallas kernels, fields(): pl.pallas_call(e_kernel, out_shape=(field, field, jax.ShapeDtypeStruct(ar...  4.61 us
    ppermute x2, starting transfers between devices, passed_along(): return lax.ppermute(block, axis, route)  3.55 us
    pallas_call x1, Pallas kernels, fields(): pl.pallas_call(h_kernel, out_shape=(field,) * 4, in_specs=[vmem] * 10, ou...  3.34 us
    ppermute x2, waiting for transfers between devices, passed_along(): return lax.ppermute(block, axis, route)  2.07 us
  transfers between devices with their start and end apart: 3, of which 1 were waited for; matrix products, arithmetic and copies ran while one was open for 5% of the time, Pallas kernels for 5%

profile of v9, /device:TPU:0, one launch (start us, length us, event | category | flops | bytes accessed | tf_op | source)
XLA Modules:
  0.0 62.3 jit_solution(10116489869702764895)
XLA Ops:
  1.3 0.1 convert_reduce_fusion.1
  1.4 0.2 convert_reduce_fusion
  1.6 0.2 fusion.7
  1.8 0.4 fusion
  2.3 0.8 %broadcast_in_dim.4 = f32[16,32,256]{2,1,0:T(8,128)} broadcast(f32[32,256]{1,0:T(8,128)S(1)} %fusion), dimensions={1,2} | broadcast | bytes 557056 | tf_op jit(solution)/shard_map/broadcast_in_dim | solution.py:219
  3.1 7.6 %all-to-all-start = ((f32[16,32,256]{2,1,0:T(8,128)}), f32[16,32,256]{2,1,0:T(8,128)}, u32[]{:S(2)}, u32[]{:S(2)}) async-start(f32[16,32,256]{2,1,0:T(8,128)} %broadcast_in_dim.4), calls=%async_computation | async-start | bytes 1048576 | tf_op jit(solution)/shard_map/all_to_all | solution.py:220
  10.7 0.9 %slice_bitcast_fusion.2 = (f32[2,32,256]{2,1,0:T(8,128)S(1)}, f32[2,32,256]{2,1,0:T(8,128)S(1)}) fusion(f32[3,8,32,256]{3,2,1,0:T(8,128)} %ha.1, f32[3,8,32,256]{3,2,1,0:T(8,128)S(1)} %copy-done.3), kind=kLoop, calls=%fused_computation.15 | loop fusion | bytes 262144 | tf_op jit(solution)/shard_map/squeeze | solution.py:213
  11.6 0.7 %pad_maximum_fusion = f32[10,32,256]{2,1,0:T(8,128)} fusion(f32[3,32,256]{2,1,0:T(8,128)S(1)} %get-tuple-element.21, f32[2,32,256]{2,1,0:T(8,128)S(1)} %get-tuple-element.23, f32[3,32,256]{2,1,0:T(8,128)S(1)} %get-tuple-element.22, f32[2,32,256]{2,1,0:T(8,128)S(1)} %get-tuple-element.24), kind=kLoop, calls=%fused_computation.1 | loop fusion | flops 245760 | bytes 655360 | tf_op jit(solution)/shard_map/concatenate | solution.py:212
  12.4 2.3 %collective-permute-start.1 = (f32[10,32,256]{2,1,0:T(8,128)}, f32[10,32,256]{2,1,0:T(8,128)S(1)}, u32[]{:S(2)}, u32[]{:S(2)}) collective-permute-start(f32[10,32,256]{2,1,0:T(8,128)} %pad_maximum_fusion), channel_id=1, source_target_pairs={{0,1},{1,2},{2,3},{3,4},{4,5},{5,6},{6,7},{7,8},{8,9},{9,10},{10,1... | collective-permute-start | bytes 983048 | tf_op jit(solution)/shard_map/ppermute | solution.py:25
  14.7 0.7 %pad_maximum_fusion.1 = f32[4,32,256]{2,1,0:T(8,128)} fusion(f32[2,32,256]{2,1,0:T(8,128)S(1)} %get-tuple-element.19, f32[2,32,256]{2,1,0:T(8,128)S(1)} %get-tuple-element.20), kind=kLoop, calls=%fused_computation.6 | loop fusion | flops 32768 | bytes 262144 | tf_op jit(solution)/shard_map/concatenate | solution.py:210
  15.3 1.3 %collective-permute-start = (f32[4,32,256]{2,1,0:T(8,128)}, f32[4,32,256]{2,1,0:T(8,128)}, u32[]{:S(2)}, u32[]{:S(2)}) collective-permute-start(f32[4,32,256]{2,1,0:T(8,128)} %pad_maximum_fusion.1), channel_id=1, source_target_pairs={{1,0},{2,1},{3,2},{4,3},{5,4},{6,5},{7,6},{8,7},{9,8},{10,9},{11,1... | collective-permute-start | bytes 393224 | tf_op jit(solution)/shard_map/ppermute | solution.py:25
  17.3 0.7 %copy.32.amp = f32[16,3]{1,0:T(8,128)} copy(f32[16,3]{0,1:T(4,128)S(1)} %copy-done.11) | data formatting | bytes 384 | tf_op args[9]
  18.0 2.1 %collective-permute-done.upper = f32[4,32,256]{2,1,0:T(8,128)} collective-permute-done((f32[4,32,256]{2,1,0:T(8,128)}, f32[4,32,256]{2,1,0:T(8,128)}, u32[]{:S(2)}, u32[]{:S(2)}) %collective-permute-start) | collective-permute-done | bytes 131104 | tf_op jit(solution)/shard_map/ppermute | solution.py:25
  20.0 1.1 %copy-done.5 = f32[3,8,32,256]{3,2,1,0:T(8,128)S(1)} copy-done((f32[3,8,32,256]{3,2,1,0:T(8,128)S(1)}, f32[3,8,32,256]{3,2,1,0:T(8,128)}, u32[]{:S(2)}) %copy-start.5) | copy-done | bytes 786456
  21.2 1.1 %copy-done.6 = f32[3,8,32,256]{3,2,1,0:T(8,128)S(1)} copy-done((f32[3,8,32,256]{3,2,1,0:T(8,128)S(1)}, f32[3,8,32,256]{3,2,1,0:T(8,128)}, u32[]{:S(2)}) %copy-start.6) | copy-done | bytes 786456
  22.3 1.1 %copy-done.7 = f32[3,8,32,256]{3,2,1,0:T(8,128)S(1)} copy-done((f32[3,8,32,256]{3,2,1,0:T(8,128)S(1)}, f32[3,8,32,256]{3,2,1,0:T(8,128)}, u32[]{:S(2)}) %copy-start.7) | copy-done | bytes 786456
  23.4 1.1 %copy-done.8 = f32[3,8,32,256]{3,2,1,0:T(8,128)S(1)} copy-done((f32[3,8,32,256]{3,2,1,0:T(8,128)S(1)}, f32[3,8,32,256]{3,2,1,0:T(8,128)}, u32[]{:S(2)}) %copy-start.8) | copy-done | bytes 786456
  24.6 3.3 %shard_map.173 = (f32[3,8,32,256]{3,2,1,0:T(8,128)}, f32[3,8,32,256]{3,2,1,0:T(8,128)}, f32[3,8,32,256]{3,2,1,0:T(8,128)S(1)}, f32[3,8,32,256]{3,2,1,0:T(8,128)S(1)}) custom-call(f32[3,8,32,256]{3,2,1,0:T(8,128)S(1)} %copy-done.1, f32[3,8,32,256]{3,2,1,0:T(8,128)S(1)} %copy-done.3, f32[3,8,32,256]{3,2,1,0:T(8,128)S(1)} %copy-done.5, ...), custom_call_target="tpu_custom_call" | custom-call | flops 7864320 | bytes 9437184 | tf_op jit(solution)/shard_map/pallas_call | solution.py:163
  27.9 0.9 %copy-done.9 = f32[3,8,32,256]{3,2,1,0:T(8,128)} copy-done((f32[3,8,32,256]{3,2,1,0:T(8,128)}, f32[3,8,32,256]{3,2,1,0:T(8,128)S(1)}, u32[]{:S(2)}) %copy-start.9) | copy-done | bytes 786456
  28.8 0.9 %copy-done.10 = f32[3,8,32,256]{3,2,1,0:T(8,128)} copy-done((f32[3,8,32,256]{3,2,1,0:T(8,128)}, f32[3,8,32,256]{3,2,1,0:T(8,128)S(1)}, u32[]{:S(2)}) %copy-start.10) | copy-done | bytes 786456
  29.7 4.6 %shard_map.174 = (f32[3,8,32,256]{3,2,1,0:T(8,128)}, f32[3,8,32,256]{3,2,1,0:T(8,128)}, f32[16,32,256]{2,1,0:T(8,128)}) custom-call(f32[3,8,32,256]{3,2,1,0:T(8,128)} %ef.3, f32[3,8,32,256]{3,2,1,0:T(8,128)} %copy-done.9, f32[3,8,32,256]{3,2,1,0:T(8,128)} %ea.3, f32[3,8,32,256]{3,2,1,0:T(8,128)} %copy-done.10, f32[16,32,256]{2,1,0:T(8,128)} %all-to-all-done.arrived, ...), custom_call_target="tpu_custom_call" | custom-call | flops 2621440 | bytes 5242880 | tf_op jit(solution)/shard_map/pallas_call | solution.py:174
  34.3 26.7 %all_to_all.10 = f32[16,32,256]{2,1,0:T(8,128)S(1)} all-to-all(f32[16,32,256]{2,1,0:T(8,128)} %get-tuple-element.18), channel_id=1, replica_groups=mesh['grp'=2,'gx'=16] {'gx'}, dimensions={0} | all-to-all | bytes 1048576 | tf_op jit(solution)/shard_map/all_to_all | solution.py:225
  61.0 0.3 fusion.9
  61.3 0.9 %convolution_bitcast_fusion = f32[1,32,256]{2,1,0:T(8,128)} fusion(f32[32,256]{1,0:T(8,128)S(1)} %fusion.9, f32[256]{0:T(256)S(1)} %convert_reduce_fusion, s32[]{:T(128)} %bitcast.6), kind=kOutput, calls=%fused_computation | convolution fusion | flops 25559040 | bytes 66564 | tf_op jit(solution)/shard_map/xb,by->xy/dot_general | solution.py:227
  (23 shorter events, 0.1 us)
Async XLA Ops:
  0.6 0.9 %copy-start = (f32[1,32,256]{2,1,0:T(8,128)S(1)}, f32[1,32,256]{2,1,0:T(8,128)}, u32[]{:S(2)}) copy-start(f32[1,32,256]{2,1,0:T(8,128)} %param.22) | copy-start | bytes 98308
  1.8 8.9 %copy-start.3 = (f32[3,8,32,256]{3,2,1,0:T(8,128)S(1)}, f32[3,8,32,256]{3,2,1,0:T(8,128)}, u32[]{:S(2)}) copy-start(f32[3,8,32,256]{3,2,1,0:T(8,128)} %hf.1) | copy-start | bytes 2359300
  2.3 9.3 %copy-start.2 = (f32[3,8,32,256]{3,2,1,0:T(8,128)S(1)}, f32[3,8,32,256]{3,2,1,0:T(8,128)}, u32[]{:S(2)}) copy-start(f32[3,8,32,256]{3,2,1,0:T(8,128)} %ea.3) | copy-start | bytes 2359300
  3.1 8.5 %copy-start.1 = (f32[3,8,32,256]{3,2,1,0:T(8,128)S(1)}, f32[3,8,32,256]{3,2,1,0:T(8,128)}, u32[]{:S(2)}) copy-start(f32[3,8,32,256]{3,2,1,0:T(8,128)} %ef.3) | copy-start | bytes 2359300
  3.1 26.6 %all-to-all-start = ((f32[16,32,256]{2,1,0:T(8,128)}), f32[16,32,256]{2,1,0:T(8,128)}, u32[]{:S(2)}, u32[]{:S(2)}) async-start(f32[16,32,256]{2,1,0:T(8,128)} %broadcast_in_dim.4), calls=%async_computation | async-start | bytes 1048576 | tf_op jit(solution)/shard_map/all_to_all | solution.py:220
  11.6 8.5 %copy-start.4 = (f32[3,8,32,256]{3,2,1,0:T(8,128)S(1)}, f32[3,8,32,256]{3,2,1,0:T(8,128)}, u32[]{:S(2)}) copy-start(f32[3,8,32,256]{3,2,1,0:T(8,128)} %ha.1) | copy-start | bytes 2359300
  12.4 7.7 %collective-permute-start.1 = (f32[10,32,256]{2,1,0:T(8,128)}, f32[10,32,256]{2,1,0:T(8,128)S(1)}, u32[]{:S(2)}, u32[]{:S(2)}) collective-permute-start(f32[10,32,256]{2,1,0:T(8,128)} %pad_maximum_fusion), channel_id=1, source_target_pairs={{0,1},{1,2},{2,3},{3,4},{4,5},{5,6},{6,7},{7,8},{8,9},{9,10},{10,1... | collective-permute-start | bytes 983048 | tf_op jit(solution)/shard_map/ppermute | solution.py:25
  14.7 2.6 %copy-start.11 = (f32[16,3]{0,1:T(4,128)S(1)}, f32[16,3]{0,1:T(4,128)}, u32[]{:S(2)}) copy-start(f32[16,3]{0,1:T(4,128)} %param.23) | copy-start | bytes 580
  15.3 4.7 %collective-permute-start = (f32[4,32,256]{2,1,0:T(8,128)}, f32[4,32,256]{2,1,0:T(8,128)}, u32[]{:S(2)}, u32[]{:S(2)}) collective-permute-start(f32[4,32,256]{2,1,0:T(8,128)} %pad_maximum_fusion.1), channel_id=1, source_target_pairs={{1,0},{2,1},{3,2},{4,3},{5,4},{6,5},{7,6},{8,7},{9,8},{10,9},{11,1... | collective-permute-start | bytes 393224 | tf_op jit(solution)/shard_map/ppermute | solution.py:25
  20.0 1.1 %copy-start.5 = (f32[3,8,32,256]{3,2,1,0:T(8,128)S(1)}, f32[3,8,32,256]{3,2,1,0:T(8,128)}, u32[]{:S(2)}) copy-start(f32[3,8,32,256]{3,2,1,0:T(8,128)} %pf.1) | copy-start | bytes 2359300
  21.2 1.1 %copy-start.6 = (f32[3,8,32,256]{3,2,1,0:T(8,128)S(1)}, f32[3,8,32,256]{3,2,1,0:T(8,128)}, u32[]{:S(2)}) copy-start(f32[3,8,32,256]{3,2,1,0:T(8,128)} %jf.1) | copy-start | bytes 2359300
  22.3 1.1 %copy-start.7 = (f32[3,8,32,256]{3,2,1,0:T(8,128)S(1)}, f32[3,8,32,256]{3,2,1,0:T(8,128)}, u32[]{:S(2)}) copy-start(f32[3,8,32,256]{3,2,1,0:T(8,128)} %pa.1) | copy-start | bytes 2359300
  23.4 1.1 %copy-start.8 = (f32[3,8,32,256]{3,2,1,0:T(8,128)S(1)}, f32[3,8,32,256]{3,2,1,0:T(8,128)}, u32[]{:S(2)}) copy-start(f32[3,8,32,256]{3,2,1,0:T(8,128)} %ja.1) | copy-start | bytes 2359300
  27.9 0.9 %copy-start.9 = (f32[3,8,32,256]{3,2,1,0:T(8,128)}, f32[3,8,32,256]{3,2,1,0:T(8,128)S(1)}, u32[]{:S(2)}) copy-start(f32[3,8,32,256]{3,2,1,0:T(8,128)S(1)} %get-tuple-element.12.qf) | copy-start | bytes 2359300
  28.8 0.9 %copy-start.10 = (f32[3,8,32,256]{3,2,1,0:T(8,128)}, f32[3,8,32,256]{3,2,1,0:T(8,128)S(1)}, u32[]{:S(2)}) copy-start(f32[3,8,32,256]{3,2,1,0:T(8,128)S(1)} %get-tuple-element.13.qa) | copy-start | bytes 2359300

commit v10 on v7

--- a/solution.py
+++ b/solution.py
@@ -40,6 +40,19 @@
 def smooth_adjoint(wx, wy, planes):
     inner = jnp.einsum("ax,zab->zxb", wx, planes, precision=HIGH)
     return jnp.einsum("zxb,by->zxy", inner, wy, precision=HIGH)
+
+
+def split_cell(cell, width_x, width_y):
+    plane = width_x * width_y
+    if plane & (plane - 1) == 0 and width_y & (width_y - 1) == 0:
+        zz = lax.shift_right_arithmetic(cell, plane.bit_length() - 1)
+        rest = lax.bitwise_and(cell, plane - 1)
+        x = lax.shift_right_arithmetic(rest, width_y.bit_length() - 1)
+        return zz, x, lax.bitwise_and(rest, width_y - 1)
+    zz = cell // plane
+    rest = cell - zz * plane
+    x = rest // width_y
+    return zz, x, rest - x * width_y
 
 
 def field_kernel(
@@ -120,12 +133,9 @@
     tile_lane = lax.broadcasted_iota(jnp.int32, (8, width_y), 1)
 
     def add_at(cell, out, value_of):
-        zz = cell // plane
+        zz, x, y = split_cell(cell, width_x, width_y)
         local = zz - index * depth
-        rest = cell - zz * plane
-        x = rest // width_y
-        y = rest - x * width_y
-        x0 = pl.multiple_of((x // 8) * 8, 8)
+        x0 = pl.multiple_of(x - lax.bitwise_and(x, 7), 8)
 
         @pl.when((local >= 0) & (local < depth))
         def _():

time: 56.5 us -> 56.1 us (level)
  no operation moved by 1% of the time
where the time goes in v10:
time: 56.1 us; the launch traced here: 55.6 us
  blocking collectives  21.4 us (38%)
  starting transfers between devices  11.1 us (20%)
  waiting for transfers between devices  8.36 us (15%)
  Pallas kernels  5.52 us (10%)
  local copies, waits for them, and re-layouts  4.12 us (7%)
  between operations  2.1 us (4%)
  matrix products  1.88 us (3%)
  other arithmetic  1.06 us (2%)
    all_to_all x1, blocking collectives, body(): lax.all_to_all(returned, 'gx', split_axis=0, concat_axis=0, tiled=True)  21.4 us
    all_to_all x1, starting transfers between devices, body(): lax.all_to_all(slots, 'gx', split_axis=0, concat_axis=0, tiled=True)  7.52 us
    all_to_all x1, waiting for transfers between devices, body(): lax.all_to_all(slots, 'gx', split_axis=0, concat_axis=0, tiled=True)  6.07 us
    pallas_call x1, Pallas kernels, fields(): pl.pallas_call(field_kernel, out_shape=(field, field, field, field, jax.S...  5.52 us
    ppermute x2, starting transfers between devices, passed_along(): return lax.ppermute(block, axis, route)  3.61 us
    unnamed x19, local copies, waits for them, and re-layouts  2.4 us
    ppermute x2, waiting for transfers between devices, passed_along(): return lax.ppermute(block, axis, route)  2.3 us
  transfers between devices with their start and end apart: 3, of which 2 were waited for; matrix products, arithmetic and copies ran while one was open for 3% of the time, Pallas kernels for 0%

profile of v10, /device:TPU:0, one launch (start us, length us, event | category | flops | bytes accessed | tf_op | source)
XLA Modules:
  0.0 55.6 jit_solution(7081136688049616359)
XLA Ops:
  0.6 0.0 copy-start
  1.3 0.1 convert_reduce_fusion.1
  1.4 0.2 convert_reduce_fusion
  1.6 0.2 fusion.7
  1.8 0.0 copy-start.3
  1.8 0.4 fusion
  2.3 0.0 copy-start.2
  2.3 0.8 %broadcast_in_dim.4 = f32[16,32,256]{2,1,0:T(8,128)} broadcast(f32[32,256]{1,0:T(8,128)S(1)} %fusion), dimensions={1,2} | broadcast | bytes 557056 | tf_op jit(solution)/shard_map/broadcast_in_dim | solution.py:222
  3.1 7.5 %all-to-all-start = ((f32[16,32,256]{2,1,0:T(8,128)}), f32[16,32,256]{2,1,0:T(8,128)S(1)}, u32[]{:S(2)}, u32[]{:S(2)}) async-start(f32[16,32,256]{2,1,0:T(8,128)} %broadcast_in_dim.4), calls=%async_computation | async-start | bytes 1048576 | tf_op jit(solution)/shard_map/all_to_all | solution.py:223
  10.6 0.9 %slice_bitcast_fusion.2 = (f32[2,32,256]{2,1,0:T(8,128)S(1)}, f32[2,32,256]{2,1,0:T(8,128)S(1)}) fusion(f32[3,8,32,256]{3,2,1,0:T(8,128)} %ha.1, f32[3,8,32,256]{3,2,1,0:T(8,128)S(1)} %copy-done.3), kind=kLoop, calls=%fused_computation.15 | loop fusion | bytes 262144 | tf_op jit(solution)/shard_map/squeeze | solution.py:216
  11.6 0.7 %pad_maximum_fusion = f32[10,32,256]{2,1,0:T(8,128)} fusion(f32[3,32,256]{2,1,0:T(8,128)S(1)} %get-tuple-element.17, f32[2,32,256]{2,1,0:T(8,128)S(1)} %get-tuple-element.19, f32[3,32,256]{2,1,0:T(8,128)S(1)} %get-tuple-element.18, f32[2,32,256]{2,1,0:T(8,128)S(1)} %get-tuple-element.20), kind=kLoop, calls=%fused_computation.1 | loop fusion | flops 245760 | bytes 655360 | tf_op jit(solution)/shard_map/concatenate | solution.py:215
  12.3 2.3 %collective-permute-start.1 = (f32[10,32,256]{2,1,0:T(8,128)}, f32[10,32,256]{2,1,0:T(8,128)S(1)}, u32[]{:S(2)}, u32[]{:S(2)}) collective-permute-start(f32[10,32,256]{2,1,0:T(8,128)} %pad_maximum_fusion), channel_id=1, source_target_pairs={{0,1},{1,2},{2,3},{3,4},{4,5},{5,6},{6,7},{7,8},{8,9},{9,10},{10,1... | collective-permute-start | bytes 983048 | tf_op jit(solution)/shard_map/ppermute | solution.py:25
  14.6 0.0 copy-start.8
  14.7 1.3 %collective-permute-start = (f32[4,32,256]{2,1,0:T(8,128)S(1)}, f32[4,32,256]{2,1,0:T(8,128)S(1)}, u32[]{:S(2)}, u32[]{:S(2)}) collective-permute-start(f32[4,32,256]{2,1,0:T(8,128)S(1)} %pad_maximum_fusion.1), channel_id=1, source_target_pairs={{1,0},{2,1},{3,2},{4,3},{5,4},{6,5},{7,6},{8,7},{9,8},{10,9},{11,1... | collective-permute-start | bytes 393224 | tf_op jit(solution)/shard_map/ppermute | solution.py:25
  16.6 0.0 copy-start.7
  16.7 0.1 copy.32.amp
  16.7 2.3 %collective-permute-done.upper = f32[4,32,256]{2,1,0:T(8,128)S(1)} collective-permute-done((f32[4,32,256]{2,1,0:T(8,128)S(1)}, f32[4,32,256]{2,1,0:T(8,128)S(1)}, u32[]{:S(2)}, u32[]{:S(2)}) %collective-permute-start) | collective-permute-done | bytes 131104 | tf_op jit(solution)/shard_map/ppermute | solution.py:25
  19.0 6.1 %all-to-all-done.arrived = f32[16,32,256]{2,1,0:T(8,128)S(1)} async-done(((f32[16,32,256]{2,1,0:T(8,128)}), f32[16,32,256]{2,1,0:T(8,128)S(1)}, u32[]{:S(2)}, u32[]{:S(2)}) %all-to-all-start) | async-done | bytes 524320 | tf_op jit(solution)/shard_map/all_to_all | solution.py:223
  25.1 1.1 %copy-done.4 = f32[3,8,32,256]{3,2,1,0:T(8,128)S(1)} copy-done((f32[3,8,32,256]{3,2,1,0:T(8,128)S(1)}, f32[3,8,32,256]{3,2,1,0:T(8,128)}, u32[]{:S(2)}) %copy-start.4) | copy-done | bytes 786456
  26.2 1.1 %copy-done.5 = f32[3,8,32,256]{3,2,1,0:T(8,128)S(1)} copy-done((f32[3,8,32,256]{3,2,1,0:T(8,128)S(1)}, f32[3,8,32,256]{3,2,1,0:T(8,128)}, u32[]{:S(2)}) %copy-start.5) | copy-done | bytes 786456
  27.4 5.5 %shard_map.173 = (f32[3,8,32,256]{3,2,1,0:T(8,128)}, f32[3,8,32,256]{3,2,1,0:T(8,128)}, f32[3,8,32,256]{3,2,1,0:T(8,128)}, f32[3,8,32,256]{3,2,1,0:T(8,128)}, f32[16,32,256]{2,1,0:T(8,128)S(1)}) custom-call(f32[3,8,32,256]{3,2,1,0:T(8,128)S(1)} %copy-done.1, f32[3,8,32,256]{3,2,1,0:T(8,128)S(1)} %copy-done.3, f32[3,8,32,256]{3,2,1,0:T(8,128)S(1)} %copy-done.4, ...), custom_call_target="tpu_custom_call" | custom-call | flops 13107200 | bytes 10485760 | tf_op jit(solution)/shard_map/pallas_call | solution.py:177
  32.9 21.4 %all_to_all.10 = f32[16,32,256]{2,1,0:T(8,128)S(1)} all-to-all(f32[16,32,256]{2,1,0:T(8,128)S(1)} %get-tuple-element.14), channel_id=1, replica_groups=mesh['grp'=2,'gx'=16] {'gx'}, dimensions={0} | all-to-all | bytes 1048576 | tf_op jit(solution)/shard_map/all_to_all | solution.py:228
  54.3 0.3 fusion.9
  54.6 0.9 %convolution_bitcast_fusion = f32[1,32,256]{2,1,0:T(8,128)} fusion(f32[32,256]{1,0:T(8,128)S(1)} %fusion.9, f32[256]{0:T(256)S(1)} %convert_reduce_fusion, s32[]{:T(128)} %bitcast), kind=kOutput, calls=%fused_computation | convolution fusion | flops 25559040 | bytes 66564 | tf_op jit(solution)/shard_map/xb,by->xy/dot_general | solution.py:230
  (16 shorter events, 0.1 us)
Async XLA Ops:
  0.6 0.9 %copy-start = (f32[1,32,256]{2,1,0:T(8,128)S(1)}, f32[1,32,256]{2,1,0:T(8,128)}, u32[]{:S(2)}) copy-start(f32[1,32,256]{2,1,0:T(8,128)} %param.22) | copy-start | bytes 98308
  1.8 8.8 %copy-start.3 = (f32[3,8,32,256]{3,2,1,0:T(8,128)S(1)}, f32[3,8,32,256]{3,2,1,0:T(8,128)}, u32[]{:S(2)}) copy-start(f32[3,8,32,256]{3,2,1,0:T(8,128)} %hf.1) | copy-start | bytes 2359300
  2.3 9.3 %copy-start.2 = (f32[3,8,32,256]{3,2,1,0:T(8,128)S(1)}, f32[3,8,32,256]{3,2,1,0:T(8,128)}, u32[]{:S(2)}) copy-start(f32[3,8,32,256]{3,2,1,0:T(8,128)} %ea.1) | copy-start | bytes 2359300
  3.1 8.4 %copy-start.1 = (f32[3,8,32,256]{3,2,1,0:T(8,128)S(1)}, f32[3,8,32,256]{3,2,1,0:T(8,128)}, u32[]{:S(2)}) copy-start(f32[3,8,32,256]{3,2,1,0:T(8,128)} %ef.1) | copy-start | bytes 2359300
  3.1 22.0 %all-to-all-start = ((f32[16,32,256]{2,1,0:T(8,128)}), f32[16,32,256]{2,1,0:T(8,128)S(1)}, u32[]{:S(2)}, u32[]{:S(2)}) async-start(f32[16,32,256]{2,1,0:T(8,128)} %broadcast_in_dim.4), calls=%async_computation | async-start | bytes 1048576 | tf_op jit(solution)/shard_map/all_to_all | solution.py:223
  12.3 6.7 %collective-permute-start.1 = (f32[10,32,256]{2,1,0:T(8,128)}, f32[10,32,256]{2,1,0:T(8,128)S(1)}, u32[]{:S(2)}, u32[]{:S(2)}) collective-permute-start(f32[10,32,256]{2,1,0:T(8,128)} %pad_maximum_fusion), channel_id=1, source_target_pairs={{0,1},{1,2},{2,3},{3,4},{4,5},{5,6},{6,7},{7,8},{8,9},{9,10},{10,1... | collective-permute-start | bytes 983048 | tf_op jit(solution)/shard_map/ppermute | solution.py:25
  14.6 2.0 %copy-start.8 = (f32[16,3]{0,1:T(4,128)S(1)}, f32[16,3]{0,1:T(4,128)}, u32[]{:S(2)}) copy-start(f32[16,3]{0,1:T(4,128)} %param.23) | copy-start | bytes 580
  14.7 4.4 %collective-permute-start = (f32[4,32,256]{2,1,0:T(8,128)S(1)}, f32[4,32,256]{2,1,0:T(8,128)S(1)}, u32[]{:S(2)}, u32[]{:S(2)}) collective-permute-start(f32[4,32,256]{2,1,0:T(8,128)S(1)} %pad_maximum_fusion.1), channel_id=1, source_target_pairs={{1,0},{2,1},{3,2},{4,3},{5,4},{6,5},{7,6},{8,7},{9,8},{10,9},{11,1... | collective-permute-start | bytes 393224 | tf_op jit(solution)/shard_map/ppermute | solution.py:25
  16.6 8.5 %copy-start.6 = (s32[16]{0:T(128)S(1)}, s32[16]{0:T(128)}, u32[]{:S(2)}) copy-start(s32[16]{0:T(128)} %src.1) | copy-start | bytes 196
  16.6 8.5 %copy-start.7 = (s32[16]{0:T(128)S(1)}, s32[16]{0:T(128)}, u32[]{:S(2)}) copy-start(s32[16]{0:T(128)} %mon.1) | copy-start | bytes 196
  25.1 1.1 %copy-start.4 = (f32[3,8,32,256]{3,2,1,0:T(8,128)S(1)}, f32[3,8,32,256]{3,2,1,0:T(8,128)}, u32[]{:S(2)}) copy-start(f32[3,8,32,256]{3,2,1,0:T(8,128)} %pf.1) | copy-start | bytes 2359300
  26.2 1.1 %copy-start.5 = (f32[3,8,32,256]{3,2,1,0:T(8,128)S(1)}, f32[3,8,32,256]{3,2,1,0:T(8,128)}, u32[]{:S(2)}) copy-start(f32[3,8,32,256]{3,2,1,0:T(8,128)} %jf.1) | copy-start | bytes 2359300

commit v11 on v10

--- a/solution.py
+++ b/solution.py
@@ -180,7 +180,7 @@
         in_specs=[vmem] * 11 + [smem] * 4,
         out_specs=(vmem,) * 5,
         scratch_shapes=[pltpu.VMEM(shape[1:], jnp.float32)],
-        compiler_params=pltpu.CompilerParams(vmem_limit_bytes=48 * 1024 * 1024),
+        compiler_params=pltpu.CompilerParams(vmem_limit_bytes=50 * 1024 * 1024),
         cost_estimate=pl.CostEstimate(
             flops=200 * cells, bytes_accessed=4 * cells * 40, transcendentals=0
         ),

time: 56.1 us -> 54.4 us (0.970)
  waiting for transfers between devices: 8.36 us -> 6.59 us
    unnamed x19 -> x15, local copies, waits for them, and re-layouts: 2.4 us -> 0.13 us
    all_to_all x1, waiting for transfers between devices: 6.07 us -> 4.29 us  [body(): lax.all_to_all(slots, 'gx', split_axis=0, concat_axis=0, tiled=True)]
    squeeze x1, local copies, waits for them, and re-layouts: 0.02 us -> 0.99 us  [body(): e_adjoint[:, -1]]
    squeeze x1, local copies, waits for them, and re-layouts: 0.01 us -> 0.85 us  [body(): e_adjoint[0:2, 0]]
  transfers between devices with their start and end apart: 3 -> 3, of which waited for: 2 -> 2; matrix products, arithmetic and copies ran while one was open for 3% -> 7% of each run, Pallas kernels for 0% -> 0%
where the time goes in v11:
time: 54.4 us; the launch traced here: 53.9 us
  blocking collectives  21.5 us (40%)
  starting transfers between devices  11.1 us (20%)
  waiting for transfers between devices  6.59 us (12%)
  Pallas kernels  6.02 us (11%)
  local copies, waits for them, and re-layouts  3.67 us (7%)
  between operations  2.08 us (4%)
  matrix products  1.88 us (3%)
  other arithmetic  1.06 us (2%)
    all_to_all x1, blocking collectives, body(): lax.all_to_all(returned, 'gx', split_axis=0, concat_axis=0, tiled=True)  21.5 us
    all_to_all x1, starting transfers between devices, body(): lax.all_to_all(slots, 'gx', split_axis=0, concat_axis=0, tiled=True)  7.51 us
    pallas_call x1, Pallas kernels, fields(): pl.pallas_call(field_kernel, out_shape=(field, field, field, field, jax.S...  6.02 us
    all_to_all x1, waiting for transfers between devices, body(): lax.all_to_all(slots, 'gx', split_axis=0, concat_axis=0, tiled=True)  4.29 us
    ppermute x2, starting transfers between devices, passed_along(): return lax.ppermute(block, axis, route)  3.61 us
    ppermute x2, waiting for transfers between devices, passed_along(): return lax.ppermute(block, axis, route)  2.3 us
  transfers between devices with their start and end apart: 3, of which 2 were waited for; matrix products, arithmetic and copies ran while one was open for 7% of the time, Pallas kernels for 0%

profile of v11, /device:TPU:0, one launch (start us, length us, event | category | flops | bytes accessed | tf_op | source)
XLA Modules:
  0.0 53.9 jit_solution(17764106362640625386)
XLA Ops:
  0.6 0.0 copy-start
  1.3 0.1 convert_reduce_fusion.1
  1.4 0.2 convert_reduce_fusion
  1.6 0.2 fusion.7
  1.8 0.4 fusion
  2.2 0.0 copy-start.2
  2.3 0.8 %broadcast_in_dim.4 = f32[16,32,256]{2,1,0:T(8,128)} broadcast(f32[32,256]{1,0:T(8,128)S(1)} %fusion), dimensions={1,2} | broadcast | bytes 557056 | tf_op jit(solution)/shard_map/broadcast_in_dim | solution.py:222
  3.1 7.5 %all-to-all-start = ((f32[16,32,256]{2,1,0:T(8,128)}), f32[16,32,256]{2,1,0:T(8,128)S(1)}, u32[]{:S(2)}, u32[]{:S(2)}) async-start(f32[16,32,256]{2,1,0:T(8,128)} %broadcast_in_dim.4), calls=%async_computation | async-start | bytes 1048576 | tf_op jit(solution)/shard_map/all_to_all | solution.py:223
  10.6 0.9 %slice_bitcast_fusion.2 = (f32[2,32,256]{2,1,0:T(8,128)S(1)}, f32[2,32,256]{2,1,0:T(8,128)S(1)}) fusion(f32[3,8,32,256]{3,2,1,0:T(8,128)} %ha.1, f32[3,8,32,256]{3,2,1,0:T(8,128)S(1)} %copy-done.2), kind=kLoop, calls=%fused_computation.15 | loop fusion | bytes 262144 | tf_op jit(solution)/shard_map/squeeze | solution.py:216
  11.5 0.0 copy-start.3
  11.5 1.0 %slice_bitcast_fusion = (f32[3,32,256]{2,1,0:T(8,128)S(1)}, f32[3,32,256]{2,1,0:T(8,128)S(1)}) fusion(f32[3,8,32,256]{3,2,1,0:T(8,128)} %ea.1, f32[3,8,32,256]{3,2,1,0:T(8,128)S(1)} %copy-done.1), kind=kLoop, calls=%fused_computation.13 | loop fusion | bytes 393216 | tf_op jit(solution)/shard_map/squeeze | solution.py:216
  12.5 0.7 %pad_maximum_fusion = f32[10,32,256]{2,1,0:T(8,128)} fusion(f32[3,32,256]{2,1,0:T(8,128)S(1)} %get-tuple-element.17, f32[2,32,256]{2,1,0:T(8,128)S(1)} %get-tuple-element.19, f32[3,32,256]{2,1,0:T(8,128)S(1)} %get-tuple-element.18, f32[2,32,256]{2,1,0:T(8,128)S(1)} %get-tuple-element.20), kind=kLoop, calls=%fused_computation.1 | loop fusion | flops 245760 | bytes 655360 | tf_op jit(solution)/shard_map/concatenate | solution.py:215
  13.3 2.3 %collective-permute-start.1 = (f32[10,32,256]{2,1,0:T(8,128)}, f32[10,32,256]{2,1,0:T(8,128)S(1)}, u32[]{:S(2)}, u32[]{:S(2)}) collective-permute-start(f32[10,32,256]{2,1,0:T(8,128)} %pad_maximum_fusion), channel_id=1, source_target_pairs={{0,1},{1,2},{2,3},{3,4},{4,5},{5,6},{6,7},{7,8},{8,9},{9,10},{10,1... | collective-permute-start | bytes 983048 | tf_op jit(solution)/shard_map/ppermute | solution.py:25
  15.6 0.9 %slice_bitcast_fusion.4 = (f32[2,32,256]{2,1,0:T(8,128)S(1)}, f32[2,32,256]{2,1,0:T(8,128)S(1)}) fusion(f32[3,8,32,256]{3,2,1,0:T(8,128)} %ea.1, f32[3,8,32,256]{3,2,1,0:T(8,128)S(1)} %copy-done.1), kind=kLoop, calls=%fused_computation.17 | loop fusion | bytes 262144 | tf_op jit(solution)/shard_map/squeeze | solution.py:213
  16.4 0.0 copy-start.6
  16.5 1.3 %collective-permute-start = (f32[4,32,256]{2,1,0:T(8,128)S(1)}, f32[4,32,256]{2,1,0:T(8,128)S(1)}, u32[]{:S(2)}, u32[]{:S(2)}) collective-permute-start(f32[4,32,256]{2,1,0:T(8,128)S(1)} %pad_maximum_fusion.1), channel_id=1, source_target_pairs={{1,0},{2,1},{3,2},{4,3},{5,4},{6,5},{7,6},{8,7},{9,8},{10,9},{11,1... | collective-permute-start | bytes 393224 | tf_op jit(solution)/shard_map/ppermute | solution.py:25
  18.4 0.0 copy-start.4
  18.4 0.1 copy.32.amp
  18.5 2.3 %collective-permute-done.upper = f32[4,32,256]{2,1,0:T(8,128)S(1)} collective-permute-done((f32[4,32,256]{2,1,0:T(8,128)S(1)}, f32[4,32,256]{2,1,0:T(8,128)S(1)}, u32[]{:S(2)}, u32[]{:S(2)}) %collective-permute-start) | collective-permute-done | bytes 131104 | tf_op jit(solution)/shard_map/ppermute | solution.py:25
  20.8 4.3 %all-to-all-done.arrived = f32[16,32,256]{2,1,0:T(8,128)S(1)} async-done(((f32[16,32,256]{2,1,0:T(8,128)}), f32[16,32,256]{2,1,0:T(8,128)S(1)}, u32[]{:S(2)}, u32[]{:S(2)}) %all-to-all-start) | async-done | bytes 524320 | tf_op jit(solution)/shard_map/all_to_all | solution.py:223
  25.1 6.0 %shard_map.173 = (f32[3,8,32,256]{3,2,1,0:T(8,128)}, f32[3,8,32,256]{3,2,1,0:T(8,128)}, f32[3,8,32,256]{3,2,1,0:T(8,128)}, f32[3,8,32,256]{3,2,1,0:T(8,128)}, f32[16,32,256]{2,1,0:T(8,128)S(1)}) custom-call(f32[3,8,32,256]{3,2,1,0:T(8,128)S(1)} %copy-done.1, f32[3,8,32,256]{3,2,1,0:T(8,128)S(1)} %copy-done.2, f32[3,8,32,256]{3,2,1,0:T(8,128)S(1)} %copy-done.3, ...), custom_call_target="tpu_custom_call" | custom-call | flops 13107200 | bytes 10485760 | tf_op jit(solution)/shard_map/pallas_call | solution.py:177
  31.2 21.5 %all_to_all.10 = f32[16,32,256]{2,1,0:T(8,128)S(1)} all-to-all(f32[16,32,256]{2,1,0:T(8,128)S(1)} %get-tuple-element.14), channel_id=1, replica_groups=mesh['grp'=2,'gx'=16] {'gx'}, dimensions={0} | all-to-all | bytes 1048576 | tf_op jit(solution)/shard_map/all_to_all | solution.py:228
  52.6 0.3 fusion.9
  52.9 0.9 %convolution_bitcast_fusion = f32[1,32,256]{2,1,0:T(8,128)} fusion(f32[32,256]{1,0:T(8,128)S(1)} %fusion.9, f32[256]{0:T(256)S(1)} %convert_reduce_fusion, s32[]{:T(128)} %bitcast), kind=kOutput, calls=%fused_computation | convolution fusion | flops 25559040 | bytes 66564 | tf_op jit(solution)/shard_map/xb,by->xy/dot_general | solution.py:230
  (12 shorter events, 0.1 us)
Async XLA Ops:
  0.6 0.9 %copy-start = (f32[1,32,256]{2,1,0:T(8,128)S(1)}, f32[1,32,256]{2,1,0:T(8,128)}, u32[]{:S(2)}) copy-start(f32[1,32,256]{2,1,0:T(8,128)} %param.22) | copy-start | bytes 98308
  2.2 8.4 %copy-start.2 = (f32[3,8,32,256]{3,2,1,0:T(8,128)S(1)}, f32[3,8,32,256]{3,2,1,0:T(8,128)}, u32[]{:S(2)}) copy-start(f32[3,8,32,256]{3,2,1,0:T(8,128)} %hf.1) | copy-start | bytes 2359300
  3.1 8.4 %copy-start.1 = (f32[3,8,32,256]{3,2,1,0:T(8,128)S(1)}, f32[3,8,32,256]{3,2,1,0:T(8,128)}, u32[]{:S(2)}) copy-start(f32[3,8,32,256]{3,2,1,0:T(8,128)} %ef.1) | copy-start | bytes 2359300
  3.1 22.0 %all-to-all-start = ((f32[16,32,256]{2,1,0:T(8,128)}), f32[16,32,256]{2,1,0:T(8,128)S(1)}, u32[]{:S(2)}, u32[]{:S(2)}) async-start(f32[16,32,256]{2,1,0:T(8,128)} %broadcast_in_dim.4), calls=%async_computation | async-start | bytes 1048576 | tf_op jit(solution)/shard_map/all_to_all | solution.py:223
  11.5 13.6 %copy-start.3 = (f32[3,8,32,256]{3,2,1,0:T(8,128)S(1)}, f32[3,8,32,256]{3,2,1,0:T(8,128)}, u32[]{:S(2)}) copy-start(f32[3,8,32,256]{3,2,1,0:T(8,128)} %pf.1) | copy-start | bytes 2359300
  13.3 7.6 %collective-permute-start.1 = (f32[10,32,256]{2,1,0:T(8,128)}, f32[10,32,256]{2,1,0:T(8,128)S(1)}, u32[]{:S(2)}, u32[]{:S(2)}) collective-permute-start(f32[10,32,256]{2,1,0:T(8,128)} %pad_maximum_fusion), channel_id=1, source_target_pairs={{0,1},{1,2},{2,3},{3,4},{4,5},{5,6},{6,7},{7,8},{8,9},{9,10},{10,1... | collective-permute-start | bytes 983048 | tf_op jit(solution)/shard_map/ppermute | solution.py:25
  16.4 2.0 %copy-start.6 = (f32[16,3]{0,1:T(4,128)S(1)}, f32[16,3]{0,1:T(4,128)}, u32[]{:S(2)}) copy-start(f32[16,3]{0,1:T(4,128)} %param.23) | copy-start | bytes 580
  16.5 4.4 %collective-permute-start = (f32[4,32,256]{2,1,0:T(8,128)S(1)}, f32[4,32,256]{2,1,0:T(8,128)S(1)}, u32[]{:S(2)}, u32[]{:S(2)}) collective-permute-start(f32[4,32,256]{2,1,0:T(8,128)S(1)} %pad_maximum_fusion.1), channel_id=1, source_target_pairs={{1,0},{2,1},{3,2},{4,3},{5,4},{6,5},{7,6},{8,7},{9,8},{10,9},{11,1... | collective-permute-start | bytes 393224 | tf_op jit(solution)/shard_map/ppermute | solution.py:25
  18.4 6.7 %copy-start.4 = (s32[16]{0:T(128)S(1)}, s32[16]{0:T(128)}, u32[]{:S(2)}) copy-start(s32[16]{0:T(128)} %src.1) | copy-start | bytes 196
  18.4 6.7 %copy-start.5 = (s32[16]{0:T(128)S(1)}, s32[16]{0:T(128)}, u32[]{:S(2)}) copy-start(s32[16]{0:T(128)} %mon.1) | copy-start | bytes 196

commit v12 on v5

--- a/solution.py
+++ b/solution.py
@@ -16,6 +16,7 @@
 HIGH = lax.Precision.HIGHEST
 KEEP = 1.0 - DAMPING * DT / 2.0
 LOSS = 1.0 + DAMPING * DT / 2.0
+SHRINK = 1.0 / LOSS
 
 
 def passed_along(block, axis, distance):
@@ -39,6 +40,19 @@
 def smooth_adjoint(wx, wy, planes):
     inner = jnp.einsum("ax,zab->zxb", wx, planes, precision=HIGH)
     return jnp.einsum("zxb,by->zxy", inner, wy, precision=HIGH)
+
+
+def split_cell(cell, width_x, width_y):
+    plane = width_x * width_y
+    if plane & (plane - 1) == 0 and width_y & (width_y - 1) == 0:
+        zz = lax.shift_right_arithmetic(cell, plane.bit_length() - 1)
+        rest = lax.bitwise_and(cell, plane - 1)
+        x = lax.shift_right_arithmetic(rest, width_y.bit_length() - 1)
+        return zz, x, lax.bitwise_and(rest, width_y - 1)
+    zz = cell // plane
+    rest = cell - zz * plane
+    x = rest // width_y
+    return zz, x, rest - x * width_y
 
 
 def field_kernel(
@@ -89,46 +103,18 @@
     def behind_x(f):
         return jnp.where(row == 0, 0.0, pltpu.roll(f, 1, 0))
 
-    plane = width_x * width_y
-    tile_row = lax.broadcasted_iota(jnp.int32, (8, width_y), 0)
-    tile_lane = lax.broadcasted_iota(jnp.int32, (8, width_y), 1)
-
-    def locate(cell):
-        zz = cell // plane
-        rest = cell - zz * plane
-        x = rest // width_y
-        y = rest - x * width_y
-        return zz - index * depth, x, y
-
-    src_at = [locate(src[s]) for s in range(src.shape[0])]
-    mon_at = [locate(mon[m]) for m in range(mon.shape[0])]
-
-    def add_at(where_, z, out, value_of):
-        local, x, y = where_
-        x0 = pl.multiple_of((x // 8) * 8, 8)
-
-        @pl.when(local == z)
-        def _():
-            rows = pl.ds(x0, 8)
-            hit = (tile_row == x - x0) & (tile_lane == y)
-            gain = DT / (1.0 + EPS_RANGE * rho[z, rows, :])
-            for c in range(3):
-                held = outs[out, c, z, rows, :]
-                outs[out, c, z, rows, :] = held + jnp.where(hit, gain * value_of(c, z, rows), 0.0)
-
     keep = index > 0
     prev = []
     for r in range(2):
         fetch(4 * r, 0).wait()
         fetch(4 * r + 1, 0).wait()
+        fetch(4 * r + 2, 0).wait()
+        fetch(4 * r + 3, 0).wait()
         hx, hy, ex, ey, ez = (below[5 * r + i] for i in range(5))
         e = ins.at[4 * r]
         curl_x = ahead_y(ez) - ez - (e[1, 0] - ey)
         curl_y = e[0, 0] - ex - (ahead_x(ez) - ez)
         prev.append((jnp.where(keep, hx - DT * curl_x, 0.0), jnp.where(keep, hy - DT * curl_y, 0.0)))
-    for r in range(2):
-        fetch(4 * r + 2, 0).wait()
-        fetch(4 * r + 3, 0).wait()
 
     for z in range(depth):
         if z + 1 < depth:
@@ -150,6 +136,7 @@
             outs[2 * r + 1, 0, z] = hx
             outs[2 * r + 1, 1, z] = hy
             outs[2 * r + 1, 2, z] = hz
+            store(2 * r + 1, z).start()
             hx_dn, hy_dn = prev[r]
             curl = (
                 hz - behind_y(hz) - (hy - hy_dn),
@@ -157,18 +144,36 @@
                 hy - behind_x(hy) - (hx - behind_y(hx)),
             )
             for c in range(3):
-                j_next = (KEEP * j[c, z] + DT * (strength * e[c, z] - p[c, z])) / LOSS
+                j_next = (KEEP * j[c, z] + DT * (strength * e[c, z] - p[c, z])) * SHRINK
                 outs[2 * r, c, z] = e[c, z] + step * (curl[c] - j_next)
             prev[r] = (hx, hy)
-            store(2 * r + 1, z).start()
-
-        for s in range(src.shape[0]):
-            add_at(src_at[s], z, 0, lambda c, zz, rows, s=s: amp[s, c])
-        for m in range(mon.shape[0]):
-            add_at(mon_at[m], z, 2, lambda c, zz, rows: ins[0, c, zz, rows, :])
+
+    tile_row = lax.broadcasted_iota(jnp.int32, (8, width_y), 0)
+    tile_lane = lax.broadcasted_iota(jnp.int32, (8, width_y), 1)
+
+    def add_at(cell, out, value_of):
+        zz, x, y = split_cell(cell, width_x, width_y)
+        local = zz - index * depth
+        x0 = pl.multiple_of(x - lax.bitwise_and(x, 7), 8)
+
+        @pl.when((local >= 0) & (local < depth))
+        def _():
+            rows = pl.ds(x0, 8)
+            hit = (tile_row == x - x0) & (tile_lane == y)
+            gain = DT / (1.0 + EPS_RANGE * rho[local, rows, :])
+            for c in range(3):
+                held = outs[out, c, local, rows, :]
+                outs[out, c, local, rows, :] = held + jnp.where(hit, gain * value_of(c, local, rows), 0.0)
+
+    for s in range(src.shape[0]):
+        add_at(src[s], 0, lambda c, local, rows, s=s: amp[s, c])
+    for m in range(mon.shape[0]):
+        add_at(mon[m], 2, lambda c, local, rows: ins[0, c, local, rows, :])
+    for z in range(depth):
         store(0, z).start()
         store(2, z).start()
 
+    for z in range(depth):
         total = None
         for c in range(3):
             fwd = outs[0, c, z]
@@ -190,7 +195,7 @@
     shape = e_forward.shape
     depth = shape[1]
     field = jax.ShapeDtypeStruct(shape, jnp.float32)
-    hbm = pl.BlockSpec(memory_space=pltpu.HBM)
+    hbm = pl.BlockSpec(memory_space=pl.ANY)
     vmem = pl.BlockSpec(memory_space=pltpu.VMEM)
     smem = pl.BlockSpec(memory_space=pltpu.SMEM)
     cells = shape[1] * shape[2] * shape[3]
@@ -206,7 +211,7 @@
             pltpu.SemaphoreType.DMA((8, depth)),
             pltpu.SemaphoreType.DMA((4, depth)),
         ],
-        compiler_params=pltpu.CompilerParams(vmem_limit_bytes=48 * 1024 * 1024),
+        compiler_params=pltpu.CompilerParams(vmem_limit_bytes=50 * 1024 * 1024),
         cost_estimate=pl.CostEstimate(
             flops=200 * cells, bytes_accessed=4 * cells * 40, transcendentals=0
         ),
@@ -245,9 +250,7 @@
         1,
     )
     owned = smooth(wx, wy, design)
-    holder = (start + index) // depth
-    target = (jnp.arange(count, dtype=jnp.int32) == holder).astype(jnp.float32)
-    slots = target[:, None, None] * owned
+    slots = jnp.broadcast_to(owned, (count,) + owned.shape[1:])
     arrived = lax.all_to_all(slots, "gx", split_axis=0, concat_axis=0, tiled=True)
     ef, hf, ea, ha, returned = fields(
         e_forward, h_forward, p_forward, j_forward, e_adjoint, h_adjoint, p_adjoint, j_adjoint,

time: 60.4 us -> 54.8 us (0.907)
  Pallas kernels: 9.04 us -> 6.36 us
  waiting for transfers between devices: 9.01 us -> 6.59 us
  other arithmetic: 1.96 us -> 1.06 us
    pallas_call x1, Pallas kernels: 9.04 us -> 6.36 us  [fields(): pl.pallas_call(field_kernel, out_shape=(field, field, field, field, jax.S...]
    unnamed x19 -> x15, local copies, waits for them, and re-layouts: 2.4 us -> 0.13 us
    all_to_all x1, waiting for transfers between devices: 6.04 us -> 4.29 us  [body(): lax.all_to_all(slots, 'gx', split_axis=0, concat_axis=0, tiled=True)]
    squeeze x1, local copies, waits for them, and re-layouts: 0.02 us -> 0.99 us  [body(): e_adjoint[:, -1]]
    mul x1 -> x0, other arithmetic: 0.9 us -> none  [body(): slots = target[:, None, None] * owned]
    broadcast_in_dim x0 -> x1, local copies, waits for them, and re-layouts: none -> 0.84 us  [body(): slots = jnp.broadcast_to(owned, (count,) + owned.shape[1:])]
    squeeze x1, local copies, waits for them, and re-layouts: 0.01 us -> 0.85 us  [body(): e_adjoint[0:2, 0]]
    ppermute x2, waiting for transfers between devices: 2.97 us -> 2.3 us  [passed_along(): return lax.ppermute(block, axis, route)]
  transfers between devices with their start and end apart: 3 -> 3, of which waited for: 2 -> 2; matrix products, arithmetic and copies ran while one was open for 3% -> 7% of each run, Pallas kernels for 0% -> 0%
where the time goes in v12:
time: 54.8 us; the launch traced here: 54.3 us
  blocking collectives  21.5 us (39%)
  starting transfers between devices  11.1 us (20%)
  waiting for transfers between devices  6.59 us (12%)
  Pallas kernels  6.36 us (12%)
  local copies, waits for them, and re-layouts  3.67 us (7%)
  between operations  2.09 us (4%)
  matrix products  1.88 us (3%)
  other arithmetic  1.06 us (2%)
    all_to_all x1, blocking collectives, body(): lax.all_to_all(returned, 'gx', split_axis=0, concat_axis=0, tiled=True)  21.5 us
    all_to_all x1, starting transfers between devices, body(): lax.all_to_all(slots, 'gx', split_axis=0, concat_axis=0, tiled=True)  7.51 us
    pallas_call x1, Pallas kernels, fields(): pl.pallas_call(field_kernel, out_shape=(field, field, field, field, jax.S...  6.36 us
    all_to_all x1, waiting for transfers between devices, body(): lax.all_to_all(slots, 'gx', split_axis=0, concat_axis=0, tiled=True)  4.29 us
    ppermute x2, starting transfers between devices, passed_along(): return lax.ppermute(block, axis, route)  3.61 us
    ppermute x2, waiting for transfers between devices, passed_along(): return lax.ppermute(block, axis, route)  2.3 us
  transfers between devices with their start and end apart: 3, of which 2 were waited for; matrix products, arithmetic and copies ran while one was open for 7% of the time, Pallas kernels for 0%

profile of v12, /device:TPU:0, one launch (start us, length us, event | category | flops | bytes accessed | tf_op | source)
XLA Modules:
  0.0 54.3 jit_solution(15111970847121827616)
XLA Ops:
  0.6 0.0 copy-start
  1.3 0.1 convert_reduce_fusion.1
  1.4 0.2 convert_reduce_fusion
  1.6 0.2 fusion.7
  1.8 0.4 fusion
  2.2 0.0 copy-start.2
  2.3 0.8 %broadcast_in_dim.4 = f32[16,32,256]{2,1,0:T(8,128)} broadcast(f32[32,256]{1,0:T(8,128)S(1)} %fusion), dimensions={1,2} | broadcast | bytes 557056 | tf_op jit(solution)/shard_map/broadcast_in_dim | solution.py:253
  3.1 7.5 %all-to-all-start = ((f32[16,32,256]{2,1,0:T(8,128)}), f32[16,32,256]{2,1,0:T(8,128)S(1)}, u32[]{:S(2)}, u32[]{:S(2)}) async-start(f32[16,32,256]{2,1,0:T(8,128)} %broadcast_in_dim.4), calls=%async_computation | async-start | bytes 1048576 | tf_op jit(solution)/shard_map/all_to_all | solution.py:254
  10.6 0.9 %slice_bitcast_fusion.2 = (f32[2,32,256]{2,1,0:T(8,128)S(1)}, f32[2,32,256]{2,1,0:T(8,128)S(1)}) fusion(f32[3,8,32,256]{3,2,1,0:T(8,128)} %ha_h.1, f32[3,8,32,256]{3,2,1,0:T(8,128)S(1)} %copy-done.2), kind=kLoop, calls=%fused_computation.15 | loop fusion | bytes 262144 | tf_op jit(solution)/shard_map/squeeze | solution.py:247
  11.5 0.0 copy-start.3
  11.5 1.0 %slice_bitcast_fusion = (f32[3,32,256]{2,1,0:T(8,128)S(1)}, f32[3,32,256]{2,1,0:T(8,128)S(1)}) fusion(f32[3,8,32,256]{3,2,1,0:T(8,128)} %ea_h.1, f32[3,8,32,256]{3,2,1,0:T(8,128)S(1)} %copy-done.1), kind=kLoop, calls=%fused_computation.13 | loop fusion | bytes 393216 | tf_op jit(solution)/shard_map/squeeze | solution.py:247
  12.5 0.7 %pad_maximum_fusion = f32[10,32,256]{2,1,0:T(8,128)} fusion(f32[3,32,256]{2,1,0:T(8,128)S(1)} %get-tuple-element.17, f32[2,32,256]{2,1,0:T(8,128)S(1)} %get-tuple-element.19, f32[3,32,256]{2,1,0:T(8,128)S(1)} %get-tuple-element.18, f32[2,32,256]{2,1,0:T(8,128)S(1)} %get-tuple-element.20), kind=kLoop, calls=%fused_computation.1 | loop fusion | flops 245760 | bytes 655360 | tf_op jit(solution)/shard_map/concatenate | solution.py:246
  13.3 2.3 %collective-permute-start.1 = (f32[10,32,256]{2,1,0:T(8,128)}, f32[10,32,256]{2,1,0:T(8,128)S(1)}, u32[]{:S(2)}, u32[]{:S(2)}) collective-permute-start(f32[10,32,256]{2,1,0:T(8,128)} %pad_maximum_fusion), channel_id=1, source_target_pairs={{0,1},{1,2},{2,3},{3,4},{4,5},{5,6},{6,7},{7,8},{8,9},{9,10},{10,1... | collective-permute-start | bytes 983048 | tf_op jit(solution)/shard_map/ppermute | solution.py:25
  15.6 0.9 %slice_bitcast_fusion.4 = (f32[2,32,256]{2,1,0:T(8,128)S(1)}, f32[2,32,256]{2,1,0:T(8,128)S(1)}) fusion(f32[3,8,32,256]{3,2,1,0:T(8,128)} %ea_h.1, f32[3,8,32,256]{3,2,1,0:T(8,128)S(1)} %copy-done.1), kind=kLoop, calls=%fused_computation.17 | loop fusion | bytes 262144 | tf_op jit(solution)/shard_map/squeeze | solution.py:244
  16.4 0.0 copy-start.6
  16.5 1.3 %collective-permute-start = (f32[4,32,256]{2,1,0:T(8,128)S(1)}, f32[4,32,256]{2,1,0:T(8,128)S(1)}, u32[]{:S(2)}, u32[]{:S(2)}) collective-permute-start(f32[4,32,256]{2,1,0:T(8,128)S(1)} %pad_maximum_fusion.1), channel_id=1, source_target_pairs={{1,0},{2,1},{3,2},{4,3},{5,4},{6,5},{7,6},{8,7},{9,8},{10,9},{11,1... | collective-permute-start | bytes 393224 | tf_op jit(solution)/shard_map/ppermute | solution.py:25
  18.4 0.0 copy-start.4
  18.4 0.1 copy.32.amp
  18.5 2.3 %collective-permute-done.upper = f32[4,32,256]{2,1,0:T(8,128)S(1)} collective-permute-done((f32[4,32,256]{2,1,0:T(8,128)S(1)}, f32[4,32,256]{2,1,0:T(8,128)S(1)}, u32[]{:S(2)}, u32[]{:S(2)}) %collective-permute-start) | collective-permute-done | bytes 131104 | tf_op jit(solution)/shard_map/ppermute | solution.py:25
  20.8 4.3 %all-to-all-done.arrived = f32[16,32,256]{2,1,0:T(8,128)S(1)} async-done(((f32[16,32,256]{2,1,0:T(8,128)}), f32[16,32,256]{2,1,0:T(8,128)S(1)}, u32[]{:S(2)}, u32[]{:S(2)}) %all-to-all-start) | async-done | bytes 524320 | tf_op jit(solution)/shard_map/all_to_all | solution.py:254
  25.1 6.4 %shard_map.173 = (f32[3,8,32,256]{3,2,1,0:T(8,128)}, f32[3,8,32,256]{3,2,1,0:T(8,128)}, f32[3,8,32,256]{3,2,1,0:T(8,128)}, f32[3,8,32,256]{3,2,1,0:T(8,128)}, f32[16,32,256]{2,1,0:T(8,128)S(1)}) custom-call(f32[3,8,32,256]{3,2,1,0:T(8,128)S(1)} %copy-done.1, f32[3,8,32,256]{3,2,1,0:T(8,128)S(1)} %copy-done.2, f32[3,8,32,256]{3,2,1,0:T(8,128)S(1)} %copy-done.3, ...), custom_call_target="tpu_custom_call" | custom-call | flops 13107200 | bytes 10485760 | tf_op jit(solution)/shard_map/pallas_call | solution.py:202
  31.5 21.5 %all_to_all.10 = f32[16,32,256]{2,1,0:T(8,128)S(1)} all-to-all(f32[16,32,256]{2,1,0:T(8,128)S(1)} %get-tuple-element.14), channel_id=1, replica_groups=mesh['grp'=2,'gx'=16] {'gx'}, dimensions={0} | all-to-all | bytes 1048576 | tf_op jit(solution)/shard_map/all_to_all | solution.py:259
  53.0 0.3 fusion.9
  53.3 0.9 %convolution_bitcast_fusion = f32[1,32,256]{2,1,0:T(8,128)} fusion(f32[32,256]{1,0:T(8,128)S(1)} %fusion.9, f32[256]{0:T(256)S(1)} %convert_reduce_fusion, s32[]{:T(128)} %bitcast), kind=kOutput, calls=%fused_computation | convolution fusion | flops 25559040 | bytes 66564 | tf_op jit(solution)/shard_map/xb,by->xy/dot_general | solution.py:261
  (12 shorter events, 0.1 us)
Async XLA Ops:
  0.6 0.9 %copy-start = (f32[1,32,256]{2,1,0:T(8,128)S(1)}, f32[1,32,256]{2,1,0:T(8,128)}, u32[]{:S(2)}) copy-start(f32[1,32,256]{2,1,0:T(8,128)} %param.22) | copy-start | bytes 98308
  2.2 8.4 %copy-start.2 = (f32[3,8,32,256]{3,2,1,0:T(8,128)S(1)}, f32[3,8,32,256]{3,2,1,0:T(8,128)}, u32[]{:S(2)}) copy-start(f32[3,8,32,256]{3,2,1,0:T(8,128)} %hf_h.1) | copy-start | bytes 2359300
  3.1 8.4 %copy-start.1 = (f32[3,8,32,256]{3,2,1,0:T(8,128)S(1)}, f32[3,8,32,256]{3,2,1,0:T(8,128)}, u32[]{:S(2)}) copy-start(f32[3,8,32,256]{3,2,1,0:T(8,128)} %ef_h.1) | copy-start | bytes 2359300
  3.1 22.0 %all-to-all-start = ((f32[16,32,256]{2,1,0:T(8,128)}), f32[16,32,256]{2,1,0:T(8,128)S(1)}, u32[]{:S(2)}, u32[]{:S(2)}) async-start(f32[16,32,256]{2,1,0:T(8,128)} %broadcast_in_dim.4), calls=%async_computation | async-start | bytes 1048576 | tf_op jit(solution)/shard_map/all_to_all | solution.py:254
  11.5 13.6 %copy-start.3 = (f32[3,8,32,256]{3,2,1,0:T(8,128)S(1)}, f32[3,8,32,256]{3,2,1,0:T(8,128)}, u32[]{:S(2)}) copy-start(f32[3,8,32,256]{3,2,1,0:T(8,128)} %pf_h.1) | copy-start | bytes 2359300
  13.3 7.6 %collective-permute-start.1 = (f32[10,32,256]{2,1,0:T(8,128)}, f32[10,32,256]{2,1,0:T(8,128)S(1)}, u32[]{:S(2)}, u32[]{:S(2)}) collective-permute-start(f32[10,32,256]{2,1,0:T(8,128)} %pad_maximum_fusion), channel_id=1, source_target_pairs={{0,1},{1,2},{2,3},{3,4},{4,5},{5,6},{6,7},{7,8},{8,9},{9,10},{10,1... | collective-permute-start | bytes 983048 | tf_op jit(solution)/shard_map/ppermute | solution.py:25
  16.4 2.0 %copy-start.6 = (f32[16,3]{0,1:T(4,128)S(1)}, f32[16,3]{0,1:T(4,128)}, u32[]{:S(2)}) copy-start(f32[16,3]{0,1:T(4,128)} %param.23) | copy-start | bytes 580
  16.5 4.4 %collective-permute-start = (f32[4,32,256]{2,1,0:T(8,128)S(1)}, f32[4,32,256]{2,1,0:T(8,128)S(1)}, u32[]{:S(2)}, u32[]{:S(2)}) collective-permute-start(f32[4,32,256]{2,1,0:T(8,128)S(1)} %pad_maximum_fusion.1), channel_id=1, source_target_pairs={{1,0},{2,1},{3,2},{4,3},{5,4},{6,5},{7,6},{8,7},{9,8},{10,9},{11,1... | collective-permute-start | bytes 393224 | tf_op jit(solution)/shard_map/ppermute | solution.py:25
  18.4 6.7 %copy-start.4 = (s32[16]{0:T(128)S(1)}, s32[16]{0:T(128)}, u32[]{:S(2)}) copy-start(s32[16]{0:T(128)} %src.1) | copy-start | bytes 196
  18.4 6.7 %copy-start.5 = (s32[16]{0:T(128)S(1)}, s32[16]{0:T(128)}, u32[]{:S(2)}) copy-start(s32[16]{0:T(128)} %mon.1) | copy-start | bytes 196

commit v13 on v8

--- a/solution.py
+++ b/solution.py
@@ -40,6 +40,19 @@
 def smooth_adjoint(wx, wy, planes):
     inner = jnp.einsum("ax,zab->zxb", wx, planes, precision=HIGH)
     return jnp.einsum("zxb,by->zxy", inner, wy, precision=HIGH)
+
+
+def split_cell(cell, width_x, width_y):
+    plane = width_x * width_y
+    if plane & (plane - 1) == 0 and width_y & (width_y - 1) == 0:
+        zz = lax.shift_right_arithmetic(cell, plane.bit_length() - 1)
+        rest = lax.bitwise_and(cell, plane - 1)
+        x = lax.shift_right_arithmetic(rest, width_y.bit_length() - 1)
+        return zz, x, lax.bitwise_and(rest, width_y - 1)
+    zz = cell // plane
+    rest = cell - zz * plane
+    x = rest // width_y
+    return zz, x, rest - x * width_y
 
 
 def shifts(width_x, width_y):
@@ -121,12 +134,9 @@
     tile_lane = lax.broadcasted_iota(jnp.int32, (8, width_y), 1)
 
     def add_at(cell, out, value_of):
-        zz = cell // plane
+        zz, x, y = split_cell(cell, width_x, width_y)
         local = zz - index * depth
-        rest = cell - zz * plane
-        x = rest // width_y
-        y = rest - x * width_y
-        x0 = pl.multiple_of((x // 8) * 8, 8)
+        x0 = pl.multiple_of(x - lax.bitwise_and(x, 7), 8)
 
         @pl.when((local >= 0) & (local < depth))
         def _():
@@ -180,7 +190,7 @@
         in_specs=[vmem] * 10 + [smem] * 4,
         out_specs=(vmem,) * 3,
         scratch_shapes=[pltpu.VMEM(shape[1:], jnp.float32)],
-        compiler_params=pltpu.CompilerParams(vmem_limit_bytes=56 * 1024 * 1024),
+        compiler_params=pltpu.CompilerParams(vmem_limit_bytes=52 * 1024 * 1024),
         cost_estimate=pl.CostEstimate(
             flops=140 * cells, bytes_accessed=4 * cells * 30, transcendentals=0
         ),

time: 57.6 us -> 56.7 us (0.984)
  Pallas kernels: 8.47 us -> 6.59 us
  waiting for transfers between devices: 4.26 us -> 5.82 us
  other arithmetic: 1.72 us -> 1.06 us
    all_to_all x1, waiting for transfers between devices: 2.19 us -> 3.49 us  [body(): lax.all_to_all(slots, 'gx', split_axis=0, concat_axis=0, tiled=True)]
    pallas_call x1, Pallas kernels: 6.14 us -> 5.15 us  [fields(): pl.pallas_call(e_kernel, out_shape=(field, field, jax.ShapeDtypeStruct(ar...]
    pallas_call x1, Pallas kernels: 2.33 us -> 1.44 us  [fields(): pl.pallas_call(h_kernel, out_shape=(field, field, jax.ShapeDtypeStruct((4...]
    concatenate x1, other arithmetic: 0.67 us -> 0.01 us  [body(): jnp.concatenate([e_forward[0:2, 0], e_adjoint[0:2, 0]], 0)]
    unnamed x15 -> x17, local copies, waits for them, and re-layouts: 1.37 us -> 1.92 us
  transfers between devices with their start and end apart: 3 -> 3, of which waited for: 2 -> 2; matrix products, arithmetic and copies ran while one was open for 5% -> 3% of each run, Pallas kernels for 4% -> 3%
where the time goes in v13:
time: 56.7 us; the launch traced here: 56.2 us
  blocking collectives  24 us (42%)
  starting transfers between devices  11.1 us (20%)
  Pallas kernels  6.59 us (12%)
  waiting for transfers between devices  5.82 us (10%)
  local copies, waits for them, and re-layouts  3.65 us (6%)
  between operations  2.08 us (4%)
  matrix products  1.88 us (3%)
  other arithmetic  1.06 us (2%)
    all_to_all x1, blocking collectives, body(): lax.all_to_all(returned, 'gx', split_axis=0, concat_axis=0, tiled=True)  24 us
    all_to_all x1, starting transfers between devices, body(): lax.all_to_all(slots, 'gx', split_axis=0, concat_axis=0, tiled=True)  7.52 us
    pallas_call x1, Pallas kernels, fields(): pl.pallas_call(e_kernel, out_shape=(field, field, jax.ShapeDtypeStruct(ar...  5.15 us
    ppermute x2, starting transfers between devices, passed_along(): return lax.ppermute(block, axis, route)  3.61 us
    all_to_all x1, waiting for transfers between devices, body(): lax.all_to_all(slots, 'gx', split_axis=0, concat_axis=0, tiled=True)  3.49 us
    ppermute x2, waiting for transfers between devices, passed_along(): return lax.ppermute(block, axis, route)  2.32 us
    unnamed x17, local copies, waits for them, and re-layouts  1.92 us
    pallas_call x1, Pallas kernels, fields(): pl.pallas_call(h_kernel, out_shape=(field, field, jax.ShapeDtypeStruct((4...  1.44 us
  transfers between devices with their start and end apart: 3, of which 2 were waited for; matrix products, arithmetic and copies ran while one was open for 3% of the time, Pallas kernels for 3%

profile of v13, /device:TPU:0, one launch (start us, length us, event | category | flops | bytes accessed | tf_op | source)
XLA Modules:
  0.0 56.2 jit_solution(15729118906973871799)
XLA Ops:
  0.6 0.0 copy-start
  1.3 0.1 convert_reduce_fusion.1
  1.4 0.2 convert_reduce_fusion
  1.6 0.2 fusion.7
  1.8 0.0 copy-start.3
  1.8 0.4 fusion
  2.3 0.0 copy-start.2
  2.3 0.8 %broadcast_in_dim.4 = f32[16,32,256]{2,1,0:T(8,128)} broadcast(f32[32,256]{1,0:T(8,128)S(1)} %fusion), dimensions={1,2} | broadcast | bytes 557056 | tf_op jit(solution)/shard_map/broadcast_in_dim | solution.py:233
  3.1 7.5 %all-to-all-start = ((f32[16,32,256]{2,1,0:T(8,128)}), f32[16,32,256]{2,1,0:T(8,128)S(1)}, u32[]{:S(2)}, u32[]{:S(2)}) async-start(f32[16,32,256]{2,1,0:T(8,128)} %broadcast_in_dim.4), calls=%async_computation | async-start | bytes 1048576 | tf_op jit(solution)/shard_map/all_to_all | solution.py:234
  10.6 0.9 %slice_bitcast_fusion.2 = (f32[2,32,256]{2,1,0:T(8,128)S(1)}, f32[2,32,256]{2,1,0:T(8,128)S(1)}) fusion(f32[3,8,32,256]{3,2,1,0:T(8,128)} %ha.1, f32[3,8,32,256]{3,2,1,0:T(8,128)S(1)} %copy-done.3), kind=kLoop, calls=%fused_computation.15 | loop fusion | bytes 262144 | tf_op jit(solution)/shard_map/squeeze | solution.py:227
  11.6 0.7 %pad_maximum_fusion = f32[10,32,256]{2,1,0:T(8,128)} fusion(f32[3,32,256]{2,1,0:T(8,128)S(1)} %get-tuple-element.19, f32[2,32,256]{2,1,0:T(8,128)S(1)} %get-tuple-element.21, f32[3,32,256]{2,1,0:T(8,128)S(1)} %get-tuple-element.20, f32[2,32,256]{2,1,0:T(8,128)S(1)} %get-tuple-element.22), kind=kLoop, calls=%fused_computation.1 | loop fusion | flops 245760 | bytes 655360 | tf_op jit(solution)/shard_map/concatenate | solution.py:226
  12.3 2.3 %collective-permute-start.1 = (f32[10,32,256]{2,1,0:T(8,128)}, f32[10,32,256]{2,1,0:T(8,128)S(1)}, u32[]{:S(2)}, u32[]{:S(2)}) collective-permute-start(f32[10,32,256]{2,1,0:T(8,128)} %pad_maximum_fusion), channel_id=1, source_target_pairs={{0,1},{1,2},{2,3},{3,4},{4,5},{5,6},{6,7},{7,8},{8,9},{9,10},{10,1... | collective-permute-start | bytes 983048 | tf_op jit(solution)/shard_map/ppermute | solution.py:25
  14.7 1.3 %collective-permute-start = (f32[4,32,256]{2,1,0:T(8,128)S(1)}, f32[4,32,256]{2,1,0:T(8,128)S(1)}, u32[]{:S(2)}, u32[]{:S(2)}) collective-permute-start(f32[4,32,256]{2,1,0:T(8,128)S(1)} %pad_maximum_fusion.1), channel_id=1, source_target_pairs={{1,0},{2,1},{3,2},{4,3},{5,4},{6,5},{7,6},{8,7},{9,8},{10,9},{11,1... | collective-permute-start | bytes 393224 | tf_op jit(solution)/shard_map/ppermute | solution.py:25
  16.6 0.1 copy.32.amp
  16.7 2.3 %collective-permute-done.upper = f32[4,32,256]{2,1,0:T(8,128)S(1)} collective-permute-done((f32[4,32,256]{2,1,0:T(8,128)S(1)}, f32[4,32,256]{2,1,0:T(8,128)S(1)}, u32[]{:S(2)}, u32[]{:S(2)}) %collective-permute-start) | collective-permute-done | bytes 131104 | tf_op jit(solution)/shard_map/ppermute | solution.py:25
  19.0 1.1 %copy-done.4 = f32[3,8,32,256]{3,2,1,0:T(8,128)S(1)} copy-done((f32[3,8,32,256]{3,2,1,0:T(8,128)S(1)}, f32[3,8,32,256]{3,2,1,0:T(8,128)}, u32[]{:S(2)}) %copy-start.4) | copy-done | bytes 786456
  20.2 1.4 %shard_map.173 = (f32[3,8,32,256]{3,2,1,0:T(8,128)}, f32[3,8,32,256]{3,2,1,0:T(8,128)}, f32[4,32,256]{2,1,0:T(8,128)S(1)}) custom-call(f32[3,8,32,256]{3,2,1,0:T(8,128)S(1)} %copy-done.1, f32[3,8,32,256]{3,2,1,0:T(8,128)S(1)} %copy-done.3, f32[3,8,32,256]{3,2,1,0:T(8,128)S(1)} %copy-done.2, f32[3,8,32,256]{3,2,1,0:T(8,128)S(1)} %copy-done.4, ...), custom_call_target="tpu_custom_call" | custom-call | flops 3932160 | bytes 4718592 | tf_op jit(solution)/shard_map/pallas_call | solution.py:177
  21.6 3.5 %all-to-all-done.arrived = f32[16,32,256]{2,1,0:T(8,128)S(1)} async-done(((f32[16,32,256]{2,1,0:T(8,128)}), f32[16,32,256]{2,1,0:T(8,128)S(1)}, u32[]{:S(2)}, u32[]{:S(2)}) %all-to-all-start) | async-done | bytes 524320 | tf_op jit(solution)/shard_map/all_to_all | solution.py:234
  25.1 0.7 %copy-done.5 = s32[16]{0:T(128)S(1)} copy-done((s32[16]{0:T(128)S(1)}, s32[16]{0:T(128)}, u32[]{:S(2)}) %copy-start.5) | copy-done | bytes 88
  25.8 0.0 copy-done.6
  25.8 5.2 %shard_map.174 = (f32[3,8,32,256]{3,2,1,0:T(8,128)}, f32[3,8,32,256]{3,2,1,0:T(8,128)}, f32[16,32,256]{2,1,0:T(8,128)S(1)}) custom-call(f32[3,8,32,256]{3,2,1,0:T(8,128)S(1)} %copy-done.1, f32[3,8,32,256]{3,2,1,0:T(8,128)} %pf.1, f32[3,8,32,256]{3,2,1,0:T(8,128)} %jf.1, f32[3,8,32,256]{3,2,1,0:T(8,128)} %ea.3, f32[3,8,32,256]{3,2,1,0:T(8,128)} %pa.1, ...), custom_call_target="tpu_custom_call" | custom-call | flops 9175040 | bytes 7864320 | tf_op jit(solution)/shard_map/pallas_call | solution.py:187
  30.9 24.0 %all_to_all.10 = f32[16,32,256]{2,1,0:T(8,128)S(1)} all-to-all(f32[16,32,256]{2,1,0:T(8,128)S(1)} %get-tuple-element.16), channel_id=1, replica_groups=mesh['grp'=2,'gx'=16] {'gx'}, dimensions={0} | all-to-all | bytes 1048576 | tf_op jit(solution)/shard_map/all_to_all | solution.py:239
  54.9 0.3 fusion.9
  55.2 0.9 %convolution_bitcast_fusion = f32[1,32,256]{2,1,0:T(8,128)} fusion(f32[32,256]{1,0:T(8,128)S(1)} %fusion.9, f32[256]{0:T(256)S(1)} %convert_reduce_fusion, s32[]{:T(128)} %bitcast.6), kind=kOutput, calls=%fused_computation | convolution fusion | flops 25559040 | bytes 66564 | tf_op jit(solution)/shard_map/xb,by->xy/dot_general | solution.py:241
  (15 shorter events, 0.1 us)
Async XLA Ops:
  0.6 0.9 %copy-start = (f32[1,32,256]{2,1,0:T(8,128)S(1)}, f32[1,32,256]{2,1,0:T(8,128)}, u32[]{:S(2)}) copy-start(f32[1,32,256]{2,1,0:T(8,128)} %param.22) | copy-start | bytes 98308
  1.8 8.8 %copy-start.3 = (f32[3,8,32,256]{3,2,1,0:T(8,128)S(1)}, f32[3,8,32,256]{3,2,1,0:T(8,128)}, u32[]{:S(2)}) copy-start(f32[3,8,32,256]{3,2,1,0:T(8,128)} %hf.1) | copy-start | bytes 2359300
  2.3 9.3 %copy-start.2 = (f32[3,8,32,256]{3,2,1,0:T(8,128)S(1)}, f32[3,8,32,256]{3,2,1,0:T(8,128)}, u32[]{:S(2)}) copy-start(f32[3,8,32,256]{3,2,1,0:T(8,128)} %ea.3) | copy-start | bytes 2359300
  3.1 8.4 %copy-start.1 = (f32[3,8,32,256]{3,2,1,0:T(8,128)S(1)}, f32[3,8,32,256]{3,2,1,0:T(8,128)}, u32[]{:S(2)}) copy-start(f32[3,8,32,256]{3,2,1,0:T(8,128)} %ef.3) | copy-start | bytes 2359300
  3.1 22.0 %all-to-all-start = ((f32[16,32,256]{2,1,0:T(8,128)}), f32[16,32,256]{2,1,0:T(8,128)S(1)}, u32[]{:S(2)}, u32[]{:S(2)}) async-start(f32[16,32,256]{2,1,0:T(8,128)} %broadcast_in_dim.4), calls=%async_computation | async-start | bytes 1048576 | tf_op jit(solution)/shard_map/all_to_all | solution.py:234
  12.3 6.7 %collective-permute-start.1 = (f32[10,32,256]{2,1,0:T(8,128)}, f32[10,32,256]{2,1,0:T(8,128)S(1)}, u32[]{:S(2)}, u32[]{:S(2)}) collective-permute-start(f32[10,32,256]{2,1,0:T(8,128)} %pad_maximum_fusion), channel_id=1, source_target_pairs={{0,1},{1,2},{2,3},{3,4},{4,5},{5,6},{6,7},{7,8},{8,9},{9,10},{10,1... | collective-permute-start | bytes 983048 | tf_op jit(solution)/shard_map/ppermute | solution.py:25
  14.6 2.0 %copy-start.7 = (f32[16,3]{0,1:T(4,128)S(1)}, f32[16,3]{0,1:T(4,128)}, u32[]{:S(2)}) copy-start(f32[16,3]{0,1:T(4,128)} %param.23) | copy-start | bytes 580
  14.7 4.4 %collective-permute-start = (f32[4,32,256]{2,1,0:T(8,128)S(1)}, f32[4,32,256]{2,1,0:T(8,128)S(1)}, u32[]{:S(2)}, u32[]{:S(2)}) collective-permute-start(f32[4,32,256]{2,1,0:T(8,128)S(1)} %pad_maximum_fusion.1), channel_id=1, source_target_pairs={{1,0},{2,1},{3,2},{4,3},{5,4},{6,5},{7,6},{8,7},{9,8},{10,9},{11,1... | collective-permute-start | bytes 393224 | tf_op jit(solution)/shard_map/ppermute | solution.py:25
  19.0 1.1 %copy-start.4 = (f32[3,8,32,256]{3,2,1,0:T(8,128)S(1)}, f32[3,8,32,256]{3,2,1,0:T(8,128)}, u32[]{:S(2)}) copy-start(f32[3,8,32,256]{3,2,1,0:T(8,128)} %ha.1) | copy-start | bytes 2359300
  25.1 0.7 %copy-start.5 = (s32[16]{0:T(128)S(1)}, s32[16]{0:T(128)}, u32[]{:S(2)}) copy-start(s32[16]{0:T(128)} %src.1) | copy-start | bytes 196
  25.1 0.7 %copy-start.6 = (s32[16]{0:T(128)S(1)}, s32[16]{0:T(128)}, u32[]{:S(2)}) copy-start(s32[16]{0:T(128)} %mon.1) | copy-start | bytes 196

commit v14 on v11

--- a/solution.py
+++ b/solution.py
@@ -57,9 +57,17 @@
 
 def field_kernel(
     ef, hf, pf, jf, ea, ha, pa, ja, arrived, upper, below, src, mon, amp, first,
-    ef_o, hf_o, ea_o, ha_o, ret_o, rho,
+    ef_oh, hf_oh, ea_oh, ha_oh, ret_o, rho, outs, out_sem,
 ):
     depth, width_x, width_y = rho.shape
+    ef_o, hf_o, ea_o, ha_o = (outs.at[a] for a in range(4))
+    targets = (ef_oh, hf_oh, ea_oh, ha_oh)
+
+    def store(a, z):
+        return pltpu.make_async_copy(
+            outs.at[a, :, pl.ds(z, 1)], targets[a].at[:, pl.ds(z, 1)], out_sem.at[a, z]
+        )
+
     slab = arrived.shape[0]
     index = lax.axis_index("gx")
     start = first[0]
@@ -125,6 +133,7 @@
             hn = new_h(e, h, z, ex_up, ey_up)
             for c in range(3):
                 h_out[c, z] = hn[c]
+            store(2 * r + 1, z).start()
             new_e(e, p, j, e_out, z, hn, prev[r], step, strength)
             prev[r] = (hn[0], hn[1])
 
@@ -151,6 +160,9 @@
     for m in range(mon.shape[0]):
         add_at(mon[m], ea_o, lambda c, local, rows: ef[c, local, rows, :])
 
+    for z in range(depth):
+        store(0, z).start()
+        store(2, z).start()
     for g in range(slab):
         ret_o[g] = jnp.zeros((width_x, width_y), jnp.float32)
     for z in range(depth):
@@ -164,6 +176,10 @@
         @pl.when((p >= 0) & (p < slab))
         def _():
             ret_o[jnp.clip(p, 0, slab - 1)] = total
+
+    for z in range(depth):
+        for a in range(4):
+            store(a, z).wait()
 
 
 def fields(e_forward, h_forward, p_forward, j_forward, e_adjoint, h_adjoint, p_adjoint, j_adjoint,
@@ -178,8 +194,12 @@
         field_kernel,
         out_shape=(field, field, field, field, jax.ShapeDtypeStruct(arrived.shape, jnp.float32)),
         in_specs=[vmem] * 11 + [smem] * 4,
-        out_specs=(vmem,) * 5,
-        scratch_shapes=[pltpu.VMEM(shape[1:], jnp.float32)],
+        out_specs=(pl.BlockSpec(memory_space=pl.ANY),) * 4 + (vmem,),
+        scratch_shapes=[
+            pltpu.VMEM(shape[1:], jnp.float32),
+            pltpu.VMEM((4,) + shape, jnp.float32),
+            pltpu.SemaphoreType.DMA((4, depth)),
+        ],
         compiler_params=pltpu.CompilerParams(vmem_limit_bytes=50 * 1024 * 1024),
         cost_estimate=pl.CostEstimate(
             flops=200 * cells, bytes_accessed=4 * cells * 40, transcendentals=0

time: 54.4 us -> 54.1 us (level)
  no operation moved by 1% of the time
where the time goes in v14:
time: 54.1 us; the launch traced here: 53.6 us
  blocking collectives  21.5 us (40%)
  starting transfers between devices  11.1 us (21%)
  waiting for transfers between devices  6.59 us (12%)
  Pallas kernels  5.66 us (10%)
  local copies, waits for them, and re-layouts  3.67 us (7%)
  between operations  2.09 us (4%)
  matrix products  1.88 us (3%)
  other arithmetic  1.06 us (2%)
    all_to_all x1, blocking collectives, body(): lax.all_to_all(returned, 'gx', split_axis=0, concat_axis=0, tiled=True)  21.5 us
    all_to_all x1, starting transfers between devices, body(): lax.all_to_all(slots, 'gx', split_axis=0, concat_axis=0, tiled=True)  7.51 us
    pallas_call x1, Pallas kernels, fields(): pl.pallas_call(field_kernel, out_shape=(field, field, field, field, jax.S...  5.66 us
    all_to_all x1, waiting for transfers between devices, body(): lax.all_to_all(slots, 'gx', split_axis=0, concat_axis=0, tiled=True)  4.29 us
    ppermute x2, starting transfers between devices, passed_along(): return lax.ppermute(block, axis, route)  3.61 us
    ppermute x2, waiting for transfers between devices, passed_along(): return lax.ppermute(block, axis, route)  2.3 us
  transfers between devices with their start and end apart: 3, of which 2 were waited for; matrix products, arithmetic and copies ran while one was open for 7% of the time, Pallas kernels for 0%

profile of v14, /device:TPU:0, one launch (start us, length us, event | category | flops | bytes accessed | tf_op | source)
XLA Modules:
  0.0 53.6 jit_solution(13743545085122627245)
XLA Ops:
  0.6 0.0 copy-start
  1.3 0.1 convert_reduce_fusion.1
  1.4 0.2 convert_reduce_fusion
  1.6 0.2 fusion.7
  1.8 0.4 fusion
  2.2 0.0 copy-start.2
  2.3 0.8 %broadcast_in_dim.4 = f32[16,32,256]{2,1,0:T(8,128)} broadcast(f32[32,256]{1,0:T(8,128)S(1)} %fusion), dimensions={1,2} | broadcast | bytes 557056 | tf_op jit(solution)/shard_map/broadcast_in_dim | solution.py:242
  3.1 7.5 %all-to-all-start = ((f32[16,32,256]{2,1,0:T(8,128)}), f32[16,32,256]{2,1,0:T(8,128)S(1)}, u32[]{:S(2)}, u32[]{:S(2)}) async-start(f32[16,32,256]{2,1,0:T(8,128)} %broadcast_in_dim.4), calls=%async_computation | async-start | bytes 1048576 | tf_op jit(solution)/shard_map/all_to_all | solution.py:243
  10.6 0.9 %slice_bitcast_fusion.2 = (f32[2,32,256]{2,1,0:T(8,128)S(1)}, f32[2,32,256]{2,1,0:T(8,128)S(1)}) fusion(f32[3,8,32,256]{3,2,1,0:T(8,128)} %ha.1, f32[3,8,32,256]{3,2,1,0:T(8,128)S(1)} %copy-done.2), kind=kLoop, calls=%fused_computation.15 | loop fusion | bytes 262144 | tf_op jit(solution)/shard_map/squeeze | solution.py:236
  11.5 0.0 copy-start.3
  11.5 1.0 %slice_bitcast_fusion = (f32[3,32,256]{2,1,0:T(8,128)S(1)}, f32[3,32,256]{2,1,0:T(8,128)S(1)}) fusion(f32[3,8,32,256]{3,2,1,0:T(8,128)} %ea.1, f32[3,8,32,256]{3,2,1,0:T(8,128)S(1)} %copy-done.1), kind=kLoop, calls=%fused_computation.13 | loop fusion | bytes 393216 | tf_op jit(solution)/shard_map/squeeze | solution.py:236
  12.5 0.7 %pad_maximum_fusion = f32[10,32,256]{2,1,0:T(8,128)} fusion(f32[3,32,256]{2,1,0:T(8,128)S(1)} %get-tuple-element.17, f32[2,32,256]{2,1,0:T(8,128)S(1)} %get-tuple-element.19, f32[3,32,256]{2,1,0:T(8,128)S(1)} %get-tuple-element.18, f32[2,32,256]{2,1,0:T(8,128)S(1)} %get-tuple-element.20), kind=kLoop, calls=%fused_computation.1 | loop fusion | flops 245760 | bytes 655360 | tf_op jit(solution)/shard_map/concatenate | solution.py:235
  13.3 2.3 %collective-permute-start.1 = (f32[10,32,256]{2,1,0:T(8,128)}, f32[10,32,256]{2,1,0:T(8,128)S(1)}, u32[]{:S(2)}, u32[]{:S(2)}) collective-permute-start(f32[10,32,256]{2,1,0:T(8,128)} %pad_maximum_fusion), channel_id=1, source_target_pairs={{0,1},{1,2},{2,3},{3,4},{4,5},{5,6},{6,7},{7,8},{8,9},{9,10},{10,1... | collective-permute-start | bytes 983048 | tf_op jit(solution)/shard_map/ppermute | solution.py:25
  15.6 0.9 %slice_bitcast_fusion.4 = (f32[2,32,256]{2,1,0:T(8,128)S(1)}, f32[2,32,256]{2,1,0:T(8,128)S(1)}) fusion(f32[3,8,32,256]{3,2,1,0:T(8,128)} %ea.1, f32[3,8,32,256]{3,2,1,0:T(8,128)S(1)} %copy-done.1), kind=kLoop, calls=%fused_computation.17 | loop fusion | bytes 262144 | tf_op jit(solution)/shard_map/squeeze | solution.py:233
  16.5 1.3 %collective-permute-start = (f32[4,32,256]{2,1,0:T(8,128)S(1)}, f32[4,32,256]{2,1,0:T(8,128)S(1)}, u32[]{:S(2)}, u32[]{:S(2)}) collective-permute-start(f32[4,32,256]{2,1,0:T(8,128)S(1)} %pad_maximum_fusion.1), channel_id=1, source_target_pairs={{1,0},{2,1},{3,2},{4,3},{5,4},{6,5},{7,6},{8,7},{9,8},{10,9},{11,1... | collective-permute-start | bytes 393224 | tf_op jit(solution)/shard_map/ppermute | solution.py:25
  18.4 0.0 copy-start.4
  18.4 0.0 copy-start.5
  18.4 0.1 copy.32.amp
  18.5 2.3 %collective-permute-done.upper = f32[4,32,256]{2,1,0:T(8,128)S(1)} collective-permute-done((f32[4,32,256]{2,1,0:T(8,128)S(1)}, f32[4,32,256]{2,1,0:T(8,128)S(1)}, u32[]{:S(2)}, u32[]{:S(2)}) %collective-permute-start) | collective-permute-done | bytes 131104 | tf_op jit(solution)/shard_map/ppermute | solution.py:25
  20.8 4.3 %all-to-all-done.arrived = f32[16,32,256]{2,1,0:T(8,128)S(1)} async-done(((f32[16,32,256]{2,1,0:T(8,128)}), f32[16,32,256]{2,1,0:T(8,128)S(1)}, u32[]{:S(2)}, u32[]{:S(2)}) %all-to-all-start) | async-done | bytes 524320 | tf_op jit(solution)/shard_map/all_to_all | solution.py:243
  25.1 5.7 %shard_map.173 = (f32[3,8,32,256]{3,2,1,0:T(8,128)}, f32[3,8,32,256]{3,2,1,0:T(8,128)}, f32[3,8,32,256]{3,2,1,0:T(8,128)}, f32[3,8,32,256]{3,2,1,0:T(8,128)}, f32[16,32,256]{2,1,0:T(8,128)S(1)}) custom-call(f32[3,8,32,256]{3,2,1,0:T(8,128)S(1)} %copy-done.1, f32[3,8,32,256]{3,2,1,0:T(8,128)S(1)} %copy-done.2, f32[3,8,32,256]{3,2,1,0:T(8,128)S(1)} %copy-done.3, ...), custom_call_target="tpu_custom_call" | custom-call | flops 13107200 | bytes 10485760 | tf_op jit(solution)/shard_map/pallas_call | solution.py:193
  30.8 21.5 %all_to_all.10 = f32[16,32,256]{2,1,0:T(8,128)S(1)} all-to-all(f32[16,32,256]{2,1,0:T(8,128)S(1)} %get-tuple-element.14), channel_id=1, replica_groups=mesh['grp'=2,'gx'=16] {'gx'}, dimensions={0} | all-to-all | bytes 1048576 | tf_op jit(solution)/shard_map/all_to_all | solution.py:248
  52.3 0.3 fusion.9
  52.6 0.9 %convolution_bitcast_fusion = f32[1,32,256]{2,1,0:T(8,128)} fusion(f32[32,256]{1,0:T(8,128)S(1)} %fusion.9, f32[256]{0:T(256)S(1)} %convert_reduce_fusion, s32[]{:T(128)} %bitcast), kind=kOutput, calls=%fused_computation | convolution fusion | flops 25559040 | bytes 66564 | tf_op jit(solution)/shard_map/xb,by->xy/dot_general | solution.py:250
  (12 shorter events, 0.1 us)
Async XLA Ops:
  0.6 0.9 %copy-start = (f32[1,32,256]{2,1,0:T(8,128)S(1)}, f32[1,32,256]{2,1,0:T(8,128)}, u32[]{:S(2)}) copy-start(f32[1,32,256]{2,1,0:T(8,128)} %param.22) | copy-start | bytes 98308
  2.2 8.4 %copy-start.2 = (f32[3,8,32,256]{3,2,1,0:T(8,128)S(1)}, f32[3,8,32,256]{3,2,1,0:T(8,128)}, u32[]{:S(2)}) copy-start(f32[3,8,32,256]{3,2,1,0:T(8,128)} %hf.1) | copy-start | bytes 2359300
  3.1 8.4 %copy-start.1 = (f32[3,8,32,256]{3,2,1,0:T(8,128)S(1)}, f32[3,8,32,256]{3,2,1,0:T(8,128)}, u32[]{:S(2)}) copy-start(f32[3,8,32,256]{3,2,1,0:T(8,128)} %ef.1) | copy-start | bytes 2359300
  3.1 22.0 %all-to-all-start = ((f32[16,32,256]{2,1,0:T(8,128)}), f32[16,32,256]{2,1,0:T(8,128)S(1)}, u32[]{:S(2)}, u32[]{:S(2)}) async-start(f32[16,32,256]{2,1,0:T(8,128)} %broadcast_in_dim.4), calls=%async_computation | async-start | bytes 1048576 | tf_op jit(solution)/shard_map/all_to_all | solution.py:243
  11.5 13.6 %copy-start.3 = (f32[3,8,32,256]{3,2,1,0:T(8,128)S(1)}, f32[3,8,32,256]{3,2,1,0:T(8,128)}, u32[]{:S(2)}) copy-start(f32[3,8,32,256]{3,2,1,0:T(8,128)} %pf.1) | copy-start | bytes 2359300
  13.3 7.6 %collective-permute-start.1 = (f32[10,32,256]{2,1,0:T(8,128)}, f32[10,32,256]{2,1,0:T(8,128)S(1)}, u32[]{:S(2)}, u32[]{:S(2)}) collective-permute-start(f32[10,32,256]{2,1,0:T(8,128)} %pad_maximum_fusion), channel_id=1, source_target_pairs={{0,1},{1,2},{2,3},{3,4},{4,5},{5,6},{6,7},{7,8},{8,9},{9,10},{10,1... | collective-permute-start | bytes 983048 | tf_op jit(solution)/shard_map/ppermute | solution.py:25
  16.4 2.0 %copy-start.6 = (f32[16,3]{0,1:T(4,128)S(1)}, f32[16,3]{0,1:T(4,128)}, u32[]{:S(2)}) copy-start(f32[16,3]{0,1:T(4,128)} %param.23) | copy-start | bytes 580
  16.5 4.4 %collective-permute-start = (f32[4,32,256]{2,1,0:T(8,128)S(1)}, f32[4,32,256]{2,1,0:T(8,128)S(1)}, u32[]{:S(2)}, u32[]{:S(2)}) collective-permute-start(f32[4,32,256]{2,1,0:T(8,128)S(1)} %pad_maximum_fusion.1), channel_id=1, source_target_pairs={{1,0},{2,1},{3,2},{4,3},{5,4},{6,5},{7,6},{8,7},{9,8},{10,9},{11,1... | collective-permute-start | bytes 393224 | tf_op jit(solution)/shard_map/ppermute | solution.py:25
  18.4 6.7 %copy-start.4 = (s32[16]{0:T(128)S(1)}, s32[16]{0:T(128)}, u32[]{:S(2)}) copy-start(s32[16]{0:T(128)} %src.1) | copy-start | bytes 196
  18.4 6.7 %copy-start.5 = (s32[16]{0:T(128)S(1)}, s32[16]{0:T(128)}, u32[]{:S(2)}) copy-start(s32[16]{0:T(128)} %mon.1) | copy-start | bytes 196

commit v15 on v14

--- a/solution.py
+++ b/solution.py
@@ -120,11 +120,7 @@
             out[c, z] = e[c, z] + step * (curl[c] - j_next)
 
     runs = ((ef, hf, pf, jf, hf_o, ef_o, 0), (ea, ha, pa, ja, ha_o, ea_o, 2))
-    prev = [lower_h(ef, 0), lower_h(ea, 5)]
-    for z in range(depth):
-        density = rho[z]
-        step = DT / (1.0 + EPS_RANGE * density)
-        strength = STRENGTH_BASE + STRENGTH_RANGE * density
+    for z in range(depth):
         for r, (e, h, p, j, h_out, e_out, up) in enumerate(runs):
             if z + 1 < depth:
                 ex_up, ey_up = e[0, z + 1], e[1, z + 1]
@@ -134,8 +130,15 @@
             for c in range(3):
                 h_out[c, z] = hn[c]
             store(2 * r + 1, z).start()
-            new_e(e, p, j, e_out, z, hn, prev[r], step, strength)
-            prev[r] = (hn[0], hn[1])
+    prev = [lower_h(ef, 0), lower_h(ea, 5)]
+    for z in range(depth):
+        density = rho[z]
+        step = DT / (1.0 + EPS_RANGE * density)
+        strength = STRENGTH_BASE + STRENGTH_RANGE * density
+        for r, (e, h, p, j, h_out, e_out, up) in enumerate(runs):
+            hn = (h_out[0, z], h_out[1, z], h_out[2, z])
+            hn_dn = prev[r] if z == 0 else (h_out[0, z - 1], h_out[1, z - 1])
+            new_e(e, p, j, e_out, z, hn, hn_dn, step, strength)
 
     plane = width_x * width_y
     tile_row = lax.broadcasted_iota(jnp.int32, (8, width_y), 0)

time: 54.1 us -> 53.7 us (level)
  no operation moved by 1% of the time
where the time goes in v15:
time: 53.7 us; the launch traced here: 53.2 us
  blocking collectives  21.5 us (40%)
  starting transfers between devices  11.1 us (21%)
  waiting for transfers between devices  6.59 us (12%)
  Pallas kernels  5.38 us (10%)
  local copies, waits for them, and re-layouts  3.67 us (7%)
  between operations  2.09 us (4%)
  matrix products  1.88 us (4%)
  other arithmetic  1.06 us (2%)
    all_to_all x1, blocking collectives, body(): lax.all_to_all(returned, 'gx', split_axis=0, concat_axis=0, tiled=True)  21.5 us
    all_to_all x1, starting transfers between devices, body(): lax.all_to_all(slots, 'gx', split_axis=0, concat_axis=0, tiled=True)  7.51 us
    pallas_call x1, Pallas kernels, fields(): pl.pallas_call(field_kernel, out_shape=(field, field, field, field, jax.S...  5.38 us
    all_to_all x1, waiting for transfers between devices, body(): lax.all_to_all(slots, 'gx', split_axis=0, concat_axis=0, tiled=True)  4.29 us
    ppermute x2, starting transfers between devices, passed_along(): return lax.ppermute(block, axis, route)  3.61 us
    ppermute x2, waiting for transfers between devices, passed_along(): return lax.ppermute(block, axis, route)  2.3 us
  transfers between devices with their start and end apart: 3, of which 2 were waited for; matrix products, arithmetic and copies ran while one was open for 7% of the time, Pallas kernels for 0%

profile of v15, /device:TPU:0, one launch (start us, length us, event | category | flops | bytes accessed | tf_op | source)
XLA Modules:
  0.0 53.2 jit_solution(2188097384025624176)
XLA Ops:
  0.6 0.0 copy-start
  1.3 0.1 convert_reduce_fusion.1
  1.4 0.2 convert_reduce_fusion
  1.6 0.2 fusion.7
  1.8 0.4 fusion
  2.2 0.0 copy-start.2
  2.3 0.8 %broadcast_in_dim.4 = f32[16,32,256]{2,1,0:T(8,128)} broadcast(f32[32,256]{1,0:T(8,128)S(1)} %fusion), dimensions={1,2} | broadcast | bytes 557056 | tf_op jit(solution)/shard_map/broadcast_in_dim | solution.py:245
  3.1 7.5 %all-to-all-start = ((f32[16,32,256]{2,1,0:T(8,128)}), f32[16,32,256]{2,1,0:T(8,128)S(1)}, u32[]{:S(2)}, u32[]{:S(2)}) async-start(f32[16,32,256]{2,1,0:T(8,128)} %broadcast_in_dim.4), calls=%async_computation | async-start | bytes 1048576 | tf_op jit(solution)/shard_map/all_to_all | solution.py:246
  10.6 0.9 %slice_bitcast_fusion.2 = (f32[2,32,256]{2,1,0:T(8,128)S(1)}, f32[2,32,256]{2,1,0:T(8,128)S(1)}) fusion(f32[3,8,32,256]{3,2,1,0:T(8,128)} %ha.1, f32[3,8,32,256]{3,2,1,0:T(8,128)S(1)} %copy-done.2), kind=kLoop, calls=%fused_computation.15 | loop fusion | bytes 262144 | tf_op jit(solution)/shard_map/squeeze | solution.py:239
  11.5 0.0 copy-start.3
  11.5 1.0 %slice_bitcast_fusion = (f32[3,32,256]{2,1,0:T(8,128)S(1)}, f32[3,32,256]{2,1,0:T(8,128)S(1)}) fusion(f32[3,8,32,256]{3,2,1,0:T(8,128)} %ea.1, f32[3,8,32,256]{3,2,1,0:T(8,128)S(1)} %copy-done.1), kind=kLoop, calls=%fused_computation.13 | loop fusion | bytes 393216 | tf_op jit(solution)/shard_map/squeeze | solution.py:239
  12.5 0.7 %pad_maximum_fusion = f32[10,32,256]{2,1,0:T(8,128)} fusion(f32[3,32,256]{2,1,0:T(8,128)S(1)} %get-tuple-element.17, f32[2,32,256]{2,1,0:T(8,128)S(1)} %get-tuple-element.19, f32[3,32,256]{2,1,0:T(8,128)S(1)} %get-tuple-element.18, f32[2,32,256]{2,1,0:T(8,128)S(1)} %get-tuple-element.20), kind=kLoop, calls=%fused_computation.1 | loop fusion | flops 245760 | bytes 655360 | tf_op jit(solution)/shard_map/concatenate | solution.py:238
  13.3 2.3 %collective-permute-start.1 = (f32[10,32,256]{2,1,0:T(8,128)}, f32[10,32,256]{2,1,0:T(8,128)S(1)}, u32[]{:S(2)}, u32[]{:S(2)}) collective-permute-start(f32[10,32,256]{2,1,0:T(8,128)} %pad_maximum_fusion), channel_id=1, source_target_pairs={{0,1},{1,2},{2,3},{3,4},{4,5},{5,6},{6,7},{7,8},{8,9},{9,10},{10,1... | collective-permute-start | bytes 983048 | tf_op jit(solution)/shard_map/ppermute | solution.py:25
  15.6 0.9 %slice_bitcast_fusion.4 = (f32[2,32,256]{2,1,0:T(8,128)S(1)}, f32[2,32,256]{2,1,0:T(8,128)S(1)}) fusion(f32[3,8,32,256]{3,2,1,0:T(8,128)} %ea.1, f32[3,8,32,256]{3,2,1,0:T(8,128)S(1)} %copy-done.1), kind=kLoop, calls=%fused_computation.17 | loop fusion | bytes 262144 | tf_op jit(solution)/shard_map/squeeze | solution.py:236
  16.4 0.0 copy-start.6
  16.5 1.3 %collective-permute-start = (f32[4,32,256]{2,1,0:T(8,128)S(1)}, f32[4,32,256]{2,1,0:T(8,128)S(1)}, u32[]{:S(2)}, u32[]{:S(2)}) collective-permute-start(f32[4,32,256]{2,1,0:T(8,128)S(1)} %pad_maximum_fusion.1), channel_id=1, source_target_pairs={{1,0},{2,1},{3,2},{4,3},{5,4},{6,5},{7,6},{8,7},{9,8},{10,9},{11,1... | collective-permute-start | bytes 393224 | tf_op jit(solution)/shard_map/ppermute | solution.py:25
  18.4 0.0 copy-start.4
  18.4 0.1 copy.32.amp
  18.5 2.3 %collective-permute-done.upper = f32[4,32,256]{2,1,0:T(8,128)S(1)} collective-permute-done((f32[4,32,256]{2,1,0:T(8,128)S(1)}, f32[4,32,256]{2,1,0:T(8,128)S(1)}, u32[]{:S(2)}, u32[]{:S(2)}) %collective-permute-start) | collective-permute-done | bytes 131104 | tf_op jit(solution)/shard_map/ppermute | solution.py:25
  20.8 4.3 %all-to-all-done.arrived = f32[16,32,256]{2,1,0:T(8,128)S(1)} async-done(((f32[16,32,256]{2,1,0:T(8,128)}), f32[16,32,256]{2,1,0:T(8,128)S(1)}, u32[]{:S(2)}, u32[]{:S(2)}) %all-to-all-start) | async-done | bytes 524320 | tf_op jit(solution)/shard_map/all_to_all | solution.py:246
  25.1 5.4 %shard_map.173 = (f32[3,8,32,256]{3,2,1,0:T(8,128)}, f32[3,8,32,256]{3,2,1,0:T(8,128)}, f32[3,8,32,256]{3,2,1,0:T(8,128)}, f32[3,8,32,256]{3,2,1,0:T(8,128)}, f32[16,32,256]{2,1,0:T(8,128)S(1)}) custom-call(f32[3,8,32,256]{3,2,1,0:T(8,128)S(1)} %copy-done.1, f32[3,8,32,256]{3,2,1,0:T(8,128)S(1)} %copy-done.2, f32[3,8,32,256]{3,2,1,0:T(8,128)S(1)} %copy-done.3, ...), custom_call_target="tpu_custom_call" | custom-call | flops 13107200 | bytes 10485760 | tf_op jit(solution)/shard_map/pallas_call | solution.py:196
  30.5 21.5 %all_to_all.10 = f32[16,32,256]{2,1,0:T(8,128)S(1)} all-to-all(f32[16,32,256]{2,1,0:T(8,128)S(1)} %get-tuple-element.14), channel_id=1, replica_groups=mesh['grp'=2,'gx'=16] {'gx'}, dimensions={0} | all-to-all | bytes 1048576 | tf_op jit(solution)/shard_map/all_to_all | solution.py:251
  52.0 0.3 fusion.9
  52.3 0.9 %convolution_bitcast_fusion = f32[1,32,256]{2,1,0:T(8,128)} fusion(f32[32,256]{1,0:T(8,128)S(1)} %fusion.9, f32[256]{0:T(256)S(1)} %convert_reduce_fusion, s32[]{:T(128)} %bitcast), kind=kOutput, calls=%fused_computation | convolution fusion | flops 25559040 | bytes 66564 | tf_op jit(solution)/shard_map/xb,by->xy/dot_general | solution.py:253
  (12 shorter events, 0.1 us)
Async XLA Ops:
  0.6 0.9 %copy-start = (f32[1,32,256]{2,1,0:T(8,128)S(1)}, f32[1,32,256]{2,1,0:T(8,128)}, u32[]{:S(2)}) copy-start(f32[1,32,256]{2,1,0:T(8,128)} %param.22) | copy-start | bytes 98308
  2.2 8.4 %copy-start.2 = (f32[3,8,32,256]{3,2,1,0:T(8,128)S(1)}, f32[3,8,32,256]{3,2,1,0:T(8,128)}, u32[]{:S(2)}) copy-start(f32[3,8,32,256]{3,2,1,0:T(8,128)} %hf.1) | copy-start | bytes 2359300
  3.1 8.4 %copy-start.1 = (f32[3,8,32,256]{3,2,1,0:T(8,128)S(1)}, f32[3,8,32,256]{3,2,1,0:T(8,128)}, u32[]{:S(2)}) copy-start(f32[3,8,32,256]{3,2,1,0:T(8,128)} %ef.1) | copy-start | bytes 2359300
  3.1 22.0 %all-to-all-start = ((f32[16,32,256]{2,1,0:T(8,128)}), f32[16,32,256]{2,1,0:T(8,128)S(1)}, u32[]{:S(2)}, u32[]{:S(2)}) async-start(f32[16,32,256]{2,1,0:T(8,128)} %broadcast_in_dim.4), calls=%async_computation | async-start | bytes 1048576 | tf_op jit(solution)/shard_map/all_to_all | solution.py:246
  11.5 13.6 %copy-start.3 = (f32[3,8,32,256]{3,2,1,0:T(8,128)S(1)}, f32[3,8,32,256]{3,2,1,0:T(8,128)}, u32[]{:S(2)}) copy-start(f32[3,8,32,256]{3,2,1,0:T(8,128)} %pf.1) | copy-start | bytes 2359300
  13.3 7.6 %collective-permute-start.1 = (f32[10,32,256]{2,1,0:T(8,128)}, f32[10,32,256]{2,1,0:T(8,128)S(1)}, u32[]{:S(2)}, u32[]{:S(2)}) collective-permute-start(f32[10,32,256]{2,1,0:T(8,128)} %pad_maximum_fusion), channel_id=1, source_target_pairs={{0,1},{1,2},{2,3},{3,4},{4,5},{5,6},{6,7},{7,8},{8,9},{9,10},{10,1... | collective-permute-start | bytes 983048 | tf_op jit(solution)/shard_map/ppermute | solution.py:25
  16.4 2.0 %copy-start.6 = (f32[16,3]{0,1:T(4,128)S(1)}, f32[16,3]{0,1:T(4,128)}, u32[]{:S(2)}) copy-start(f32[16,3]{0,1:T(4,128)} %param.23) | copy-start | bytes 580
  16.5 4.4 %collective-permute-start = (f32[4,32,256]{2,1,0:T(8,128)S(1)}, f32[4,32,256]{2,1,0:T(8,128)S(1)}, u32[]{:S(2)}, u32[]{:S(2)}) collective-permute-start(f32[4,32,256]{2,1,0:T(8,128)S(1)} %pad_maximum_fusion.1), channel_id=1, source_target_pairs={{1,0},{2,1},{3,2},{4,3},{5,4},{6,5},{7,6},{8,7},{9,8},{10,9},{11,1... | collective-permute-start | bytes 393224 | tf_op jit(solution)/shard_map/ppermute | solution.py:25
  18.4 6.7 %copy-start.4 = (s32[16]{0:T(128)S(1)}, s32[16]{0:T(128)}, u32[]{:S(2)}) copy-start(s32[16]{0:T(128)} %src.1) | copy-start | bytes 196
  18.4 6.7 %copy-start.5 = (s32[16]{0:T(128)S(1)}, s32[16]{0:T(128)}, u32[]{:S(2)}) copy-start(s32[16]{0:T(128)} %mon.1) | copy-start | bytes 196

commit v16 on v15

--- a/solution.py
+++ b/solution.py
@@ -17,6 +17,9 @@
 KEEP = 1.0 - DAMPING * DT / 2.0
 LOSS = 1.0 + DAMPING * DT / 2.0
 SHRINK = 1.0 / LOSS
+KEEP_SHRUNK = KEEP / LOSS
+DT_SHRUNK = DT / LOSS
+AHEAD_GAIN = 1.0 + GAIN_FIELD
 
 
 def passed_along(block, axis, distance):
@@ -107,7 +110,7 @@
             jnp.where(keep, hy - DT * curl_y, 0.0),
         )
 
-    def new_e(e, p, j, out, z, hn, hn_dn, step, strength):
+    def new_e(e, p, j, out, z, hn, hn_dn, step, drift):
         hx, hy, hz = hn
         hx_dn, hy_dn = hn_dn
         curl = (
@@ -116,7 +119,7 @@
             hy - behind_x(hy) - (hx - behind_y(hx)),
         )
         for c in range(3):
-            j_next = (KEEP * j[c, z] + DT * (strength * e[c, z] - p[c, z])) * SHRINK
+            j_next = KEEP_SHRUNK * j[c, z] + drift * e[c, z] - DT_SHRUNK * p[c, z]
             out[c, z] = e[c, z] + step * (curl[c] - j_next)
 
     runs = ((ef, hf, pf, jf, hf_o, ef_o, 0), (ea, ha, pa, ja, ha_o, ea_o, 2))
@@ -134,11 +137,11 @@
     for z in range(depth):
         density = rho[z]
         step = DT / (1.0 + EPS_RANGE * density)
-        strength = STRENGTH_BASE + STRENGTH_RANGE * density
+        drift = DT_SHRUNK * (STRENGTH_BASE + STRENGTH_RANGE * density)
         for r, (e, h, p, j, h_out, e_out, up) in enumerate(runs):
             hn = (h_out[0, z], h_out[1, z], h_out[2, z])
             hn_dn = prev[r] if z == 0 else (h_out[0, z - 1], h_out[1, z - 1])
-            new_e(e, p, j, e_out, z, hn, hn_dn, step, strength)
+            new_e(e, p, j, e_out, z, hn, hn_dn, step, drift)
 
     plane = width_x * width_y
     tile_row = lax.broadcasted_iota(jnp.int32, (8, width_y), 0)
@@ -172,7 +175,7 @@
         total = None
         for c in range(3):
             fwd = ef_o[c, z]
-            term = ea_o[c, z] * (fwd - ef[c, z] + GAIN_FIELD * fwd)
+            term = ea_o[c, z] * (AHEAD_GAIN * fwd - ef[c, z])
             total = term if total is None else total + term
         p = index * depth + z - start
 

time: 53.7 us -> 53.6 us (level)
  no operation moved by 1% of the time
where the time goes in v16:
time: 53.6 us; the launch traced here: 53.1 us
  blocking collectives  21.5 us (40%)
  starting transfers between devices  11.1 us (21%)
  waiting for transfers between devices  6.59 us (12%)
  Pallas kernels  5.25 us (10%)
  local copies, waits for them, and re-layouts  3.67 us (7%)
  between operations  2.09 us (4%)
  matrix products  1.88 us (4%)
  other arithmetic  1.06 us (2%)
    all_to_all x1, blocking collectives, body(): lax.all_to_all(returned, 'gx', split_axis=0, concat_axis=0, tiled=True)  21.5 us
    all_to_all x1, starting transfers between devices, body(): lax.all_to_all(slots, 'gx', split_axis=0, concat_axis=0, tiled=True)  7.51 us
    pallas_call x1, Pallas kernels, fields(): pl.pallas_call(field_kernel, out_shape=(field, field, field, field, jax.S...  5.25 us
    all_to_all x1, waiting for transfers between devices, body(): lax.all_to_all(slots, 'gx', split_axis=0, concat_axis=0, tiled=True)  4.29 us
    ppermute x2, starting transfers between devices, passed_along(): return lax.ppermute(block, axis, route)  3.61 us
    ppermute x2, waiting for transfers between devices, passed_along(): return lax.ppermute(block, axis, route)  2.3 us
  transfers between devices with their start and end apart: 3, of which 2 were waited for; matrix products, arithmetic and copies ran while one was open for 7% of the time, Pallas kernels for 0%

profile of v16, /device:TPU:0, one launch (start us, length us, event | category | flops | bytes accessed | tf_op | source)
XLA Modules:
  0.0 53.1 jit_solution(17448883565380310865)
XLA Ops:
  0.6 0.0 copy-start
  1.3 0.1 convert_reduce_fusion.1
  1.4 0.2 convert_reduce_fusion
  1.6 0.2 fusion.7
  1.8 0.4 fusion
  2.2 0.0 copy-start.2
  2.3 0.8 %broadcast_in_dim.4 = f32[16,32,256]{2,1,0:T(8,128)} broadcast(f32[32,256]{1,0:T(8,128)S(1)} %fusion), dimensions={1,2} | broadcast | bytes 557056 | tf_op jit(solution)/shard_map/broadcast_in_dim | solution.py:248
  3.1 7.5 %all-to-all-start = ((f32[16,32,256]{2,1,0:T(8,128)}), f32[16,32,256]{2,1,0:T(8,128)S(1)}, u32[]{:S(2)}, u32[]{:S(2)}) async-start(f32[16,32,256]{2,1,0:T(8,128)} %broadcast_in_dim.4), calls=%async_computation | async-start | bytes 1048576 | tf_op jit(solution)/shard_map/all_to_all | solution.py:249
  10.6 0.9 %slice_bitcast_fusion.2 = (f32[2,32,256]{2,1,0:T(8,128)S(1)}, f32[2,32,256]{2,1,0:T(8,128)S(1)}) fusion(f32[3,8,32,256]{3,2,1,0:T(8,128)} %ha.1, f32[3,8,32,256]{3,2,1,0:T(8,128)S(1)} %copy-done.2), kind=kLoop, calls=%fused_computation.15 | loop fusion | bytes 262144 | tf_op jit(solution)/shard_map/squeeze | solution.py:242
  11.5 0.0 copy-start.3
  11.5 1.0 %slice_bitcast_fusion = (f32[3,32,256]{2,1,0:T(8,128)S(1)}, f32[3,32,256]{2,1,0:T(8,128)S(1)}) fusion(f32[3,8,32,256]{3,2,1,0:T(8,128)} %ea.1, f32[3,8,32,256]{3,2,1,0:T(8,128)S(1)} %copy-done.1), kind=kLoop, calls=%fused_computation.13 | loop fusion | bytes 393216 | tf_op jit(solution)/shard_map/squeeze | solution.py:242
  12.5 0.7 %pad_maximum_fusion = f32[10,32,256]{2,1,0:T(8,128)} fusion(f32[3,32,256]{2,1,0:T(8,128)S(1)} %get-tuple-element.17, f32[2,32,256]{2,1,0:T(8,128)S(1)} %get-tuple-element.19, f32[3,32,256]{2,1,0:T(8,128)S(1)} %get-tuple-element.18, f32[2,32,256]{2,1,0:T(8,128)S(1)} %get-tuple-element.20), kind=kLoop, calls=%fused_computation.1 | loop fusion | flops 245760 | bytes 655360 | tf_op jit(solution)/shard_map/concatenate | solution.py:241
  13.3 2.3 %collective-permute-start.1 = (f32[10,32,256]{2,1,0:T(8,128)}, f32[10,32,256]{2,1,0:T(8,128)S(1)}, u32[]{:S(2)}, u32[]{:S(2)}) collective-permute-start(f32[10,32,256]{2,1,0:T(8,128)} %pad_maximum_fusion), channel_id=1, source_target_pairs={{0,1},{1,2},{2,3},{3,4},{4,5},{5,6},{6,7},{7,8},{8,9},{9,10},{10,1... | collective-permute-start | bytes 983048 | tf_op jit(solution)/shard_map/ppermute | solution.py:28
  15.6 0.9 %slice_bitcast_fusion.4 = (f32[2,32,256]{2,1,0:T(8,128)S(1)}, f32[2,32,256]{2,1,0:T(8,128)S(1)}) fusion(f32[3,8,32,256]{3,2,1,0:T(8,128)} %ea.1, f32[3,8,32,256]{3,2,1,0:T(8,128)S(1)} %copy-done.1), kind=kLoop, calls=%fused_computation.17 | loop fusion | bytes 262144 | tf_op jit(solution)/shard_map/squeeze | solution.py:239
  16.4 0.0 copy-start.6
  16.5 1.3 %collective-permute-start = (f32[4,32,256]{2,1,0:T(8,128)S(1)}, f32[4,32,256]{2,1,0:T(8,128)S(1)}, u32[]{:S(2)}, u32[]{:S(2)}) collective-permute-start(f32[4,32,256]{2,1,0:T(8,128)S(1)} %pad_maximum_fusion.1), channel_id=1, source_target_pairs={{1,0},{2,1},{3,2},{4,3},{5,4},{6,5},{7,6},{8,7},{9,8},{10,9},{11,1... | collective-permute-start | bytes 393224 | tf_op jit(solution)/shard_map/ppermute | solution.py:28
  18.4 0.0 copy-start.4
  18.4 0.1 copy.32.amp
  18.5 2.3 %collective-permute-done.upper = f32[4,32,256]{2,1,0:T(8,128)S(1)} collective-permute-done((f32[4,32,256]{2,1,0:T(8,128)S(1)}, f32[4,32,256]{2,1,0:T(8,128)S(1)}, u32[]{:S(2)}, u32[]{:S(2)}) %collective-permute-start) | collective-permute-done | bytes 131104 | tf_op jit(solution)/shard_map/ppermute | solution.py:28
  20.8 4.3 %all-to-all-done.arrived = f32[16,32,256]{2,1,0:T(8,128)S(1)} async-done(((f32[16,32,256]{2,1,0:T(8,128)}), f32[16,32,256]{2,1,0:T(8,128)S(1)}, u32[]{:S(2)}, u32[]{:S(2)}) %all-to-all-start) | async-done | bytes 524320 | tf_op jit(solution)/shard_map/all_to_all | solution.py:249
  25.1 5.3 %shard_map.173 = (f32[3,8,32,256]{3,2,1,0:T(8,128)}, f32[3,8,32,256]{3,2,1,0:T(8,128)}, f32[3,8,32,256]{3,2,1,0:T(8,128)}, f32[3,8,32,256]{3,2,1,0:T(8,128)}, f32[16,32,256]{2,1,0:T(8,128)S(1)}) custom-call(f32[3,8,32,256]{3,2,1,0:T(8,128)S(1)} %copy-done.1, f32[3,8,32,256]{3,2,1,0:T(8,128)S(1)} %copy-done.2, f32[3,8,32,256]{3,2,1,0:T(8,128)S(1)} %copy-done.3, ...), custom_call_target="tpu_custom_call" | custom-call | flops 13107200 | bytes 10485760 | tf_op jit(solution)/shard_map/pallas_call | solution.py:199
  30.4 21.5 %all_to_all.10 = f32[16,32,256]{2,1,0:T(8,128)S(1)} all-to-all(f32[16,32,256]{2,1,0:T(8,128)S(1)} %get-tuple-element.14), channel_id=1, replica_groups=mesh['grp'=2,'gx'=16] {'gx'}, dimensions={0} | all-to-all | bytes 1048576 | tf_op jit(solution)/shard_map/all_to_all | solution.py:254
  51.9 0.3 fusion.9
  52.2 0.9 %convolution_bitcast_fusion = f32[1,32,256]{2,1,0:T(8,128)} fusion(f32[32,256]{1,0:T(8,128)S(1)} %fusion.9, f32[256]{0:T(256)S(1)} %convert_reduce_fusion, s32[]{:T(128)} %bitcast), kind=kOutput, calls=%fused_computation | convolution fusion | flops 25559040 | bytes 66564 | tf_op jit(solution)/shard_map/xb,by->xy/dot_general | solution.py:256
  (12 shorter events, 0.1 us)
Async XLA Ops:
  0.6 0.9 %copy-start = (f32[1,32,256]{2,1,0:T(8,128)S(1)}, f32[1,32,256]{2,1,0:T(8,128)}, u32[]{:S(2)}) copy-start(f32[1,32,256]{2,1,0:T(8,128)} %param.22) | copy-start | bytes 98308
  2.2 8.4 %copy-start.2 = (f32[3,8,32,256]{3,2,1,0:T(8,128)S(1)}, f32[3,8,32,256]{3,2,1,0:T(8,128)}, u32[]{:S(2)}) copy-start(f32[3,8,32,256]{3,2,1,0:T(8,128)} %hf.1) | copy-start | bytes 2359300
  3.1 8.4 %copy-start.1 = (f32[3,8,32,256]{3,2,1,0:T(8,128)S(1)}, f32[3,8,32,256]{3,2,1,0:T(8,128)}, u32[]{:S(2)}) copy-start(f32[3,8,32,256]{3,2,1,0:T(8,128)} %ef.1) | copy-start | bytes 2359300
  3.1 22.0 %all-to-all-start = ((f32[16,32,256]{2,1,0:T(8,128)}), f32[16,32,256]{2,1,0:T(8,128)S(1)}, u32[]{:S(2)}, u32[]{:S(2)}) async-start(f32[16,32,256]{2,1,0:T(8,128)} %broadcast_in_dim.4), calls=%async_computation | async-start | bytes 1048576 | tf_op jit(solution)/shard_map/all_to_all | solution.py:249
  11.5 13.6 %copy-start.3 = (f32[3,8,32,256]{3,2,1,0:T(8,128)S(1)}, f32[3,8,32,256]{3,2,1,0:T(8,128)}, u32[]{:S(2)}) copy-start(f32[3,8,32,256]{3,2,1,0:T(8,128)} %pf.1) | copy-start | bytes 2359300
  13.3 7.6 %collective-permute-start.1 = (f32[10,32,256]{2,1,0:T(8,128)}, f32[10,32,256]{2,1,0:T(8,128)S(1)}, u32[]{:S(2)}, u32[]{:S(2)}) collective-permute-start(f32[10,32,256]{2,1,0:T(8,128)} %pad_maximum_fusion), channel_id=1, source_target_pairs={{0,1},{1,2},{2,3},{3,4},{4,5},{5,6},{6,7},{7,8},{8,9},{9,10},{10,1... | collective-permute-start | bytes 983048 | tf_op jit(solution)/shard_map/ppermute | solution.py:28
  16.4 2.0 %copy-start.6 = (f32[16,3]{0,1:T(4,128)S(1)}, f32[16,3]{0,1:T(4,128)}, u32[]{:S(2)}) copy-start(f32[16,3]{0,1:T(4,128)} %param.23) | copy-start | bytes 580
  16.5 4.4 %collective-permute-start = (f32[4,32,256]{2,1,0:T(8,128)S(1)}, f32[4,32,256]{2,1,0:T(8,128)S(1)}, u32[]{:S(2)}, u32[]{:S(2)}) collective-permute-start(f32[4,32,256]{2,1,0:T(8,128)S(1)} %pad_maximum_fusion.1), channel_id=1, source_target_pairs={{1,0},{2,1},{3,2},{4,3},{5,4},{6,5},{7,6},{8,7},{9,8},{10,9},{11,1... | collective-permute-start | bytes 393224 | tf_op jit(solution)/shard_map/ppermute | solution.py:28
  18.4 6.7 %copy-start.4 = (s32[16]{0:T(128)S(1)}, s32[16]{0:T(128)}, u32[]{:S(2)}) copy-start(s32[16]{0:T(128)} %src.1) | copy-start | bytes 196
  18.4 6.7 %copy-start.5 = (s32[16]{0:T(128)S(1)}, s32[16]{0:T(128)}, u32[]{:S(2)}) copy-start(s32[16]{0:T(128)} %mon.1) | copy-start | bytes 196
